TPU v7x, 256 devices: a whole 4x4x8 slice. The times are simulated.
256 devices in a mesh: tok: 64 (over z, x, core), mlp: 4 (over y).
Axes of the slice: x: 4, y: 4, z: 8, core: 2. Of those that a mesh axis runs over, the one named last changes fastest.
Arguments:
- new_x: bfloat16 [16, 512, 8192], P(None, ('tok', 'mlp')), may hold values from -6 to 6
- gate_input: bfloat16 [16, 512, 8192], P(None, ('tok', 'mlp')), may hold values from -40 to 40
- state_proj: bfloat16 [16, 512, 8, 256], P(None, ('tok', 'mlp')), may hold values from -1.796875 to 1.796875
- step_size: float32 [16, 512, 128], P('mlp', None, 'tok'), may hold values from 0.25 to 4
- decay_rate: float32 [128], P('tok'), may hold values from -12 to -3
- x_cache: bfloat16 [16, 3072, 8192], P('mlp', None, 'tok'), may hold values from -6 to 6
- b_cache: bfloat16 [16, 8, 3072, 128], P('mlp', None, 'tok'), may hold values from -1.8 to 1.8
- decay_cache: float32 [16, 128, 3072], P('mlp', 'tok'), may hold values from -1 to 0
- lengths: int32 [16], P('mlp'), may hold values from 64 to 3072, as said below
- sink_pos: int32 [16, 4], P('mlp'), may hold values from 0 to 63, as said below
- windows: int32 [16], P('mlp'), may hold values from 1024 to 2048, as said below
- norm_gain: float32 [8192], replicated, may hold values from 0.5 to 1.5
Outputs:
- mixer_normed: bfloat16 [16, 512, 8192], P(None, ('tok', 'mlp'))
Inputs may be any that keep to these rules, and one draw needn't show every extreme that they name: `lengths`: some request holds exactly 3072 cached positions. `windows`: some request has a window of exactly 2048. `sink_pos`: a request's sink positions increase and lie below its length.
All inputs are finite; a program needn't handle non-finite values.
Results may differ from a plain program's by a relative error of at most 0.0061.
Values may be sent and summed in bfloat16 or wider, within the bound.
No kernel may reach another device: no remote copies, remote signals or barrier semaphores. Data moves between devices by JAX's collectives and lax.ppermute only.
A program may use at most 64 MiB of HBM per device.

v0:
```python
import jax
import jax.numpy as jnp
from jax import lax
from jax.sharding import PartitionSpec as P

EPS = 1e-05


def weighted_sum(queries, key_b, key_x, query_side, key_side, keep_mask, sink_only):
    scores = jnp.dot(queries, key_b.T, preferred_element_type=jnp.float32)
    head_count = query_side.shape[0]
    head_width = key_x.shape[1] // head_count
    pieces = []
    for head in range(head_count):
        log_weight = query_side[head][:, None] + key_side[head][None, :]
        decayed = jnp.exp(jnp.minimum(log_weight, 0.0))
        weight = jnp.where(keep_mask, decayed, jnp.where(sink_only, 1.0, 0.0))
        weighted = (scores * weight).astype(jnp.bfloat16)
        values = key_x[:, head * head_width : (head + 1) * head_width]
        pieces.append(jnp.dot(weighted, values, preferred_element_type=jnp.float32))
    return jnp.concatenate(pieces, axis=1)


def per_device(
    new_x,
    gate_input,
    state_proj,
    step_size,
    decay_rate,
    x_cache,
    b_cache,
    decay_cache,
    lengths,
    sink_pos,
    windows,
    norm_gain,
):
    n_tok = lax.axis_size("tok")
    groups = state_proj.shape[2]
    state_dim = b_cache.shape[3]
    copies = n_tok // groups
    heads_dev = decay_rate.shape[0]
    requests = step_size.shape[0]
    new_len = step_size.shape[1]
    cache_len = x_cache.shape[1]
    shared_b = lax.all_to_all(
        jnp.repeat(b_cache, copies, axis=1), "tok", split_axis=1, concat_axis=2, tiled=True
    )
    owned_x, owned_bc = (
        lax.all_to_all(new_x, "mlp", split_axis=0, concat_axis=1, tiled=True),
        lax.all_to_all(state_proj, "mlp", split_axis=0, concat_axis=1, tiled=True),
    )
    head_x, head_bc = (
        lax.all_to_all(owned_x, "tok", split_axis=2, concat_axis=1, tiled=True),
        lax.all_to_all(
            jnp.repeat(owned_bc, copies, axis=2), "tok", split_axis=2, concat_axis=1, tiled=True
        ),
    )
    token_order = jnp.arange(new_len, dtype=jnp.int32)
    head_decay_values = jnp.exp(decay_rate)
    step_head = step_size[:, token_order, :]
    cum_new = jnp.cumsum(-(step_size * head_decay_values), axis=1)[:, token_order, :]
    scaled = (
        head_x.astype(jnp.float32).reshape(requests, new_len, heads_dev, -1) * step_head[..., None]
    )
    scaled = scaled.reshape(requests, new_len, -1).astype(jnp.bfloat16)
    positions = jnp.arange(cache_len, dtype=jnp.int32)
    live_mask = positions[None, :] < lengths[:, None]
    masked = jnp.where(live_mask[:, None, :], decay_cache, 0.0)
    local_sum = jnp.cumsum(masked, axis=2)
    tail_sum = local_sum[:, :, -1:] - local_sum

    def one_request(request_parts):
        bc_now, x_now, cum_now, tail_now, old_x, old_b, length, sink_now, window = request_parts
        b_new = bc_now[:, 0, :state_dim]
        c_now = bc_now[:, 0, state_dim:]
        query_pos = length + token_order
        cum_rows = cum_now.T
        new_gap = token_order[:, None] - token_order[None, :]
        keep_new = (new_gap >= 0) & (new_gap < window)
        first_sum = weighted_sum(
            c_now, b_new, x_now, cum_rows, -cum_rows, keep_new, jnp.zeros_like(keep_new)
        )
        inside = positions < length
        span = query_pos[:, None] - positions[None, :]
        in_window = (span < window) & inside[None, :]
        sink_hit = jnp.any(positions[None, :] == sink_now[:, None], axis=0) & inside
        sink_only = sink_hit[None, :] & jnp.logical_not(in_window)
        return first_sum + weighted_sum(
            c_now, old_b, old_x, cum_rows, tail_now, in_window, sink_only
        )

    mixer_out = lax.map(
        one_request,
        (head_bc, scaled, cum_new, tail_sum, x_cache, shared_b[:, 0], lengths, sink_pos, windows),
    )
    mixer_out = mixer_out.astype(jnp.bfloat16)
    spread_back = lax.all_to_all(mixer_out, "tok", split_axis=1, concat_axis=2, tiled=True)
    merged = lax.all_to_all(spread_back, "mlp", split_axis=1, concat_axis=0, tiled=True)
    mixer_tok = lax.optimization_barrier(merged)
    gated_out = mixer_tok.astype(jnp.float32) * jax.nn.silu(gate_input.astype(jnp.float32))
    grouped = gated_out.reshape(gated_out.shape[0], gated_out.shape[1], groups, -1)
    norm_scale = lax.rsqrt(jnp.mean(grouped * grouped, axis=-1, keepdims=True) + EPS)
    normed = (grouped * norm_scale).reshape(gated_out.shape) * norm_gain
    return normed.astype(jnp.bfloat16)


def solution(mesh):
    return jax.shard_map(
        per_device,
        mesh=mesh,
        in_specs=(
            P(None, ("tok", "mlp"), None),
            P(None, ("tok", "mlp"), None),
            P(None, ("tok", "mlp"), None, None),
            P("mlp", None, "tok"),
            P("tok"),
            P("mlp", None, "tok"),
            P("mlp", None, "tok", None),
            P("mlp", "tok", None),
            P("mlp"),
            P("mlp", None),
            P("mlp"),
            P(),
        ),
        out_specs=P(None, ("tok", "mlp"), None),
        check_vma=False,
    )
```

profile of v0, /device:TPU:1, one launch (start us, length us, event | category | flops | bytes accessed | tf_op | source)
XLA Modules:
  0.0 366.3 jit_solution(10278418547323945325)
XLA Ops:
  0.0 12.9 %all_to_all.108 = bf16[16,2,8192]{2,1,0:T(2,128)(2,1)S(1)} all-to-all(bf16[16,2,8192]{2,1,0:T(2,128)(2,1)} %param.14), channel_id=1, replica_groups=mesh['tok'=64,'mlp'=4] {'mlp'}, dimensions={0} | all-to-all | bytes 1048576 | tf_op jit(solution)/shard_map/all_to_all | solution.py:50
  12.9 3.3 all-to-all-start
  16.7 8.2 %copy.152 = bf16[4,8,8192]{1,0,2:T(4,128)(2,1)} copy(bf16[4,8,8192]{2,0,1:T(4,128)(2,1)S(1)} %bitcast.152) | data formatting | bytes 1048576 | tf_op jit(solution)/shard_map/all_to_all | solution.py:50
  24.9 11.2 %reshape.174 = bf16[64,2,2048]{2,1,0:T(2,128)(2,1)} reshape(bf16[8192,4,8]{2,1,0:T(4,128)(2,1)} %bitcast.143) | data formatting | bytes 1048576
  36.2 14.0 %all-to-all-start.3 = ((bf16[64,2,2048]{2,1,0:T(2,128)(2,1)}), bf16[64,2,2048]{2,1,0:T(2,128)(2,1)S(1)}, u32[]{:S(2)}, u32[]{:S(2)}) async-start(bf16[64,2,2048]{2,1,0:T(2,128)(2,1)} %reshape.174), calls=%async_computation.3 | async-start | bytes 1048576 | tf_op jit(solution)/shard_map/all_to_all | solution.py:54
  50.2 17.6 %all-to-all-done.3 = bf16[64,2,2048]{2,1,0:T(2,128)(2,1)S(1)} async-done(((bf16[64,2,2048]{2,1,0:T(2,128)(2,1)}), bf16[64,2,2048]{2,1,0:T(2,128)(2,1)S(1)}, u32[]{:S(2)}, u32[]{:S(2)}) %all-to-all-start.3) | async-done | bytes 524320 | tf_op jit(solution)/shard_map/all_to_all | solution.py:54
  67.9 1.1 broadcast_in_dim.34
  69.0 5.8 %all-to-all-start.1 = ((bf16[4,8,64,256]{3,1,0,2:T(8,128)(2,1)}), bf16[4,8,64,256]{3,1,0,2:T(8,128)(2,1)S(1)}, u32[]{:S(2)}, u32[]{:S(2)}) async-start(bf16[4,8,64,256]{3,1,0,2:T(8,128)(2,1)} %bitcast.3), calls=%async_computation.1 | async-start | bytes 2097152 | tf_op jit(solution)/shard_map/all_to_all | solution.py:55
  74.8 28.1 %all-to-all-done.1 = bf16[4,8,64,256]{3,1,0,2:T(8,128)(2,1)S(1)} async-done(((bf16[4,8,64,256]{3,1,0,2:T(8,128)(2,1)}), bf16[4,8,64,256]{3,1,0,2:T(8,128)(2,1)S(1)}, u32[]{:S(2)}, u32[]{:S(2)}) %all-to-all-start.1) | async-done | bytes 1048608 | tf_op jit(solution)/shard_map/all_to_all | solution.py:55
  103.0 2.5 broadcast_in_dim.44
  105.5 6.4 %all-to-all-start.4 = ((bf16[4,64,48,128]{3,2,0,1:T(8,128)(2,1)}), bf16[4,64,48,128]{3,2,0,1:T(8,128)(2,1)}, u32[]{:S(2)}, u32[]{:S(2)}) async-start(bf16[4,64,48,128]{3,2,0,1:T(8,128)(2,1)} %bitcast.19), calls=%async_computation.4 | async-start | bytes 6291456 | tf_op jit(solution)/shard_map/all_to_all | solution.py:46
  112.4 2.4 reduce-window.14
  116.0 2.1 gather_fusion
  118.3 2.1 gather_fusion.1
  120.6 1.1 mul.65
  121.7 1.5 copy.157
  124.2 2.3 reduce-window.16
  128.7 10.9 %reshape.175 = bf16[8192,4,8]{2,1,0:T(4,128)(2,1)} reshape(bf16[64,2,2048]{2,1,0:T(2,128)(2,1)S(1)} %all-to-all-done.3) | data formatting | bytes 1048576
  139.6 9.7 %copy.153 = bf16[4,8,8192]{2,1,0:T(8,128)(2,1)S(1)} copy(bf16[4,8,8192]{1,0,2:T(4,128)(2,1)} %bitcast.144) | data formatting | bytes 1048576 | tf_op jit(solution)/shard_map/all_to_all | solution.py:54
  149.6 1.4 fusion.54
  151.0 1.1 copy.184
  152.1 32.2 %all-to-all-done.4 = bf16[4,64,48,128]{3,2,0,1:T(8,128)(2,1)} async-done(((bf16[4,64,48,128]{3,2,0,1:T(8,128)(2,1)}), bf16[4,64,48,128]{3,2,0,1:T(8,128)(2,1)}, u32[]{:S(2)}, u32[]{:S(2)}) %all-to-all-start.4) | async-done | bytes 3145760 | tf_op jit(solution)/shard_map/all_to_all | solution.py:46
  184.3 2.4 copy.159
  186.7 135.0 %while.12 = (s32[]{:T(128)}, bf16[4,512,128]{2,0,1:T(4,128)(2,1)}, bf16[4,512,1,256]{3,1,2,0:T(8,128)(2,1)}, s32[4]{0:T(128)}, f32[4,512,2]{1,2,0:T(2,128)S(1)},...) while((s32[]{:T(128)}, bf16[4,512,128]{2,0,1:T(4,128)(2,1)}, ...), condition=%wide.region_6.7_spmd.clone.clone, body=%wide.region_4.6_spmd.clone.clone.sunk | while | flops 979137024 | bytes 48118092 | solution.py:93
  188.2 1.3 dynamic_slice.76
  190.4 1.1 convolution_bitcast_fusion.4
  191.6 1.1 convolution_bitcast_fusion.5
  192.7 3.6 fusion.85
  197.1 1.3 dynamic_slice.77
  200.5 1.3 dynamic-slice_bitcast_fusion.10
  201.9 6.8 %fusion.88 = f32[1,512,64]{1,2,0:T(8,128)S(1)} fusion(f32[512,3072]{1,0:T(8,128)} %fusion.85, f32[3072]{0:T(1024)S(1)} %bitcast.160, f32[512]{0:T(512)S(1)} %bitcast.164, s32[]{:T(128)} %bitcast.135, s32[512]{0:T(512)S(1)} %iota_add_fusion.2, pred[3072]{0:T(1024)(128)(4,1)S(1)} %get-tuple-element.353, pred[3072]{0:T(1024)(128)(4,1)S(1)} %get-tuple-element.354, ...), kind=kOutput, calls=%fused_computation.19.clone.1 | convolution fusion | flops 218628096 | bytes 7231492 | tf_op jit(solution)/shard_map/while/body/eval_jaxpr/dot_general | solution.py:20
  208.8 4.3 %fusion.89 = f32[1,512,64]{1,2,0:T(8,128)S(1)} fusion(f32[512,3072]{1,0:T(8,128)S(1)} %bitcast.142, f32[3072]{0:T(1024)S(1)} %bitcast.159, f32[512]{0:T(512)S(1)} %bitcast.162, s32[]{:T(128)} %bitcast.135, s32[512]{0:T(512)S(1)} %iota_add_fusion.2, pred[3072]{0:T(1024)(128)(4,1)S(1)} %get-tuple-element.353, ...), kind=kOutput, calls=%fused_computation.18.clone.1 | convolution fusion | flops 218628096 | bytes 7231492 | tf_op jit(solution)/shard_map/while/body/eval_jaxpr/dot_general | solution.py:20
  213.2 7.4 %dynamic_update_slice.7 = bf16[4,512,128]{2,0,1:T(4,128)(2,1)} dynamic-update-slice(bf16[4,512,128]{2,0,1:T(4,128)(2,1)} %get-tuple-element.371, bf16[1,512,128]{2,0,1:T(2,128)(2,1)S(1)} %copy.187, s32[]{:T(128)S(6)} %copy.191, s32[]{:T(128)} %constant.27.clone.1..sunk, s32[]{:T(128)} %constant.27.clone.1..sunk) | dynamic-update-slice | bytes 262148 | tf_op jit(solution)/shard_map/while/body/jit(dynamic_update_index_in_dim)/dynamic_update_slice | solution.py:93
  221.9 1.3 dynamic_slice.76
  224.1 1.1 convolution_bitcast_fusion.4
  225.2 1.1 convolution_bitcast_fusion.5
  226.4 3.6 fusion.85
  230.8 1.3 dynamic_slice.77
  234.2 1.3 dynamic-slice_bitcast_fusion.10
  235.6 6.8 %fusion.88 = f32[1,512,64]{1,2,0:T(8,128)S(1)} fusion(f32[512,3072]{1,0:T(8,128)} %fusion.85, f32[3072]{0:T(1024)S(1)} %bitcast.160, f32[512]{0:T(512)S(1)} %bitcast.164, s32[]{:T(128)} %bitcast.135, s32[512]{0:T(512)S(1)} %iota_add_fusion.2, pred[3072]{0:T(1024)(128)(4,1)S(1)} %get-tuple-element.353, pred[3072]{0:T(1024)(128)(4,1)S(1)} %get-tuple-element.354, ...), kind=kOutput, calls=%fused_computation.19.clone.1 | convolution fusion | flops 218628096 | bytes 7231492 | tf_op jit(solution)/shard_map/while/body/eval_jaxpr/dot_general | solution.py:20
  242.5 4.3 %fusion.89 = f32[1,512,64]{1,2,0:T(8,128)S(1)} fusion(f32[512,3072]{1,0:T(8,128)S(1)} %bitcast.142, f32[3072]{0:T(1024)S(1)} %bitcast.159, f32[512]{0:T(512)S(1)} %bitcast.162, s32[]{:T(128)} %bitcast.135, s32[512]{0:T(512)S(1)} %iota_add_fusion.2, pred[3072]{0:T(1024)(128)(4,1)S(1)} %get-tuple-element.353, ...), kind=kOutput, calls=%fused_computation.18.clone.1 | convolution fusion | flops 218628096 | bytes 7231492 | tf_op jit(solution)/shard_map/while/body/eval_jaxpr/dot_general | solution.py:20
  246.9 7.4 %dynamic_update_slice.7 = bf16[4,512,128]{2,0,1:T(4,128)(2,1)} dynamic-update-slice(bf16[4,512,128]{2,0,1:T(4,128)(2,1)} %get-tuple-element.371, bf16[1,512,128]{2,0,1:T(2,128)(2,1)S(1)} %copy.187, s32[]{:T(128)S(6)} %copy.191, s32[]{:T(128)} %constant.27.clone.1..sunk, s32[]{:T(128)} %constant.27.clone.1..sunk) | dynamic-update-slice | bytes 262148 | tf_op jit(solution)/shard_map/while/body/jit(dynamic_update_index_in_dim)/dynamic_update_slice | solution.py:93
  255.6 1.3 dynamic_slice.76
  257.8 1.1 convolution_bitcast_fusion.4
  259.0 1.1 convolution_bitcast_fusion.5
  260.1 3.7 fusion.85
  264.5 1.3 dynamic_slice.77
  267.9 1.3 dynamic-slice_bitcast_fusion.10
  269.3 6.8 %fusion.88 = f32[1,512,64]{1,2,0:T(8,128)S(1)} fusion(f32[512,3072]{1,0:T(8,128)} %fusion.85, f32[3072]{0:T(1024)S(1)} %bitcast.160, f32[512]{0:T(512)S(1)} %bitcast.164, s32[]{:T(128)} %bitcast.135, s32[512]{0:T(512)S(1)} %iota_add_fusion.2, pred[3072]{0:T(1024)(128)(4,1)S(1)} %get-tuple-element.353, pred[3072]{0:T(1024)(128)(4,1)S(1)} %get-tuple-element.354, ...), kind=kOutput, calls=%fused_computation.19.clone.1 | convolution fusion | flops 218628096 | bytes 7231492 | tf_op jit(solution)/shard_map/while/body/eval_jaxpr/dot_general | solution.py:20
  276.2 4.3 %fusion.89 = f32[1,512,64]{1,2,0:T(8,128)S(1)} fusion(f32[512,3072]{1,0:T(8,128)S(1)} %bitcast.142, f32[3072]{0:T(1024)S(1)} %bitcast.159, f32[512]{0:T(512)S(1)} %bitcast.162, s32[]{:T(128)} %bitcast.135, s32[512]{0:T(512)S(1)} %iota_add_fusion.2, pred[3072]{0:T(1024)(128)(4,1)S(1)} %get-tuple-element.353, ...), kind=kOutput, calls=%fused_computation.18.clone.1 | convolution fusion | flops 218628096 | bytes 7231492 | tf_op jit(solution)/shard_map/while/body/eval_jaxpr/dot_general | solution.py:20
  280.6 7.4 %dynamic_update_slice.7 = bf16[4,512,128]{2,0,1:T(4,128)(2,1)} dynamic-update-slice(bf16[4,512,128]{2,0,1:T(4,128)(2,1)} %get-tuple-element.371, bf16[1,512,128]{2,0,1:T(2,128)(2,1)S(1)} %copy.187, s32[]{:T(128)S(6)} %copy.191, s32[]{:T(128)} %constant.27.clone.1..sunk, s32[]{:T(128)} %constant.27.clone.1..sunk) | dynamic-update-slice | bytes 262148 | tf_op jit(solution)/shard_map/while/body/jit(dynamic_update_index_in_dim)/dynamic_update_slice | solution.py:93
  289.3 1.3 dynamic_slice.76
  291.6 1.1 convolution_bitcast_fusion.4
  292.7 1.1 convolution_bitcast_fusion.5
  293.8 3.6 fusion.85
  298.3 1.3 dynamic_slice.77
  301.6 1.3 dynamic-slice_bitcast_fusion.10
  303.0 6.8 %fusion.88 = f32[1,512,64]{1,2,0:T(8,128)S(1)} fusion(f32[512,3072]{1,0:T(8,128)} %fusion.85, f32[3072]{0:T(1024)S(1)} %bitcast.160, f32[512]{0:T(512)S(1)} %bitcast.164, s32[]{:T(128)} %bitcast.135, s32[512]{0:T(512)S(1)} %iota_add_fusion.2, pred[3072]{0:T(1024)(128)(4,1)S(1)} %get-tuple-element.353, pred[3072]{0:T(1024)(128)(4,1)S(1)} %get-tuple-element.354, ...), kind=kOutput, calls=%fused_computation.19.clone.1 | convolution fusion | flops 218628096 | bytes 7231492 | tf_op jit(solution)/shard_map/while/body/eval_jaxpr/dot_general | solution.py:20
  309.9 4.3 %fusion.89 = f32[1,512,64]{1,2,0:T(8,128)S(1)} fusion(f32[512,3072]{1,0:T(8,128)S(1)} %bitcast.142, f32[3072]{0:T(1024)S(1)} %bitcast.159, f32[512]{0:T(512)S(1)} %bitcast.162, s32[]{:T(128)} %bitcast.135, s32[512]{0:T(512)S(1)} %iota_add_fusion.2, pred[3072]{0:T(1024)(128)(4,1)S(1)} %get-tuple-element.353, ...), kind=kOutput, calls=%fused_computation.18.clone.1 | convolution fusion | flops 218628096 | bytes 7231492 | tf_op jit(solution)/shard_map/while/body/eval_jaxpr/dot_general | solution.py:20
  314.3 7.4 %dynamic_update_slice.7 = bf16[4,512,128]{2,0,1:T(4,128)(2,1)} dynamic-update-slice(bf16[4,512,128]{2,0,1:T(4,128)(2,1)} %get-tuple-element.371, bf16[1,512,128]{2,0,1:T(2,128)(2,1)S(1)} %copy.187, s32[]{:T(128)S(6)} %copy.191, s32[]{:T(128)} %constant.27.clone.1..sunk, s32[]{:T(128)} %constant.27.clone.1..sunk) | dynamic-update-slice | bytes 262148 | tf_op jit(solution)/shard_map/while/body/jit(dynamic_update_index_in_dim)/dynamic_update_slice | solution.py:93
  321.7 24.4 %all_to_all.109 = bf16[4,512,128]{2,0,1:T(4,128)(2,1)S(1)} all-to-all(bf16[4,512,128]{2,0,1:T(4,128)(2,1)} %get-tuple-element.84), channel_id=1, replica_groups=mesh['tok'=64,'mlp'=4] {'tok'}, dimensions={1} | all-to-all | bytes 1048576 | tf_op jit(solution)/shard_map/all_to_all | solution.py:98
  346.6 12.9 %all_to_all.110 = bf16[4,8,8192]{2,0,1:T(4,128)(2,1)S(1)} all-to-all(bf16[4,8,8192]{2,0,1:T(4,128)(2,1)S(1)} %copy.166), channel_id=1, replica_groups=mesh['tok'=64,'mlp'=4] {'mlp'}, dimensions={1} | all-to-all | bytes 1048576 | tf_op jit(solution)/shard_map/all_to_all | solution.py:99
  360.1 2.5 fusion.56
  364.9 1.4 multiply_convert_fusion.4
  (119 shorter events, 30.3 us)
Async XLA Ops:
  12.9 23.2 %all-to-all-start = ((bf16[16,2,8,256]{3,2,1,0:T(8,128)(2,1)}), bf16[16,2,8,256]{3,2,1,0:T(8,128)(2,1)S(1)}, u32[]{:S(2)}, u32[]{:S(2)}) async-start(bf16[16,2,8,256]{3,2,1,0:T(8,128)(2,1)} %param.16), calls=%async_computation | async-start | bytes 262144 | tf_op jit(solution)/shard_map/all_to_all | solution.py:51
  24.9 49.9 %copy-start = (bf16[4,8,48,128]{3,2,1,0:T(8,128)(2,1)S(1)}, bf16[4,8,48,128]{3,2,1,0:T(8,128)(2,1)}, u32[]{:S(2)}) copy-start(bf16[4,8,48,128]{3,2,1,0:T(8,128)(2,1)} %param.20) | copy-start | bytes 1179652
  36.2 31.7 %all-to-all-start.3 = ((bf16[64,2,2048]{2,1,0:T(2,128)(2,1)}), bf16[64,2,2048]{2,1,0:T(2,128)(2,1)S(1)}, u32[]{:S(2)}, u32[]{:S(2)}) async-start(bf16[64,2,2048]{2,1,0:T(2,128)(2,1)} %reshape.174), calls=%async_computation.3 | async-start | bytes 1048576 | tf_op jit(solution)/shard_map/all_to_all | solution.py:54
  69.0 43.0 %copy-start.4 = (f32[2]{0:T(128)S(1)}, f32[2]{0:T(128)}, u32[]{:S(2)}) copy-start(f32[2]{0:T(128)} %param.18) | copy-start | bytes 28
  69.0 43.0 %copy-start.2 = (f32[4,512,2]{1,2,0:T(2,128)S(1)}, f32[4,512,2]{1,2,0:T(2,128)}, u32[]{:S(2)}) copy-start(f32[4,512,2]{1,2,0:T(2,128)} %param.17) | copy-start | bytes 49156
  69.0 34.0 %all-to-all-start.1 = ((bf16[4,8,64,256]{3,1,0,2:T(8,128)(2,1)}), bf16[4,8,64,256]{3,1,0,2:T(8,128)(2,1)S(1)}, u32[]{:S(2)}, u32[]{:S(2)}) async-start(bf16[4,8,64,256]{3,1,0,2:T(8,128)(2,1)} %bitcast.3), calls=%async_computation.1 | async-start | bytes 2097152 | tf_op jit(solution)/shard_map/all_to_all | solution.py:55
  105.5 78.8 %all-to-all-start.4 = ((bf16[4,64,48,128]{3,2,0,1:T(8,128)(2,1)}), bf16[4,64,48,128]{3,2,0,1:T(8,128)(2,1)}, u32[]{:S(2)}, u32[]{:S(2)}) async-start(bf16[4,64,48,128]{3,2,0,1:T(8,128)(2,1)} %bitcast.19), calls=%async_computation.4 | async-start | bytes 6291456 | tf_op jit(solution)/shard_map/all_to_all | solution.py:46
  111.9 12.1 %copy-start.1 = (f32[4,2,3072]{2,1,0:T(2,128)S(1)}, f32[4,2,3072]{2,1,0:T(2,128)}, u32[]{:S(2)}) copy-start(f32[4,2,3072]{2,1,0:T(2,128)} %param.21) | copy-start | bytes 294916
  200.5 8.2 %slice-start = ((s8[6291456]{0:T(1024)(128)(4,1)}), s8[4194304]{0:T(1024)(128)(4,1)S(1)}, s32[]{:S(2)}) async-start(s8[6291456]{0:T(1024)(128)(4,1)} %bitcast.141), calls=%async_computation.7 | async-start | bytes 8388608 | tf_op jit(solution)/shard_map/while
  201.9 6.9 %slice-start.1 = ((s8[6291456]{0:T(1024)(128)(4,1)}), s8[2097152]{0:T(1024)(128)(4,1)S(1)}, s32[]{:S(2)}) async-start(s8[6291456]{0:T(1024)(128)(4,1)} %bitcast.141), calls=%async_computation.8 | async-start | bytes 4194304 | tf_op jit(solution)/shard_map/while
  234.2 8.2 %slice-start = ((s8[6291456]{0:T(1024)(128)(4,1)}), s8[4194304]{0:T(1024)(128)(4,1)S(1)}, s32[]{:S(2)}) async-start(s8[6291456]{0:T(1024)(128)(4,1)} %bitcast.141), calls=%async_computation.7 | async-start | bytes 8388608 | tf_op jit(solution)/shard_map/while
  235.6 6.9 %slice-start.1 = ((s8[6291456]{0:T(1024)(128)(4,1)}), s8[2097152]{0:T(1024)(128)(4,1)S(1)}, s32[]{:S(2)}) async-start(s8[6291456]{0:T(1024)(128)(4,1)} %bitcast.141), calls=%async_computation.8 | async-start | bytes 4194304 | tf_op jit(solution)/shard_map/while
  267.9 8.2 %slice-start = ((s8[6291456]{0:T(1024)(128)(4,1)}), s8[4194304]{0:T(1024)(128)(4,1)S(1)}, s32[]{:S(2)}) async-start(s8[6291456]{0:T(1024)(128)(4,1)} %bitcast.141), calls=%async_computation.7 | async-start | bytes 8388608 | tf_op jit(solution)/shard_map/while
  269.3 6.9 %slice-start.1 = ((s8[6291456]{0:T(1024)(128)(4,1)}), s8[2097152]{0:T(1024)(128)(4,1)S(1)}, s32[]{:S(2)}) async-start(s8[6291456]{0:T(1024)(128)(4,1)} %bitcast.141), calls=%async_computation.8 | async-start | bytes 4194304 | tf_op jit(solution)/shard_map/while
  301.6 8.2 %slice-start = ((s8[6291456]{0:T(1024)(128)(4,1)}), s8[4194304]{0:T(1024)(128)(4,1)S(1)}, s32[]{:S(2)}) async-start(s8[6291456]{0:T(1024)(128)(4,1)} %bitcast.141), calls=%async_computation.7 | async-start | bytes 8388608 | tf_op jit(solution)/shard_map/while
  303.0 6.9 %slice-start.1 = ((s8[6291456]{0:T(1024)(128)(4,1)}), s8[2097152]{0:T(1024)(128)(4,1)S(1)}, s32[]{:S(2)}) async-start(s8[6291456]{0:T(1024)(128)(4,1)} %bitcast.141), calls=%async_computation.8 | async-start | bytes 4194304 | tf_op jit(solution)/shard_map/while
  346.2 18.7 %copy-start.3 = (f32[8192]{0:T(1024)S(1)}, f32[8192]{0:T(1024)}, u32[]{:S(2)}) copy-start(f32[8192]{0:T(1024)} %param.25) | copy-start | bytes 98308
where the time goes:
time: 370 us; the launch traced here: 366 us
  local copies, waits for them, and re-layouts  119 us (32%)
  waiting for transfers between devices  78 us (21%)
  matrix products  68.9 us (19%)
  blocking collectives  50.2 us (14%)
  starting transfers between devices  29.6 us (8%)
  other arithmetic  19.4 us (5%)
    dot_general x16, matrix products, weighted_sum(): pieces.append(jnp.dot(weighted, values, preferred_element_type=jnp.float32))  53.2 us
    all_to_all x1, waiting for transfers between devices, per_device(): lax.all_to_all(jnp.repeat(b_cache, copies, axis=1), 'tok', split_axis=1,...  32.2 us
    dynamic_update_slice x8, local copies, waits for them, and re-layouts, per_device(): lax.map(one_request, (head_bc, scaled, cum_new, tail_sum, x_cache, shared...  30.2 us
    all_to_all x1, waiting for transfers between devices, per_device(): lax.all_to_all(jnp.repeat(owned_bc, copies, axis=2), 'tok', split_axis=2,...  28.1 us
    all_to_all x1, blocking collectives, per_device(): lax.all_to_all(mixer_out, 'tok', split_axis=1, concat_axis=2, tiled=True)  24.4 us
    unnamed x16, local copies, waits for them, and re-layouts  22.8 us
    all_to_all x1, waiting for transfers between devices, per_device(): lax.all_to_all(owned_x, 'tok', split_axis=2, concat_axis=1, tiled=True)  17.6 us
    dot_general x8, matrix products, weighted_sum(): scores = jnp.dot(queries, key_b.T, preferred_element_type=jnp.float32)  15.8 us
  transfers between devices with their start and end apart: 4, of which 3 were waited for; matrix products, arithmetic and copies ran while one was open for 16% of the time, Pallas kernels for 0%

commit v1 on v0

v1 whole, which is shorter than its diff:
```python
import jax
import jax.numpy as jnp
from jax import lax
from jax.sharding import PartitionSpec as P

EPS = 1e-05


def per_device(
    new_x,
    gate_input,
    state_proj,
    step_size,
    decay_rate,
    x_cache,
    b_cache,
    decay_cache,
    lengths,
    sink_pos,
    windows,
    norm_gain,
):
    n_tok = lax.axis_size("tok")
    n_mlp = lax.axis_size("mlp")
    n_dev = n_tok * n_mlp
    groups = state_proj.shape[2]
    state_dim = b_cache.shape[3]
    copies = n_tok // groups
    heads_dev = decay_rate.shape[0]
    requests = step_size.shape[0]
    new_len = step_size.shape[1]
    tok_blk = new_x.shape[1]
    cache_len = x_cache.shape[1]
    chans = x_cache.shape[2]
    head_dim = chans // heads_dev

    x_part = new_x.reshape(n_mlp, requests, tok_blk, n_tok, chans).transpose(3, 0, 1, 2, 4)
    sp = state_proj.reshape(n_mlp, requests, tok_blk, groups, 2 * state_dim)
    sp = jnp.repeat(sp, copies, axis=3).transpose(3, 0, 1, 2, 4)
    packed = jnp.concatenate([x_part, sp], axis=-1).reshape(n_dev, requests, tok_blk, -1)
    got = lax.all_to_all(packed, ("tok", "mlp"), 0, 0, tiled=True)
    got = got.transpose(1, 0, 2, 3).reshape(requests, new_len, -1)
    head_x = got[..., :chans]
    b_new = got[..., chans : chans + state_dim]
    c_now = got[..., chans + state_dim :]

    shared_b = lax.all_to_all(
        jnp.repeat(b_cache, copies, axis=1), "tok", split_axis=1, concat_axis=2, tiled=True
    )[:, 0]

    head_decay_values = jnp.exp(decay_rate)
    cum_new = jnp.cumsum(-(step_size * head_decay_values), axis=1)
    scaled = head_x.astype(jnp.float32).reshape(requests, new_len, heads_dev, head_dim)
    scaled = (scaled * step_size[..., None]).astype(jnp.bfloat16)

    positions = jnp.arange(cache_len, dtype=jnp.int32)
    token_order = jnp.arange(new_len, dtype=jnp.int32)
    live = positions[None, :] < lengths[:, None]
    masked = jnp.where(live[:, None, :], decay_cache, 0.0)
    local_sum = jnp.cumsum(masked, axis=2)
    tail_sum = local_sum[:, :, -1:] - local_sum

    col_scale = jnp.exp(tail_sum)
    row_scale = jnp.exp(cum_new)
    x_scaled = x_cache.astype(jnp.float32).reshape(requests, cache_len, heads_dev, head_dim)
    x_scaled = x_scaled * col_scale.transpose(0, 2, 1)[..., None]
    x_scaled = x_scaled.reshape(requests, cache_len, chans)
    x_hi = x_scaled.astype(jnp.bfloat16)
    x_lo = (x_scaled - x_hi.astype(jnp.float32)).astype(jnp.bfloat16)
    x_pair = jnp.concatenate([x_hi, x_lo], axis=-1)

    query_pos = lengths[:, None] + token_order[None, :]
    in_window = (query_pos[:, :, None] - positions[None, None, :] < windows[:, None, None]) & live[
        :, None, :
    ]
    score_old = jnp.einsum("rnk,rsk->rns", c_now, shared_b, preferred_element_type=jnp.float32)
    probs_old = jnp.where(in_window, score_old, 0.0).astype(jnp.bfloat16)
    acc = jnp.einsum("rns,rsc->rnc", probs_old, x_pair, preferred_element_type=jnp.float32)
    old_out = (acc[..., :chans] + acc[..., chans:]).reshape(requests, new_len, heads_dev, head_dim)
    old_out = old_out * row_scale[..., None]

    sink_b = jnp.take_along_axis(shared_b, sink_pos[:, :, None], axis=1)
    sink_x = jnp.take_along_axis(x_cache, sink_pos[:, :, None], axis=1)
    sink_live = sink_pos < lengths[:, None]
    sink_gap = query_pos[:, :, None] - sink_pos[:, None, :]
    sink_only = sink_live[:, None, :] & jnp.logical_not(sink_gap < windows[:, None, None])
    score_sink = jnp.einsum("rnk,rjk->rnj", c_now, sink_b, preferred_element_type=jnp.float32)
    probs_sink = jnp.where(sink_only, score_sink, 0.0).astype(jnp.bfloat16)
    sink_out = jnp.einsum("rnj,rjc->rnc", probs_sink, sink_x, preferred_element_type=jnp.float32)

    score_new = jnp.einsum("rnk,rjk->rnj", c_now, b_new, preferred_element_type=jnp.float32)
    new_gap = token_order[:, None] - token_order[None, :]
    keep_new = (new_gap[None] >= 0) & (new_gap[None] < windows[:, None, None])
    cum_t = cum_new.transpose(0, 2, 1)
    decay_new = jnp.exp(jnp.minimum(cum_t[:, :, :, None] - cum_t[:, :, None, :], 0.0))
    weight_new = jnp.where(keep_new[:, None], decay_new, 0.0)
    probs_new = (score_new[:, None] * weight_new).astype(jnp.bfloat16)
    new_out = jnp.einsum("rhnj,rjhd->rnhd", probs_new, scaled, preferred_element_type=jnp.float32)

    mixer_out = (old_out + new_out).reshape(requests, new_len, chans) + sink_out
    mixer_out = mixer_out.astype(jnp.bfloat16)

    back = mixer_out.reshape(requests, n_dev, tok_blk, chans).transpose(1, 0, 2, 3)
    back = lax.all_to_all(back, ("tok", "mlp"), 0, 0, tiled=True)
    back = back.reshape(n_tok, n_mlp, requests, tok_blk, chans).transpose(1, 2, 3, 0, 4)
    mixer_tok = lax.optimization_barrier(back.reshape(n_mlp * requests, tok_blk, n_tok * chans))

    gated_out = mixer_tok.astype(jnp.float32) * jax.nn.silu(gate_input.astype(jnp.float32))
    grouped = gated_out.reshape(gated_out.shape[0], gated_out.shape[1], groups, -1)
    norm_scale = lax.rsqrt(jnp.mean(grouped * grouped, axis=-1, keepdims=True) + EPS)
    normed = (grouped * norm_scale).reshape(gated_out.shape) * norm_gain
    return normed.astype(jnp.bfloat16)


def solution(mesh):
    return jax.shard_map(
        per_device,
        mesh=mesh,
        in_specs=(
            P(None, ("tok", "mlp"), None),
            P(None, ("tok", "mlp"), None),
            P(None, ("tok", "mlp"), None, None),
            P("mlp", None, "tok"),
            P("tok"),
            P("mlp", None, "tok"),
            P("mlp", None, "tok", None),
            P("mlp", "tok", None),
            P("mlp"),
            P("mlp", None),
            P("mlp"),
            P(),
        ),
        out_specs=P(None, ("tok", "mlp"), None),
        check_vma=False,
    )
```

time: 370 us -> 201 us (0.54)
  local copies, waits for them, and re-layouts: 119 us -> 24.8 us
  matrix products: 68.9 us -> 22.2 us
  blocking collectives: 50.2 us -> 27.5 us
  starting transfers between devices: 29.6 us -> 21.2 us
  waiting for transfers between devices: 78 us -> 83.5 us
    dot_general x24 -> x4, matrix products: 68.9 us -> 22.2 us  [the longest x1 12.1 us: per_device(): jnp.einsum('rns,rsc->rnc', probs_old, x_pair, preferred_element_type=jnp....]
    dynamic_update_slice x8 -> x0, local copies, waits for them, and re-layouts: 30.2 us -> none  [per_device(): lax.map(one_request, (head_bc, scaled, cum_new, tail_sum, x_cache, shared...]
    all_to_all x3 -> x1, blocking collectives: 50.2 us -> 27.5 us  [per_device(): back = lax.all_to_all(back, ('tok', 'mlp'), 0, 0, tiled=True)]
    all_to_all x9 -> x0, local copies, waits for them, and re-layouts: 20.5 us -> none  [the longest x1 9.73 us: per_device(): lax.all_to_all(owned_x, 'tok', split_axis=2, concat_axis=1, tiled=True)]
    unnamed x16 -> x29, local copies, waits for them, and re-layouts: 22.8 us -> 4.91 us
    squeeze x12 -> x0, local copies, waits for them, and re-layouts: 12.9 us -> none  [per_device(): lax.map(one_request, (head_bc, scaled, cum_new, tail_sum, x_cache, shared...]
    dynamic_slice x8 -> x0, local copies, waits for them, and re-layouts: 10.3 us -> none  [per_device(): lax.map(one_request, (head_bc, scaled, cum_new, tail_sum, x_cache, shared...]
    all_to_all x1, waiting for transfers between devices: 32.2 us -> 41.6 us  [per_device(): lax.all_to_all(jnp.repeat(b_cache, copies, axis=1), 'tok', split_axis=1,...]
  transfers between devices with their start and end apart: 4 -> 2, of which waited for: 3 -> 2; matrix products, arithmetic and copies ran while one was open for 16% -> 15% of each run, Pallas kernels for 0% -> 0%
where the time goes in v1:
time: 201 us; the launch traced here: 200 us
  waiting for transfers between devices  83.5 us (42%)
  blocking collectives  27.5 us (14%)
  local copies, waits for them, and re-layouts  24.8 us (12%)
  matrix products  22.2 us (11%)
  starting transfers between devices  21.2 us (11%)
  other arithmetic  20.8 us (10%)
    all_to_all x1, waiting for transfers between devices, per_device(): got = lax.all_to_all(packed, ('tok', 'mlp'), 0, 0, tiled=True)  41.9 us
    all_to_all x1, waiting for transfers between devices, per_device(): lax.all_to_all(jnp.repeat(b_cache, copies, axis=1), 'tok', split_axis=1,...  41.6 us
    all_to_all x1, blocking collectives, per_device(): back = lax.all_to_all(back, ('tok', 'mlp'), 0, 0, tiled=True)  27.5 us
    all_to_all x1, starting transfers between devices, per_device(): got = lax.all_to_all(packed, ('tok', 'mlp'), 0, 0, tiled=True)  15.6 us
    dot_general x1, matrix products, per_device(): jnp.einsum('rns,rsc->rnc', probs_old, x_pair, preferred_element_type=jnp....  12.1 us
    another operation x6, other arithmetic  6.42 us
    convert_element_type x1, other arithmetic, per_device(): x_hi = x_scaled.astype(jnp.bfloat16)  5.77 us
    dot_general x1, matrix products, per_device(): jnp.einsum('rhnj,rjhd->rnhd', probs_new, scaled, preferred_element_type=j...  5.67 us
  transfers between devices with their start and end apart: 2, of which 2 were waited for; matrix products, arithmetic and copies ran while one was open for 15% of the time, Pallas kernels for 0%

profile of v1, /device:TPU:1, one launch (start us, length us, event | category | flops | bytes accessed | tf_op | source)
XLA Modules:
  0.0 200.5 jit_solution(14063526025793134945)
XLA Ops:
  0.0 1.0 copy.66
  1.0 1.4 reshape.170
  2.4 0.0 copy-start.5
  2.4 0.4 copy.67
  2.8 0.5 broadcast_in_dim.38
  3.3 1.9 pad_maximum_fusion
  5.2 15.6 %all-to-all-start = ((bf16[256,4,2,384]{3,1,2,0:T(4,128)(2,1)}), bf16[256,4,2,384]{3,1,2,0:T(4,128)(2,1)S(1)}, u32[]{:S(2)}, u32[]{:S(2)}) async-start(bf16[256,4,2,384]{3,1,2,0:T(4,128)(2,1)} %bitcast.4), calls=%async_computation | async-start | bytes 3145728 | tf_op jit(solution)/shard_map/all_to_all | solution.py:41
  20.9 0.0 copy-start.10
  21.0 0.0 copy-start.6
  21.0 41.9 %all-to-all-done = bf16[256,4,2,384]{3,1,2,0:T(4,128)(2,1)S(1)} async-done(((bf16[256,4,2,384]{3,1,2,0:T(4,128)(2,1)}), bf16[256,4,2,384]{3,1,2,0:T(4,128)(2,1)S(1)}, u32[]{:S(2)}, u32[]{:S(2)}) %all-to-all-start) | async-done | bytes 1572896 | tf_op jit(solution)/shard_map/all_to_all | solution.py:41
  62.9 2.4 %broadcast_in_dim.39 = bf16[4,8,8,48,128]{4,3,0,2,1:T(8,128)(2,1)} broadcast(bf16[4,8,48,128]{3,2,0,1:T(8,128)(2,1)S(1)} %copy.69), dimensions={0,1,3,4} | broadcast | bytes 3538944 | tf_op jit(solution)/shard_map/broadcast_in_dim | solution.py:48
  65.4 5.5 %all-to-all-start.1 = ((bf16[4,64,48,128]{3,2,0,1:T(8,128)(2,1)}), bf16[4,64,48,128]{3,2,0,1:T(8,128)(2,1)S(1)}, u32[]{:S(2)}, u32[]{:S(2)}) async-start(bf16[4,64,48,128]{3,2,0,1:T(8,128)(2,1)} %bitcast.62), calls=%async_computation.1 | async-start | bytes 6291456 | tf_op jit(solution)/shard_map/all_to_all | solution.py:47
  70.9 0.0 copy-start.12
  70.9 0.0 copy-start.9
  70.9 0.1 iota_compare_fusion
  71.0 0.1 broadcast_select_fusion
  71.1 0.1 reshape.176
  71.2 2.3 %reduce-window.14 = f32[4,2,24,128]{3,2,1,0:T(8,128)S(1)} reduce-window(f32[4,2,24,128]{3,2,1,0:T(8,128)S(1)} %reshape.176, f32[]{:T(128)} %constant.13.clone.1), window={size=1x1x1x128 pad=0_0x0_0x0_0x127_0}, to_apply=%region_0.0 | reduce-window | flops 3121152 | bytes 196612 | tf_op jit(solution)/shard_map/reduce-window
  73.5 0.2 slice_reduce_fusion
  73.7 0.8 reduce-window.15
  74.5 0.1 broadcast_add_fusion
  74.6 0.1 reduce_window_sum.39
  74.7 0.1 slice.47
  74.7 0.1 copy.83
  74.8 0.1 copy.73
  74.9 4.7 %copy.71 = bf16[4,3072,128]{1,2,0:T(8,128)(2,1)} copy(bf16[4,3072,128]{2,1,0:T(8,128)(2,1)} %param.19) | data formatting | bytes 6291456 | tf_op args[5]
  79.7 0.1 negate_bitcast_fusion
  79.8 2.4 %reduce-window.16 = f32[4,2,4,128]{3,2,1,0:T(4,128)S(1)} reduce-window(f32[4,2,4,128]{3,2,1,0:T(4,128)S(1)} %reshape.179, f32[]{:T(128)} %constant.13.clone.1), window={size=1x1x1x128 pad=0_0x0_0x0_0x127_0}, to_apply=%region_2.3 | reduce-window | flops 520192 | bytes 32772 | tf_op jit(solution)/shard_map/reduce-window.2
  82.2 0.2 slice_reduce_fusion.1
  82.4 0.7 reduce-window.19
  83.1 0.1 broadcast_add_fusion.1
  83.2 0.1 reshape.201
  83.3 1.4 gather_fusion.1
  84.7 0.1 exponential_bitcast_fusion
  84.8 5.8 %fusion.6 = (bf16[4,3072,128]{1,2,0:T(8,128)(2,1)}, bf16[4,3072,128]{1,2,0:T(8,128)(2,1)}) fusion(bf16[4,3072,128]{1,2,0:T(8,128)(2,1)} %copy.71, f32[4,3072,2]{1,2,0:T(2,128)S(1)} %exponential_bitcast_fusion), kind=kLoop, calls=%fused_computation.13 | loop fusion | flops 9437184 | bytes 9535488 | tf_op jit(solution)/shard_map/convert_element_type | solution.py:68
  90.6 0.1 broadcast_compare_fusion
  90.7 0.1 iota_subtract_fusion
  90.8 0.1 broadcast_compare_fusion.1
  90.9 0.1 iota_add_fusion
  91.0 1.7 compare_and_fusion
  92.8 1.5 fusion.49
  94.3 1.1 copy_convert_fusion
  95.3 2.5 %copy.75 = f32[4,512,128]{1,2,0:T(8,128)} copy(f32[4,512,128]{2,1,0:T(8,128)} %copy_convert_fusion) | data formatting | bytes 2097152 | tf_op jit(solution)/shard_map/reshape | solution.py:53
  97.9 3.8 %fusion.18 = f32[4,512,512]{2,1,0:T(8,128)} fusion(bf16[4,512,128]{2,0,1:T(4,128)(2,1)} %get-tuple-element.12, bf16[4,512,128]{2,0,1:T(4,128)(2,1)} %get-tuple-element.11), kind=kOutput, calls=%fused_computation.34 | convolution fusion | flops 268435456 | bytes 5242880 | tf_op jit(solution)/shard_map/rnk,rjk->rnj/dot_general | solution.py:91
  101.7 41.6 %all-to-all-done.1 = bf16[4,64,48,128]{3,2,0,1:T(8,128)(2,1)S(1)} async-done(((bf16[4,64,48,128]{3,2,0,1:T(8,128)(2,1)}), bf16[4,64,48,128]{3,2,0,1:T(8,128)(2,1)S(1)}, u32[]{:S(2)}, u32[]{:S(2)}) %all-to-all-start.1) | async-done | bytes 3145760 | tf_op jit(solution)/shard_map/all_to_all | solution.py:47
  143.3 2.2 %copy.70 = bf16[4,64,48,128]{3,2,1,0:T(8,128)(2,1)} copy(bf16[4,64,48,128]{3,2,0,1:T(8,128)(2,1)S(1)} %all-to-all-done.1) | data formatting | bytes 6291456 | tf_op jit(solution)/shard_map/all_to_all | solution.py:47
  145.5 1.3 gather_fusion
  146.8 12.1 %fusion.1 = f32[4,512,256]{1,2,0:T(8,128)S(1)} fusion(s32[4]{0:T(128)S(1)} %copy-done.11, s32[4,512]{1,0:T(4,128)S(1)} %iota_add_fusion, pred[4,3072]{1,0:T(4,128)(4,1)S(1)} %iota_compare_fusion, bf16[4,3072,128]{1,2,0:T(8,128)(2,1)} %get-tuple-element.9, bf16[4,3072,128]{1,2,0:T(8,128)(2,1)} %get-tuple-element.8, bf16[4,3072,128]{2,1,0:T(8,128)(2,1)} %bitcast.66, ...), kind=kOutput, calls=%fused_computation.5 | convolution fusion | flops 4875878400 | bytes 12079120 | tf_op jit(solution)/shard_map/rns,rsc->rnc/dot_general | solution.py:78
  158.9 0.2 slice_add_fusion
  159.2 5.7 %fusion.12 = f32[4,512,2,64]{1,3,2,0:T(8,128)} fusion(f32[4,2,512]{2,1,0:T(2,128)S(1)} %reduce_window_sum.41, f32[4,512,512]{2,1,0:T(8,128)} %fusion.18, pred[4,512,512]{2,1,0:T(8,128)(4,1)S(1)} %copy-done.3, f32[4,512,2,64]{1,3,2,0:T(8,128)S(1)} %bitcast.71, f32[4,512,2,64]{1,3,2,0:T(8,128)} %bitcast.72, f32[4,512,2]{1,2,0:T(2,128)S(1)} %copy-done.9, ...), kind=kOutput, calls=%fused_computation.21 | convolution fusion | flops 279969792 | bytes 8437760 | tf_op jit(solution)/shard_map/rhnj,rjhd->rnhd/dot_general | solution.py:98
  164.8 1.6 copy.77
  166.4 0.6 fusion.13
  167.0 0.4 copy.98
  167.4 27.5 %all_to_all.19 = bf16[256,4,2,128]{3,2,1,0:T(2,128)(2,1)S(1)} all-to-all(bf16[256,4,2,128]{3,2,1,0:T(2,128)(2,1)S(1)} %bitcast.67), channel_id=1, replica_groups=mesh['tok'=64,'mlp'=4] {'tok','mlp'}, dimensions={0} | all-to-all | bytes 1048576 | tf_op jit(solution)/shard_map/all_to_all | solution.py:104
  195.0 0.2 copy.79
  195.2 0.1 reshape.186
  195.3 1.5 fusion.47
  196.8 0.9 mul.89
  197.7 0.2 reduce_sum.9
  197.9 0.1 copy.80
  197.9 0.1 copy.81
  198.0 0.1 mul.90
  198.2 0.9 mul.91
  199.1 1.4 multiply_convert_fusion.6
  (29 shorter events, 0.2 us)
Async XLA Ops:
  2.4 18.5 %copy-start.5 = (bf16[4,8,48,128]{3,2,1,0:T(8,128)(2,1)S(1)}, bf16[4,8,48,128]{3,2,1,0:T(8,128)(2,1)}, u32[]{:S(2)}) copy-start(bf16[4,8,48,128]{3,2,1,0:T(8,128)(2,1)} %param.20) | copy-start | bytes 1179652
  5.2 57.7 %all-to-all-start = ((bf16[256,4,2,384]{3,1,2,0:T(4,128)(2,1)}), bf16[256,4,2,384]{3,1,2,0:T(4,128)(2,1)S(1)}, u32[]{:S(2)}, u32[]{:S(2)}) async-start(bf16[256,4,2,384]{3,1,2,0:T(4,128)(2,1)} %bitcast.4), calls=%async_computation | async-start | bytes 3145728 | tf_op jit(solution)/shard_map/all_to_all | solution.py:41
  20.9 49.9 %copy-start.10 = (s32[4]{0:T(128)S(1)}, s32[4]{0:T(128)}, u32[]{:S(2)}) copy-start(s32[4]{0:T(128)} %param.22) | copy-start | bytes 52
  21.0 50.1 %copy-start.6 = (f32[4,2,3072]{2,1,0:T(2,128)S(1)}, f32[4,2,3072]{2,1,0:T(2,128)}, u32[]{:S(2)}) copy-start(f32[4,2,3072]{2,1,0:T(2,128)} %param.21) | copy-start | bytes 294916
  62.9 2.4 %copy-start = (bf16[256,4,2,384]{3,1,2,0:T(4,128)(2,1)}, bf16[256,4,2,384]{3,1,2,0:T(4,128)(2,1)S(1)}, u32[]{:S(2)}) copy-start(bf16[256,4,2,384]{3,1,2,0:T(4,128)(2,1)S(1)} %all-to-all-done) | copy-start | bytes 4718596
  65.4 77.9 %all-to-all-start.1 = ((bf16[4,64,48,128]{3,2,0,1:T(8,128)(2,1)}), bf16[4,64,48,128]{3,2,0,1:T(8,128)(2,1)S(1)}, u32[]{:S(2)}, u32[]{:S(2)}) async-start(bf16[4,64,48,128]{3,2,0,1:T(8,128)(2,1)} %bitcast.62), calls=%async_computation.1 | async-start | bytes 6291456 | tf_op jit(solution)/shard_map/all_to_all | solution.py:47
  70.9 8.8 %copy-start.12 = (f32[2]{0:T(128)S(1)}, f32[2]{0:T(128)}, u32[]{:S(2)}) copy-start(f32[2]{0:T(128)} %param.18) | copy-start | bytes 28
  70.9 8.7 %copy-start.9 = (f32[4,512,2]{1,2,0:T(2,128)S(1)}, f32[4,512,2]{1,2,0:T(2,128)}, u32[]{:S(2)}) copy-start(f32[4,512,2]{1,2,0:T(2,128)} %param.17) | copy-start | bytes 49156
  70.9 12.3 %copy-start.8 = (s32[4,4]{1,0:T(4,128)S(1)}, s32[4,4]{1,0:T(4,128)}, u32[]{:S(2)}) copy-start(s32[4,4]{1,0:T(4,128)} %param.23) | copy-start | bytes 196
  84.8 6.2 %copy-start.11 = (s32[4]{0:T(128)S(1)}, s32[4]{0:T(128)}, u32[]{:S(2)}) copy-start(s32[4]{0:T(128)} %param.24) | copy-start | bytes 52
  90.6 2.2 %copy-start.1 = (bf16[256,4,2,384]{3,1,2,0:T(4,128)(2,1)S(1)}, bf16[256,4,2,384]{3,1,2,0:T(4,128)(2,1)}, u32[]{:S(2)}) copy-start(bf16[256,4,2,384]{3,1,2,0:T(4,128)(2,1)} %copy-done) | copy-start | bytes 4718596
  146.8 12.3 %copy-start.3 = (pred[4,512,512]{2,1,0:T(8,128)(4,1)S(1)}, pred[4,512,512]{2,1,0:T(8,128)(4,1)}, u32[]{:S(2)}) copy-start(pred[4,512,512]{2,1,0:T(8,128)(4,1)} %compare_and_fusion) | copy-start | bytes 3145732
  159.1 7.3 %copy-start.2 = (bf16[4,512,128]{2,0,1:T(4,128)(2,1)S(1)}, bf16[4,512,128]{2,0,1:T(4,128)(2,1)}, u32[]{:S(2)}) copy-start(bf16[4,512,128]{2,0,1:T(4,128)(2,1)} %get-tuple-element.11) | copy-start | bytes 1572868
  164.8 30.5 %copy-start.4 = (bf16[16,2,8192]{2,1,0:T(2,128)(2,1)S(1)}, bf16[16,2,8192]{2,1,0:T(2,128)(2,1)}, u32[]{:S(2)}) copy-start(bf16[16,2,8192]{2,1,0:T(2,128)(2,1)} %param.15) | copy-start | bytes 1572868
  195.3 3.8 %copy-start.7 = (f32[8192]{0:T(1024)S(1)}, f32[8192]{0:T(1024)}, u32[]{:S(2)}) copy-start(f32[8192]{0:T(1024)} %param.25) | copy-start | bytes 98308

commit v2 on v1

--- a/solution.py
+++ b/solution.py
@@ -1,9 +1,10 @@
 import jax
 import jax.numpy as jnp
 from jax import lax
-from jax.sharding import PartitionSpec as P
+from jax.sharding import Mesh, PartitionSpec as P
 
 EPS = 1e-05
+GROUPS = 8
 
 
 def per_device(
@@ -20,12 +21,13 @@
     windows,
     norm_gain,
 ):
-    n_tok = lax.axis_size("tok")
+    n_tz = lax.axis_size("tz")
+    n_txc = lax.axis_size("txc")
+    n_tok = n_tz * n_txc
     n_mlp = lax.axis_size("mlp")
     n_dev = n_tok * n_mlp
     groups = state_proj.shape[2]
     state_dim = b_cache.shape[3]
-    copies = n_tok // groups
     heads_dev = decay_rate.shape[0]
     requests = step_size.shape[0]
     new_len = step_size.shape[1]
@@ -34,19 +36,23 @@
     chans = x_cache.shape[2]
     head_dim = chans // heads_dev
 
+    part_b = lax.all_to_all(b_cache, "tz", split_axis=1, concat_axis=1, tiled=True)
+    shared_b = lax.all_gather(part_b, "txc", axis=2)
+    shared_b = shared_b.reshape(requests, cache_len, state_dim)
+
+    sp = state_proj.reshape(n_mlp, requests, tok_blk, groups, 2 * state_dim)
+    sp = sp.transpose(3, 0, 1, 2, 4).reshape(groups * n_mlp, requests, tok_blk, -1)
+    sp = lax.all_to_all(sp, ("tz", "mlp"), 0, 0, tiled=True)
+    sp = lax.all_gather(sp, "txc", axis=1)
+    sp = sp.reshape(n_tz, n_mlp, n_txc, requests, tok_blk, -1).transpose(3, 0, 2, 1, 4, 5)
+    sp = sp.reshape(requests, new_len, -1)
+    b_new = sp[..., :state_dim]
+    c_now = sp[..., state_dim:]
+
     x_part = new_x.reshape(n_mlp, requests, tok_blk, n_tok, chans).transpose(3, 0, 1, 2, 4)
-    sp = state_proj.reshape(n_mlp, requests, tok_blk, groups, 2 * state_dim)
-    sp = jnp.repeat(sp, copies, axis=3).transpose(3, 0, 1, 2, 4)
-    packed = jnp.concatenate([x_part, sp], axis=-1).reshape(n_dev, requests, tok_blk, -1)
-    got = lax.all_to_all(packed, ("tok", "mlp"), 0, 0, tiled=True)
-    got = got.transpose(1, 0, 2, 3).reshape(requests, new_len, -1)
-    head_x = got[..., :chans]
-    b_new = got[..., chans : chans + state_dim]
-    c_now = got[..., chans + state_dim :]
-
-    shared_b = lax.all_to_all(
-        jnp.repeat(b_cache, copies, axis=1), "tok", split_axis=1, concat_axis=2, tiled=True
-    )[:, 0]
+    x_part = x_part.reshape(n_dev, requests, tok_blk, chans)
+    head_x = lax.all_to_all(x_part, ("tz", "txc", "mlp"), 0, 0, tiled=True)
+    head_x = head_x.transpose(1, 0, 2, 3).reshape(requests, new_len, chans)
 
     head_decay_values = jnp.exp(decay_rate)
     cum_new = jnp.cumsum(-(step_size * head_decay_values), axis=1)
@@ -101,7 +107,7 @@
     mixer_out = mixer_out.astype(jnp.bfloat16)
 
     back = mixer_out.reshape(requests, n_dev, tok_blk, chans).transpose(1, 0, 2, 3)
-    back = lax.all_to_all(back, ("tok", "mlp"), 0, 0, tiled=True)
+    back = lax.all_to_all(back, ("tz", "txc", "mlp"), 0, 0, tiled=True)
     back = back.reshape(n_tok, n_mlp, requests, tok_blk, chans).transpose(1, 2, 3, 0, 4)
     mixer_tok = lax.optimization_barrier(back.reshape(n_mlp * requests, tok_blk, n_tok * chans))
 
@@ -113,23 +119,26 @@
 
 
 def solution(mesh):
+    n_tok, n_mlp = mesh.shape["tok"], mesh.shape["mlp"]
+    split = Mesh(mesh.devices.reshape(GROUPS, n_tok // GROUPS, n_mlp), ("tz", "txc", "mlp"))
+    tok = ("tz", "txc")
     return jax.shard_map(
         per_device,
-        mesh=mesh,
+        mesh=split,
         in_specs=(
-            P(None, ("tok", "mlp"), None),
-            P(None, ("tok", "mlp"), None),
-            P(None, ("tok", "mlp"), None, None),
-            P("mlp", None, "tok"),
-            P("tok"),
-            P("mlp", None, "tok"),
-            P("mlp", None, "tok", None),
-            P("mlp", "tok", None),
+            P(None, (*tok, "mlp"), None),
+            P(None, (*tok, "mlp"), None),
+            P(None, (*tok, "mlp"), None, None),
+            P("mlp", None, tok),
+            P(tok),
+            P("mlp", None, tok),
+            P("mlp", None, tok, None),
+            P("mlp", tok, None),
             P("mlp"),
             P("mlp", None),
             P("mlp"),
             P(),
         ),
-        out_specs=P(None, ("tok", "mlp"), None),
+        out_specs=P(None, (*tok, "mlp"), None),
         check_vma=False,
     )

time: 201 us -> 165 us (0.82)
  waiting for transfers between devices: 83.5 us -> 9.62 us
  blocking collectives: 27.5 us -> 54.8 us
  between operations: 0.37 us -> 13.8 us
  starting transfers between devices: 21.2 us -> 13.7 us
  other arithmetic: 20.8 us -> 24.8 us
    all_to_all x2, waiting for transfers between devices: 83.5 us -> 9.09 us  [the longest x1 9.09 us: per_device(): lax.all_to_all(b_cache, 'tz', split_axis=1, concat_axis=1, tiled=True)]
    all_to_all x1 -> x2, blocking collectives: 27.5 us -> 54.8 us  [the longest x1 33.5 us: per_device(): back = lax.all_to_all(back, ('tz', 'txc', 'mlp'), 0, 0, tiled=True)]
    all_to_all x2, starting transfers between devices: 21.2 us -> 13.4 us  [the longest x1 10 us: per_device(): head_x = lax.all_to_all(x_part, ('tz', 'txc', 'mlp'), 0, 0, tiled=True)]
    convert_element_type x0 -> x2, other arithmetic: none -> 6.69 us  [the longest x1 5.28 us: per_device(): scaled = (scaled * step_size[..., None]).astype(jnp.bfloat16)]
    all_gather x0 -> x1, local copies, waits for them, and re-layouts: none -> 3.87 us  [per_device(): shared_b = lax.all_gather(part_b, 'txc', axis=2)]
    broadcast_in_dim x2 -> x0, local copies, waits for them, and re-layouts: 2.93 us -> none  [the longest x1 2.44 us: per_device(): jnp.repeat(b_cache, copies, axis=1)]
    convert_element_type x0 -> x2, local copies, waits for them, and re-layouts: none -> 2.24 us  [per_device(): head_x.astype(jnp.float32).reshape(requests, new_len, heads_dev, head_dim)]
    all_to_all x1 -> x0, local copies, waits for them, and re-layouts: 2.22 us -> none  [per_device(): lax.all_to_all(jnp.repeat(b_cache, copies, axis=1), 'tok', split_axis=1,...]
  transfers between devices with their start and end apart: 2 -> 4, of which waited for: 2 -> 1; matrix products, arithmetic and copies ran while one was open for 15% -> 25% of each run, Pallas kernels for 0% -> 0%
where the time goes in v2:
time: 165 us; the launch traced here: 164 us
  blocking collectives  54.8 us (33%)
  local copies, waits for them, and re-layouts  26.4 us (16%)
  other arithmetic  24.8 us (15%)
  matrix products  20.9 us (13%)
  between operations  13.8 us (8%)
  starting transfers between devices  13.7 us (8%)
  waiting for transfers between devices  9.62 us (6%)
    all_to_all x1, blocking collectives, per_device(): back = lax.all_to_all(back, ('tz', 'txc', 'mlp'), 0, 0, tiled=True)  33.5 us
    all_to_all x1, blocking collectives, per_device(): sp = lax.all_to_all(sp, ('tz', 'mlp'), 0, 0, tiled=True)  21.3 us
    dot_general x1, matrix products, per_device(): jnp.einsum('rns,rsc->rnc', probs_old, x_pair, preferred_element_type=jnp....  12 us
    all_to_all x1, starting transfers between devices, per_device(): head_x = lax.all_to_all(x_part, ('tz', 'txc', 'mlp'), 0, 0, tiled=True)  10 us
    all_to_all x1, waiting for transfers between devices, per_device(): lax.all_to_all(b_cache, 'tz', split_axis=1, concat_axis=1, tiled=True)  9.09 us
    unnamed x32, local copies, waits for them, and re-layouts  6.55 us
    another operation x6, other arithmetic  6.41 us
    dot_general x1, matrix products, per_device(): jnp.einsum('rhnj,rjhd->rnhd', probs_new, scaled, preferred_element_type=j...  5.57 us
  transfers between devices with their start and end apart: 4, of which 1 were waited for; matrix products, arithmetic and copies ran while one was open for 25% of the time, Pallas kernels for 0%

profile of v2, /device:TPU:1, one launch (start us, length us, event | category | flops | bytes accessed | tf_op | source)
XLA Modules:
  0.0 164.0 jit_solution(17189552474198450353)
XLA Ops:
  6.6 1.1 copy.64
  7.6 21.3 %all_to_all.20 = bf16[32,4,2,256]{3,2,1,0:T(2,128)(2,1)} all-to-all(bf16[32,4,2,256]{3,2,1,0:T(2,128)(2,1)S(1)} %bitcast.82), channel_id=1, replica_groups=mesh['tz'=8,'txc'=8,'mlp'=4] {'tz','mlp'}, dimensions={0} | all-to-all | bytes 262144 | tf_op jit(solution)/shard_map/all_to_all | solution.py:45
  28.9 1.8 %copy.67 = bf16[4,8,48,128]{3,2,0,1:T(8,128)(2,1)} copy(bf16[4,8,48,128]{3,2,1,0:T(8,128)(2,1)} %param.20) | data formatting | bytes 786432 | tf_op args[6]
  30.7 3.5 %all-to-all-start.1 = ((bf16[4,8,48,128]{3,2,0,1:T(8,128)(2,1)}), bf16[4,8,48,128]{3,2,0,1:T(8,128)(2,1)S(1)}, u32[]{:S(2)}, u32[]{:S(2)}) async-start(bf16[4,8,48,128]{3,2,0,1:T(8,128)(2,1)} %copy.67), calls=%async_computation.1 | async-start | bytes 786432 | tf_op jit(solution)/shard_map/all_to_all | solution.py:39
  34.2 1.4 reshape.178
  35.6 0.4 copy.72
  36.1 1.3 copy.73
  37.4 9.1 %all-to-all-done.1 = bf16[4,8,48,128]{3,2,0,1:T(8,128)(2,1)S(1)} async-done(((bf16[4,8,48,128]{3,2,0,1:T(8,128)(2,1)}), bf16[4,8,48,128]{3,2,0,1:T(8,128)(2,1)S(1)}, u32[]{:S(2)}, u32[]{:S(2)}) %all-to-all-start.1) | async-done | bytes 393248 | tf_op jit(solution)/shard_map/all_to_all | solution.py:39
  46.5 10.0 %all-to-all-start.2 = ((bf16[256,4,2,128]{3,2,1,0:T(2,128)(2,1)}), bf16[256,4,2,128]{3,2,1,0:T(2,128)(2,1)}, u32[]{:S(2)}, u32[]{:S(2)}) async-start(bf16[256,4,2,128]{3,2,1,0:T(2,128)(2,1)} %copy.73), calls=%async_computation.2 | async-start | bytes 1048576 | tf_op jit(solution)/shard_map/all_to_all | solution.py:54
  56.5 0.2 all-gather.7.cloned.1.call-start
  56.7 0.5 all-gather.7.cloned.1.call-update
  57.3 0.1 iota_compare_fusion
  57.4 0.1 broadcast_select_fusion
  57.4 0.1 reshape.173
  57.5 2.3 %reduce-window.14 = f32[4,2,24,128]{3,2,1,0:T(8,128)S(1)} reduce-window(f32[4,2,24,128]{3,2,1,0:T(8,128)S(1)} %reshape.173, f32[]{:T(128)} %constant.13.clone.1), window={size=1x1x1x128 pad=0_0x0_0x0_0x127_0}, to_apply=%region_0.0 | reduce-window | flops 3121152 | bytes 196612 | tf_op jit(solution)/shard_map/reduce-window
  59.8 0.2 slice_reduce_fusion
  60.0 0.8 reduce-window.15
  60.8 0.1 broadcast_add_fusion
  61.0 0.1 slice.43
  61.1 0.1 copy.84
  61.2 0.1 copy.71
  61.3 0.1 negate_bitcast_fusion
  61.4 2.4 %reduce-window.16 = f32[4,2,4,128]{3,2,1,0:T(4,128)S(1)} reduce-window(f32[4,2,4,128]{3,2,1,0:T(4,128)S(1)} %reshape.176, f32[]{:T(128)} %constant.13.clone.1), window={size=1x1x1x128 pad=0_0x0_0x0_0x127_0}, to_apply=%region_2.3 | reduce-window | flops 520192 | bytes 32772 | tf_op jit(solution)/shard_map/reduce-window.2
  63.8 0.2 slice_reduce_fusion.1
  64.0 0.7 reduce-window.19
  64.7 1.1 iota_subtract_fusion
  65.8 0.5 and_bitcast_fusion
  66.3 0.6 shift-left_or_fusion
  66.9 0.1 broadcast_add_fusion.1
  67.0 0.1 exponential_bitcast_fusion
  67.1 0.1 broadcast_compare_fusion
  67.2 1.4 copy.75
  68.6 3.2 %copy.69 = bf16[4,3072,128]{1,2,0:T(8,128)(2,1)S(1)} copy(bf16[4,3072,128]{2,1,0:T(8,128)(2,1)} %param.19) | data formatting | bytes 6291456 | tf_op args[5]
  71.8 0.8 reshape.201
  72.6 1.4 gather_fusion.1
  74.1 3.9 %fusion.6 = (bf16[4,3072,128]{1,2,0:T(8,128)(2,1)}, bf16[4,3072,128]{1,2,0:T(8,128)(2,1)}) fusion(bf16[4,3072,128]{1,2,0:T(8,128)(2,1)S(1)} %copy.69, f32[4,3072,2]{1,2,0:T(2,128)S(1)} %exponential_bitcast_fusion), kind=kLoop, calls=%fused_computation.13 | loop fusion | flops 9437184 | bytes 9535488 | tf_op jit(solution)/shard_map/convert_element_type | solution.py:74
  77.9 0.1 broadcast_compare_fusion.1
  78.1 1.8 %compare_and_fusion = pred[4,512,512]{2,1,0:T(8,128)(4,1)} fusion(s32[512,512]{1,0:T(8,128)S(1)} %copy-done, s32[4]{0:T(128)S(1)} %copy-done.11, pred[512,512]{1,0:T(8,128)(4,1)S(1)} %broadcast_compare_fusion), kind=kLoop, calls=%fused_computation.16 | loop fusion | flops 2097152 | bytes 2359312 | tf_op jit(solution)/shard_map/and | solution.py:99
  79.9 1.4 convert_bitcast_fusion
  81.3 0.4 copy.74
  81.7 1.9 %reshape.184 = f32[4,512,2,64]{3,2,1,0:T(2,128)S(1)} reshape(f32[4,256,2,128]{3,2,1,0:T(2,128)S(1)} %copy.74) | data formatting | bytes 2097152 | tf_op jit(solution)/shard_map/convert_element_type | solution.py:59
  83.5 5.3 %multiply_convert_fusion.2 = bf16[4,512,2,64]{3,2,1,0:T(2,128)(2,1)} fusion(f32[4,512,2,64]{3,2,1,0:T(2,128)S(1)} %reshape.184, f32[4,512,2]{2,1,0:T(8,128)} %copy.75), kind=kLoop, calls=%fused_computation.18 | loop fusion | flops 524288 | bytes 1589248 | tf_op jit(solution)/shard_map/convert_element_type | solution.py:60
  88.8 1.8 %copy.65 = bf16[8,4,8,4,2,256]{5,3,4,1,2,0:T(4,128)(2,1)S(1)} copy(bf16[8,4,8,4,2,256]{5,4,3,2,1,0:T(2,128)(2,1)} %bitcast.80) | data formatting | bytes 2097152 | tf_op jit(solution)/shard_map/reshape | solution.py:47
  90.7 0.4 fusion.50
  91.0 2.7 %fusion.20 = f32[4,512,512]{2,1,0:T(8,128)} fusion(bf16[4,512,128]{2,0,1:T(4,128)(2,1)S(1)} %get-tuple-element.11, bf16[4,512,128]{2,0,1:T(4,128)(2,1)S(1)} %get-tuple-element.10), kind=kOutput, calls=%fused_computation.36 | convolution fusion | flops 268435456 | bytes 5242880 | tf_op jit(solution)/shard_map/rnk,rjk->rnj/dot_general | solution.py:97
  93.7 3.9 %copy.68 = bf16[4,8,384,128]{3,2,1,0:T(8,128)(2,1)} copy(bf16[4,8,384,128]{3,2,0,1:T(8,128)(2,1)} %all-gather.7.cloned.1.call-done) | data formatting | bytes 6291456 | tf_op jit(solution)/shard_map/all_gather | solution.py:40
  97.6 1.3 gather_fusion
  98.9 12.0 %fusion.1 = f32[4,512,256]{1,2,0:T(8,128)S(1)} fusion(s32[4]{0:T(128)S(1)} %copy-done.12, s32[4,512]{1,0:T(4,128)S(1)} %iota_add_fusion, pred[4,3072]{1,0:T(4,128)(4,1)S(1)} %iota_compare_fusion, bf16[4,3072,128]{1,2,0:T(8,128)(2,1)} %get-tuple-element.9, bf16[4,3072,128]{1,2,0:T(8,128)(2,1)} %get-tuple-element.8, bf16[4,3072,128]{2,1,0:T(8,128)(2,1)} %bitcast.74, ...), kind=kOutput, calls=%fused_computation.5 | convolution fusion | flops 4875878400 | bytes 12079120 | tf_op jit(solution)/shard_map/rns,rsc->rnc/dot_general | solution.py:84
  111.0 0.2 slice_add_fusion
  111.2 5.6 %fusion.12 = f32[4,512,2,64]{1,3,2,0:T(8,128)S(1)} fusion(f32[4,2,512]{2,1,0:T(2,128)S(1)} %reduce_window_sum.41, f32[4,512,512]{2,1,0:T(8,128)} %fusion.20, pred[4,512,512]{2,1,0:T(8,128)(4,1)} %compare_and_fusion, bf16[4,512,2,64]{3,2,1,0:T(2,128)(2,1)} %multiply_convert_fusion.2, f32[4,512,2,64]{1,3,2,0:T(8,128)S(1)} %bitcast.79, ...), kind=kOutput, calls=%fused_computation.21 | convolution fusion | flops 279445504 | bytes 7897088 | tf_op jit(solution)/shard_map/rhnj,rjhd->rnhd/dot_general | solution.py:104
  116.8 0.3 copy.78
  117.1 0.6 fusion.13
  117.7 0.4 copy.99
  118.1 33.5 %all_to_all.21 = bf16[256,4,2,128]{3,2,1,0:T(2,128)(2,1)S(1)} all-to-all(bf16[256,4,2,128]{3,2,1,0:T(2,128)(2,1)S(1)} %bitcast.76), channel_id=1, replica_groups=mesh['tz'=8,'txc'=8,'mlp'=4] {'tz','txc','mlp'}, dimensions={0} | all-to-all | bytes 1048576 | tf_op jit(solution)/shard_map/all_to_all | solution.py:110
  151.6 0.2 copy.80
  151.8 0.1 reshape.183
  152.0 1.5 fusion.48
  153.5 0.9 mul.89
  154.4 0.2 reduce_sum.9
  154.5 0.1 copy.81
  154.6 0.1 copy.82
  154.7 0.1 mul.90
  154.8 0.9 mul.91
  155.7 1.4 multiply_convert_fusion.7
  (40 shorter events, 0.3 us)
Async XLA Ops:
  6.5 50.7 %copy-start.9 = (s32[4]{0:T(128)S(1)}, s32[4]{0:T(128)}, u32[]{:S(2)}) copy-start(s32[4]{0:T(128)} %param.22) | copy-start | bytes 52
  6.5 50.8 %copy-start.3 = (f32[4,2,3072]{2,1,0:T(2,128)S(1)}, f32[4,2,3072]{2,1,0:T(2,128)}, u32[]{:S(2)}) copy-start(f32[4,2,3072]{2,1,0:T(2,128)} %param.21) | copy-start | bytes 294916
  6.5 54.7 %copy-start.13 = (f32[2]{0:T(128)S(1)}, f32[2]{0:T(128)}, u32[]{:S(2)}) copy-start(f32[2]{0:T(128)} %param.18) | copy-start | bytes 28
  6.5 54.7 %copy-start.4 = (f32[4,512,2]{1,2,0:T(2,128)S(1)}, f32[4,512,2]{1,2,0:T(2,128)}, u32[]{:S(2)}) copy-start(f32[4,512,2]{1,2,0:T(2,128)} %param.17) | copy-start | bytes 49156
  6.5 82.3 %all-gather.5.cloned.1.call-start = ((), (), s32[]{:S(2)}) async-start(), calls=%async_computation.4 | async-start | bytes 1179648 | tf_op jit(solution)/shard_map/all_gather | solution.py:46
  28.9 36.9 %copy-start.6 = (s32[4,4]{1,0:T(4,128)S(1)}, s32[4,4]{1,0:T(4,128)}, u32[]{:S(2)}) copy-start(s32[4,4]{1,0:T(4,128)} %param.23) | copy-start | bytes 196
  30.7 15.7 %all-to-all-start.1 = ((bf16[4,8,48,128]{3,2,0,1:T(8,128)(2,1)}), bf16[4,8,48,128]{3,2,0,1:T(8,128)(2,1)S(1)}, u32[]{:S(2)}, u32[]{:S(2)}) async-start(bf16[4,8,48,128]{3,2,0,1:T(8,128)(2,1)} %copy.67), calls=%async_computation.1 | async-start | bytes 786432 | tf_op jit(solution)/shard_map/all_to_all | solution.py:39
  46.5 10.2 %copy-start.1 = (bf16[4,8,48,128]{3,2,0,1:T(8,128)(2,1)}, bf16[4,8,48,128]{3,2,0,1:T(8,128)(2,1)S(1)}, u32[]{:S(2)}) copy-start(bf16[4,8,48,128]{3,2,0,1:T(8,128)(2,1)S(1)} %all-to-all-done.1) | copy-start | bytes 1179652
  46.5 33.4 %all-to-all-start.2 = ((bf16[256,4,2,128]{3,2,1,0:T(2,128)(2,1)}), bf16[256,4,2,128]{3,2,1,0:T(2,128)(2,1)}, u32[]{:S(2)}, u32[]{:S(2)}) async-start(bf16[256,4,2,128]{3,2,1,0:T(2,128)(2,1)} %copy.73), calls=%async_computation.2 | async-start | bytes 1048576 | tf_op jit(solution)/shard_map/all_to_all | solution.py:54
  56.5 37.2 %all-gather.7.cloned.1.call-start = ((), (), s32[]{:S(2)}) async-start(), calls=%async_computation.5 | async-start | bytes 3538944 | tf_op jit(solution)/shard_map/all_gather | solution.py:40
  74.0 3.9 %copy-start.7 = (s32[4,4]{1,0:T(4,128)S(1)}, s32[4,4]{1,0:T(4,128)}, u32[]{:S(2)}) copy-start(s32[4,4]{1,0:T(4,128)} %param.23) | copy-start | bytes 196
  74.0 3.9 %copy-start.10 = (s32[4]{0:T(128)S(1)}, s32[4]{0:T(128)}, u32[]{:S(2)}) copy-start(s32[4]{0:T(128)} %param.22) | copy-start | bytes 52
  74.0 4.1 %copy-start = (s32[512,512]{1,0:T(8,128)S(1)}, s32[512,512]{1,0:T(8,128)}, u32[]{:S(2)}) copy-start(s32[512,512]{1,0:T(8,128)} %iota_subtract_fusion) | copy-start | bytes 3145732
  74.0 4.1 %copy-start.11 = (s32[4]{0:T(128)S(1)}, s32[4]{0:T(128)}, u32[]{:S(2)}) copy-start(s32[4]{0:T(128)} %param.24) | copy-start | bytes 52
  93.7 5.2 %copy-start.12 = (s32[4]{0:T(128)S(1)}, s32[4]{0:T(128)}, u32[]{:S(2)}) copy-start(s32[4]{0:T(128)} %param.24) | copy-start | bytes 52
  111.2 5.9 %copy-start.8 = (pred[4,4]{1,0:T(4,128)(4,1)S(1)}, pred[4,4]{1,0:T(4,128)(4,1)}, u32[]{:S(2)}) copy-start(pred[4,4]{1,0:T(4,128)(4,1)} %and_bitcast_fusion) | copy-start | bytes 52
  116.8 35.2 %copy-start.2 = (bf16[16,2,8192]{2,1,0:T(2,128)(2,1)S(1)}, bf16[16,2,8192]{2,1,0:T(2,128)(2,1)}, u32[]{:S(2)}) copy-start(bf16[16,2,8192]{2,1,0:T(2,128)(2,1)} %param.15) | copy-start | bytes 1572868
  152.0 3.8 %copy-start.5 = (f32[8192]{0:T(1024)S(1)}, f32[8192]{0:T(1024)}, u32[]{:S(2)}) copy-start(f32[8192]{0:T(1024)} %param.25) | copy-start | bytes 98308
Sparse Core Ops, SparseCore 0:
  29.1 22.5 all-gather.4
  59.1 32.5 all-gather.6

commit v3 on v2

--- a/solution.py
+++ b/solution.py
@@ -37,15 +37,16 @@
     head_dim = chans // heads_dev
 
     part_b = lax.all_to_all(b_cache, "tz", split_axis=1, concat_axis=1, tiled=True)
-    shared_b = lax.all_gather(part_b, "txc", axis=2)
-    shared_b = shared_b.reshape(requests, cache_len, state_dim)
-
     sp = state_proj.reshape(n_mlp, requests, tok_blk, groups, 2 * state_dim)
     sp = sp.transpose(3, 0, 1, 2, 4).reshape(groups * n_mlp, requests, tok_blk, -1)
     sp = lax.all_to_all(sp, ("tz", "mlp"), 0, 0, tiled=True)
-    sp = lax.all_gather(sp, "txc", axis=1)
-    sp = sp.reshape(n_tz, n_mlp, n_txc, requests, tok_blk, -1).transpose(3, 0, 2, 1, 4, 5)
-    sp = sp.reshape(requests, new_len, -1)
+    packed = jnp.concatenate([part_b.reshape(-1), sp.reshape(-1)])
+    packed = lax.all_gather(packed, "txc")
+    b_size = part_b.size
+    shared_b = packed[:, :b_size].reshape(n_txc, requests, n_tz, -1, state_dim)
+    shared_b = shared_b.transpose(1, 2, 0, 3, 4).reshape(requests, cache_len, state_dim)
+    sp = packed[:, b_size:].reshape(n_txc, n_tz, n_mlp, requests, tok_blk, -1)
+    sp = sp.transpose(3, 1, 0, 2, 4, 5).reshape(requests, new_len, -1)
     b_new = sp[..., :state_dim]
     c_now = sp[..., state_dim:]
 

time: 165 us -> 168 us (1.018)
  blocking collectives: 54.8 us -> 33.4 us
  starting transfers between devices: 13.7 us -> 25.5 us
  waiting for transfers between devices: 9.62 us -> 19.7 us
  local copies, waits for them, and re-layouts: 26.4 us -> 32 us
  matrix products: 20.9 us -> 17.1 us
    all_to_all x1 -> x0, blocking collectives: 21.3 us -> none  [per_device(): sp = lax.all_to_all(sp, ('tz', 'mlp'), 0, 0, tiled=True)]
    all_to_all x0 -> x1, starting transfers between devices: none -> 12 us  [per_device(): sp = lax.all_to_all(sp, ('tz', 'mlp'), 0, 0, tiled=True)]
    all_to_all x0 -> x1, waiting for transfers between devices: none -> 7.51 us  [per_device(): sp = lax.all_to_all(sp, ('tz', 'mlp'), 0, 0, tiled=True)]
    all_to_all x1, waiting for transfers between devices: 9.09 us -> 12.1 us  [per_device(): lax.all_to_all(b_cache, 'tz', split_axis=1, concat_axis=1, tiled=True)]
    unnamed x32 -> x38, local copies, waits for them, and re-layouts: 6.55 us -> 9.3 us
    transpose x0 -> x1, local copies, waits for them, and re-layouts: none -> 2.37 us  [per_device(): shared_b.transpose(1, 2, 0, 3, 4).reshape(requests, cache_len, state_dim)]
    all_gather x1, local copies, waits for them, and re-layouts: 3.87 us -> 5.92 us  [per_device(): packed = lax.all_gather(packed, 'txc')]
    dot_general x1, matrix products: 2.66 us -> 0.71 us  [per_device(): jnp.einsum('rnk,rjk->rnj', c_now, b_new, preferred_element_type=jnp.float32)]
  transfers between devices with their start and end apart: 4 -> 4, of which waited for: 1 -> 2; matrix products, arithmetic and copies ran while one was open for 25% -> 21% of each run, Pallas kernels for 0% -> 0%
where the time goes in v3:
time: 168 us; the launch traced here: 167 us
  blocking collectives  33.4 us (20%)
  local copies, waits for them, and re-layouts  32 us (19%)
  other arithmetic  25.7 us (15%)
  starting transfers between devices  25.5 us (15%)
  waiting for transfers between devices  19.7 us (12%)
  matrix products  17.1 us (10%)
  between operations  13.8 us (8%)
    all_to_all x1, blocking collectives, per_device(): back = lax.all_to_all(back, ('tz', 'txc', 'mlp'), 0, 0, tiled=True)  33.4 us
    all_to_all x1, waiting for transfers between devices, per_device(): lax.all_to_all(b_cache, 'tz', split_axis=1, concat_axis=1, tiled=True)  12.1 us
    dot_general x1, matrix products, per_device(): jnp.einsum('rns,rsc->rnc', probs_old, x_pair, preferred_element_type=jnp....  12 us
    all_to_all x1, starting transfers between devices, per_device(): sp = lax.all_to_all(sp, ('tz', 'mlp'), 0, 0, tiled=True)  12 us
    all_to_all x1, starting transfers between devices, per_device(): head_x = lax.all_to_all(x_part, ('tz', 'txc', 'mlp'), 0, 0, tiled=True)  10 us
    unnamed x38, local copies, waits for them, and re-layouts  9.3 us
    all_to_all x1, waiting for transfers between devices, per_device(): sp = lax.all_to_all(sp, ('tz', 'mlp'), 0, 0, tiled=True)  7.51 us
    another operation x6, other arithmetic  6.41 us
  transfers between devices with their start and end apart: 4, of which 2 were waited for; matrix products, arithmetic and copies ran while one was open for 21% of the time, Pallas kernels for 0%

profile of v3, /device:TPU:1, one launch (start us, length us, event | category | flops | bytes accessed | tf_op | source)
XLA Modules:
  0.0 167.2 jit_solution(18344963510962033115)
XLA Ops:
  6.5 1.7 %copy.86 = bf16[4,4,2,8,256]{4,2,1,0,3:T(2,128)(2,1)} copy(bf16[4,4,2,8,256]{4,3,2,1,0:T(8,128)(2,1)} %bitcast.88) | data formatting | bytes 262144 | tf_op jit(solution)/shard_map/reshape | solution.py:40
  8.2 12.0 %all-to-all-start.1 = ((bf16[32,4,2,256]{3,2,1,0:T(2,128)(2,1)}), bf16[32,4,2,256]{3,2,1,0:T(2,128)(2,1)S(1)}, u32[]{:S(2)}, u32[]{:S(2)}) async-start(bf16[32,4,2,256]{3,2,1,0:T(2,128)(2,1)} %bitcast.3), calls=%async_computation.1 | async-start | bytes 262144 | tf_op jit(solution)/shard_map/all_to_all | solution.py:42
  20.3 1.8 %copy.84 = bf16[4,8,48,128]{3,2,0,1:T(8,128)(2,1)} copy(bf16[4,8,48,128]{3,2,1,0:T(8,128)(2,1)} %param.20) | data formatting | bytes 786432 | tf_op args[6]
  22.1 7.5 %all-to-all-done.1 = bf16[32,4,2,256]{3,2,1,0:T(2,128)(2,1)S(1)} async-done(((bf16[32,4,2,256]{3,2,1,0:T(2,128)(2,1)}), bf16[32,4,2,256]{3,2,1,0:T(2,128)(2,1)S(1)}, u32[]{:S(2)}, u32[]{:S(2)}) %all-to-all-start.1) | async-done | bytes 131104 | tf_op jit(solution)/shard_map/all_to_all | solution.py:42
  29.6 3.5 %all-to-all-start = ((bf16[4,8,48,128]{3,2,0,1:T(8,128)(2,1)}), bf16[4,8,48,128]{3,2,0,1:T(8,128)(2,1)S(1)}, u32[]{:S(2)}, u32[]{:S(2)}) async-start(bf16[4,8,48,128]{3,2,0,1:T(8,128)(2,1)} %copy.84), calls=%async_computation | async-start | bytes 786432 | tf_op jit(solution)/shard_map/all_to_all | solution.py:39
  33.1 0.1 copy.107
  33.2 12.1 %all-to-all-done = bf16[4,8,48,128]{3,2,0,1:T(8,128)(2,1)S(1)} async-done(((bf16[4,8,48,128]{3,2,0,1:T(8,128)(2,1)}), bf16[4,8,48,128]{3,2,0,1:T(8,128)(2,1)S(1)}, u32[]{:S(2)}, u32[]{:S(2)}) %all-to-all-start) | async-done | bytes 393248 | tf_op jit(solution)/shard_map/all_to_all | solution.py:39
  45.4 0.8 pad_maximum_fusion
  46.3 0.4 reshape.190
  46.7 0.4 copy.93
  47.1 1.3 copy.94
  48.4 10.0 %all-to-all-start.2 = ((bf16[256,4,2,128]{3,2,1,0:T(2,128)(2,1)}), bf16[256,4,2,128]{3,2,1,0:T(2,128)(2,1)}, u32[]{:S(2)}, u32[]{:S(2)}) async-start(bf16[256,4,2,128]{3,2,1,0:T(2,128)(2,1)} %copy.94), calls=%async_computation.2 | async-start | bytes 1048576 | tf_op jit(solution)/shard_map/all_to_all | solution.py:55
  58.5 0.1 iota_compare_fusion
  58.6 0.1 reshape.185
  58.7 2.3 %reduce-window.14 = f32[4,2,24,128]{3,2,1,0:T(8,128)S(1)} reduce-window(f32[4,2,24,128]{3,2,1,0:T(8,128)S(1)} %reshape.185, f32[]{:T(128)} %constant.13.clone.1), window={size=1x1x1x128 pad=0_0x0_0x0_0x127_0}, to_apply=%region_0.0 | reduce-window | flops 3121152 | bytes 196612 | tf_op jit(solution)/shard_map/reduce-window
  61.0 0.2 slice_reduce_fusion
  61.2 0.8 reduce-window.15
  62.0 0.1 broadcast_add_fusion
  62.3 0.1 copy.105
  62.4 0.1 copy.92
  62.5 0.1 negate_bitcast_fusion
  62.6 2.4 %reduce-window.16 = f32[4,2,4,128]{3,2,1,0:T(4,128)S(1)} reduce-window(f32[4,2,4,128]{3,2,1,0:T(4,128)S(1)} %reshape.188, f32[]{:T(128)} %constant.13.clone.1), window={size=1x1x1x128 pad=0_0x0_0x0_0x127_0}, to_apply=%region_2.3 | reduce-window | flops 520192 | bytes 32772 | tf_op jit(solution)/shard_map/reduce-window.2
  65.0 0.2 slice_reduce_fusion.1
  65.2 0.7 reduce-window.19
  65.9 1.1 iota_subtract_fusion
  67.0 0.5 and_bitcast_fusion
  67.5 0.6 shift-left_or_fusion
  68.2 0.1 exponential_bitcast_fusion
  68.4 0.1 broadcast_compare_fusion
  68.5 1.3 copy.96
  69.8 3.2 %copy.90 = bf16[4,3072,128]{1,2,0:T(8,128)(2,1)S(1)} copy(bf16[4,3072,128]{2,1,0:T(8,128)(2,1)} %param.19) | data formatting | bytes 6291456 | tf_op args[5]
  73.0 0.8 reshape.210
  73.8 1.4 gather_fusion.1
  75.2 4.0 %fusion.6 = (bf16[4,3072,128]{1,2,0:T(8,128)(2,1)}, bf16[4,3072,128]{1,2,0:T(8,128)(2,1)}) fusion(bf16[4,3072,128]{1,2,0:T(8,128)(2,1)S(1)} %copy.90, f32[4,3072,2]{1,2,0:T(2,128)S(1)} %exponential_bitcast_fusion), kind=kLoop, calls=%fused_computation.13 | loop fusion | flops 9437184 | bytes 9535488 | tf_op jit(solution)/shard_map/convert_element_type | solution.py:75
  79.4 1.8 %compare_and_fusion = pred[4,512,512]{2,1,0:T(8,128)(4,1)} fusion(s32[512,512]{1,0:T(8,128)S(1)} %copy-done, s32[4]{0:T(128)S(1)} %copy-done.13, pred[512,512]{1,0:T(8,128)(4,1)S(1)} %broadcast_compare_fusion), kind=kLoop, calls=%fused_computation.16 | loop fusion | flops 2097152 | bytes 2359312 | tf_op jit(solution)/shard_map/and | solution.py:100
  81.2 1.4 convert_bitcast_fusion
  82.6 0.4 copy.95
  82.9 1.9 %reshape.196 = f32[4,512,2,64]{3,2,1,0:T(2,128)S(1)} reshape(f32[4,256,2,128]{3,2,1,0:T(2,128)S(1)} %copy.95) | data formatting | bytes 2097152 | tf_op jit(solution)/shard_map/convert_element_type | solution.py:60
  84.8 5.3 %multiply_convert_fusion.2 = bf16[4,512,2,64]{3,2,1,0:T(2,128)(2,1)} fusion(f32[4,512,2,64]{3,2,1,0:T(2,128)S(1)} %reshape.196, f32[4,512,2]{2,1,0:T(8,128)} %copy.96), kind=kLoop, calls=%fused_computation.19 | loop fusion | flops 524288 | bytes 1589248 | tf_op jit(solution)/shard_map/convert_element_type | solution.py:61
  90.1 5.9 %reshape.209 = bf16[8,262144]{1,0:T(8,128)(2,1)} reshape(bf16[2097152]{0:T(1024)(128)(2,1)} %all-gather.3.cloned.1.call-done) | data formatting | bytes 8388608 | tf_op jit(solution)/shard_map/all_gather | solution.py:44
  96.0 2.1 %slice_bitcast_fusion = bf16[1,8,1536,128]{3,1,2,0:T(8,128)(2,1)S(1)} fusion(bf16[8,262144]{1,0:T(8,128)(2,1)} %reshape.209), kind=kLoop, calls=%fused_computation.17 | loop fusion | bytes 6291456
  98.2 0.5 copy.87
  98.7 0.4 fusion.49
  99.1 2.4 %copy.89 = bf16[4,8,8,48,128]{4,3,2,1,0:T(8,128)(2,1)} copy(bf16[4,8,8,48,128]{4,2,3,1,0:T(8,128)(2,1)S(1)} %bitcast.75) | data formatting | bytes 6291456 | tf_op jit(solution)/shard_map/transpose | solution.py:47
  101.5 1.3 gather_fusion
  102.8 12.0 %fusion.1 = f32[4,512,256]{1,2,0:T(8,128)S(1)} fusion(s32[4]{0:T(128)S(1)} %copy-done.14, s32[4,512]{1,0:T(4,128)S(1)} %iota_add_fusion, pred[4,3072]{1,0:T(4,128)(4,1)S(1)} %iota_compare_fusion, bf16[4,3072,128]{1,2,0:T(8,128)(2,1)} %get-tuple-element.9, bf16[4,3072,128]{1,2,0:T(8,128)(2,1)} %get-tuple-element.8, bf16[4,3072,128]{2,1,0:T(8,128)(2,1)} %bitcast.78, ...), kind=kOutput, calls=%fused_computation.5 | convolution fusion | flops 4875878400 | bytes 12079120 | tf_op jit(solution)/shard_map/rns,rsc->rnc/dot_general | solution.py:85
  114.8 0.2 slice_add_fusion
  115.1 0.7 fusion.19
  115.8 0.3 copy-done.1
  116.1 0.3 copy-done.2
  116.4 3.8 %fusion.12 = f32[4,512,2,64]{1,3,2,0:T(8,128)S(1)} fusion(f32[4,2,512]{2,1,0:T(2,128)S(1)} %reduce_window_sum.41, f32[4,512,512]{2,1,0:T(8,128)S(1)} %fusion.19, pred[4,512,512]{2,1,0:T(8,128)(4,1)S(1)} %copy-done.1, bf16[4,512,2,64]{3,2,1,0:T(2,128)(2,1)S(1)} %copy-done.2, f32[4,512,2,64]{1,3,2,0:T(8,128)S(1)} %bitcast.84, ...), kind=kOutput, calls=%fused_computation.22 | convolution fusion | flops 279445504 | bytes 7897088 | tf_op jit(solution)/shard_map/rhnj,rjhd->rnhd/dot_general | solution.py:105
  120.2 0.3 copy.99
  120.5 0.6 fusion.13
  121.1 0.4 copy.123
  121.5 33.4 %all_to_all.20 = bf16[256,4,2,128]{3,2,1,0:T(2,128)(2,1)S(1)} all-to-all(bf16[256,4,2,128]{3,2,1,0:T(2,128)(2,1)S(1)} %bitcast.80), channel_id=1, replica_groups=mesh['tz'=8,'txc'=8,'mlp'=4] {'tz','txc','mlp'}, dimensions={0} | all-to-all | bytes 1048576 | tf_op jit(solution)/shard_map/all_to_all | solution.py:111
  154.9 0.2 copy.101
  155.1 0.1 reshape.195
  155.2 1.5 fusion.47
  156.7 0.9 mul.89
  157.6 0.2 reduce_sum.9
  157.9 0.1 copy.103
  157.9 0.1 mul.90
  158.1 0.9 mul.91
  159.0 1.4 multiply_convert_fusion.7
  (49 shorter events, 0.8 us)
Async XLA Ops:
  6.5 39.7 %copy-start.3 = (bf16[16,2,8192]{2,1,0:T(2,128)(2,1)S(1)}, bf16[16,2,8192]{2,1,0:T(2,128)(2,1)}, u32[]{:S(2)}) copy-start(bf16[16,2,8192]{2,1,0:T(2,128)(2,1)} %param.14) | copy-start | bytes 1572868
  8.2 21.4 %all-to-all-start.1 = ((bf16[32,4,2,256]{3,2,1,0:T(2,128)(2,1)}), bf16[32,4,2,256]{3,2,1,0:T(2,128)(2,1)S(1)}, u32[]{:S(2)}, u32[]{:S(2)}) async-start(bf16[32,4,2,256]{3,2,1,0:T(2,128)(2,1)} %bitcast.3), calls=%async_computation.1 | async-start | bytes 262144 | tf_op jit(solution)/shard_map/all_to_all | solution.py:42
  20.3 38.2 %copy-start.11 = (s32[4]{0:T(128)S(1)}, s32[4]{0:T(128)}, u32[]{:S(2)}) copy-start(s32[4]{0:T(128)} %param.22) | copy-start | bytes 52
  20.3 38.3 %copy-start.5 = (f32[4,2,3072]{2,1,0:T(2,128)S(1)}, f32[4,2,3072]{2,1,0:T(2,128)}, u32[]{:S(2)}) copy-start(f32[4,2,3072]{2,1,0:T(2,128)} %param.21) | copy-start | bytes 294916
  22.1 40.3 %copy-start.15 = (f32[2]{0:T(128)S(1)}, f32[2]{0:T(128)}, u32[]{:S(2)}) copy-start(f32[2]{0:T(128)} %param.18) | copy-start | bytes 28
  22.1 40.4 %copy-start.6 = (f32[4,512,2]{1,2,0:T(2,128)S(1)}, f32[4,512,2]{1,2,0:T(2,128)}, u32[]{:S(2)}) copy-start(f32[4,512,2]{1,2,0:T(2,128)} %param.17) | copy-start | bytes 49156
  29.6 15.7 %all-to-all-start = ((bf16[4,8,48,128]{3,2,0,1:T(8,128)(2,1)}), bf16[4,8,48,128]{3,2,0,1:T(8,128)(2,1)S(1)}, u32[]{:S(2)}, u32[]{:S(2)}) async-start(bf16[4,8,48,128]{3,2,0,1:T(8,128)(2,1)} %copy.84), calls=%async_computation | async-start | bytes 786432 | tf_op jit(solution)/shard_map/all_to_all | solution.py:39
  33.1 57.0 %all-gather.3.cloned.1.call-start = ((), (), s32[]{:S(2)}) async-start(), calls=%async_computation.4 | async-start | bytes 4718592 | tf_op jit(solution)/shard_map/all_gather | solution.py:44
  45.4 21.6 %copy-start.8 = (s32[4,4]{1,0:T(4,128)S(1)}, s32[4,4]{1,0:T(4,128)}, u32[]{:S(2)}) copy-start(s32[4,4]{1,0:T(4,128)} %param.23) | copy-start | bytes 196
  48.4 32.7 %all-to-all-start.2 = ((bf16[256,4,2,128]{3,2,1,0:T(2,128)(2,1)}), bf16[256,4,2,128]{3,2,1,0:T(2,128)(2,1)}, u32[]{:S(2)}, u32[]{:S(2)}) async-start(bf16[256,4,2,128]{3,2,1,0:T(2,128)(2,1)} %copy.94), calls=%async_computation.2 | async-start | bytes 1048576 | tf_op jit(solution)/shard_map/all_to_all | solution.py:55
  75.2 4.0 %copy-start.9 = (s32[4,4]{1,0:T(4,128)S(1)}, s32[4,4]{1,0:T(4,128)}, u32[]{:S(2)}) copy-start(s32[4,4]{1,0:T(4,128)} %param.23) | copy-start | bytes 196
  75.2 4.0 %copy-start.12 = (s32[4]{0:T(128)S(1)}, s32[4]{0:T(128)}, u32[]{:S(2)}) copy-start(s32[4]{0:T(128)} %param.22) | copy-start | bytes 52
  75.2 4.2 %copy-start = (s32[512,512]{1,0:T(8,128)S(1)}, s32[512,512]{1,0:T(8,128)}, u32[]{:S(2)}) copy-start(s32[512,512]{1,0:T(8,128)} %iota_subtract_fusion) | copy-start | bytes 3145732
  75.2 4.2 %copy-start.13 = (s32[4]{0:T(128)S(1)}, s32[4]{0:T(128)}, u32[]{:S(2)}) copy-start(s32[4]{0:T(128)} %param.24) | copy-start | bytes 52
  96.0 2.2 %slice-start = ((bf16[8,262144]{1,0:T(8,128)(2,1)}), bf16[8,65536]{1,0:T(8,128)(2,1)S(1)}, s32[]{:S(2)}) async-start(bf16[8,262144]{1,0:T(8,128)(2,1)} %reshape.209), calls=%async_computation.5 | async-start | bytes 2097152 | tf_op jit(solution)/shard_map/slice | solution.py:48
  98.7 4.1 %copy-start.14 = (s32[4]{0:T(128)S(1)}, s32[4]{0:T(128)}, u32[]{:S(2)}) copy-start(s32[4]{0:T(128)} %param.24) | copy-start | bytes 52
  114.8 1.2 copy-start.1
  114.8 1.5 copy-start.2
  116.4 4.1 %copy-start.10 = (pred[4,4]{1,0:T(4,128)(4,1)S(1)}, pred[4,4]{1,0:T(4,128)(4,1)}, u32[]{:S(2)}) copy-start(pred[4,4]{1,0:T(4,128)(4,1)} %and_bitcast_fusion) | copy-start | bytes 52
  120.2 35.0 %copy-start.4 = (bf16[16,2,8192]{2,1,0:T(2,128)(2,1)S(1)}, bf16[16,2,8192]{2,1,0:T(2,128)(2,1)}, u32[]{:S(2)}) copy-start(bf16[16,2,8192]{2,1,0:T(2,128)(2,1)} %param.15) | copy-start | bytes 1572868
  155.2 3.8 %copy-start.7 = (f32[8192]{0:T(1024)S(1)}, f32[8192]{0:T(1024)}, u32[]{:S(2)}) copy-start(f32[8192]{0:T(1024)} %param.25) | copy-start | bytes 98308
Sparse Core Ops, SparseCore 0:
  46.4 37.6 all-gather.2

commit v4 on v2

--- a/solution.py
+++ b/solution.py
@@ -36,23 +36,21 @@
     chans = x_cache.shape[2]
     head_dim = chans // heads_dev
 
+    x_part = new_x.reshape(n_mlp, requests, tok_blk, n_tok, chans).transpose(3, 0, 1, 2, 4)
+    sp = state_proj.reshape(n_mlp, requests, tok_blk, groups, n_txc, -1)
+    sp = sp.transpose(3, 4, 0, 1, 2, 5).reshape(n_tok, n_mlp, requests, tok_blk, -1)
+    packed = jnp.concatenate([x_part, sp], axis=-1).reshape(n_dev, requests, tok_blk, -1)
+    got = lax.all_to_all(packed, ("tz", "txc", "mlp"), 0, 0, tiled=True)
+    got = got.transpose(1, 0, 2, 3).reshape(requests, new_len, -1)
+    sp = lax.all_gather(got[..., chans:], "txc", axis=2).reshape(requests, new_len, -1)
+    head_x = got[..., :chans]
+    b_new = sp[..., :state_dim]
+    c_now = sp[..., state_dim:]
+
+    got, b_cache = lax.optimization_barrier((got, b_cache))
     part_b = lax.all_to_all(b_cache, "tz", split_axis=1, concat_axis=1, tiled=True)
     shared_b = lax.all_gather(part_b, "txc", axis=2)
     shared_b = shared_b.reshape(requests, cache_len, state_dim)
-
-    sp = state_proj.reshape(n_mlp, requests, tok_blk, groups, 2 * state_dim)
-    sp = sp.transpose(3, 0, 1, 2, 4).reshape(groups * n_mlp, requests, tok_blk, -1)
-    sp = lax.all_to_all(sp, ("tz", "mlp"), 0, 0, tiled=True)
-    sp = lax.all_gather(sp, "txc", axis=1)
-    sp = sp.reshape(n_tz, n_mlp, n_txc, requests, tok_blk, -1).transpose(3, 0, 2, 1, 4, 5)
-    sp = sp.reshape(requests, new_len, -1)
-    b_new = sp[..., :state_dim]
-    c_now = sp[..., state_dim:]
-
-    x_part = new_x.reshape(n_mlp, requests, tok_blk, n_tok, chans).transpose(3, 0, 1, 2, 4)
-    x_part = x_part.reshape(n_dev, requests, tok_blk, chans)
-    head_x = lax.all_to_all(x_part, ("tz", "txc", "mlp"), 0, 0, tiled=True)
-    head_x = head_x.transpose(1, 0, 2, 3).reshape(requests, new_len, chans)
 
     head_decay_values = jnp.exp(decay_rate)
     cum_new = jnp.cumsum(-(step_size * head_decay_values), axis=1)

time: 165 us -> 182 us (1.10)
  blocking collectives: 54.8 us -> 94.9 us
  starting transfers between devices: 13.7 us -> 0.04 us
  other arithmetic: 24.8 us -> 16.4 us
    all_to_all x1 -> x2, blocking collectives: 21.3 us -> 63.8 us  [the longest x1 46.3 us: per_device(): got = lax.all_to_all(packed, ('tz', 'txc', 'mlp'), 0, 0, tiled=True)]
    all_to_all x2 -> x0, starting transfers between devices: 13.4 us -> none  [the longest x1 10 us: per_device(): head_x = lax.all_to_all(x_part, ('tz', 'txc', 'mlp'), 0, 0, tiled=True)]
    all_gather x1, waiting for transfers between devices: 0.01 us -> 10.6 us  [per_device(): shared_b = lax.all_gather(part_b, 'txc', axis=2)]
    all_to_all x2 -> x0, waiting for transfers between devices: 9.09 us -> none  [the longest x1 9.09 us: per_device(): lax.all_to_all(b_cache, 'tz', split_axis=1, concat_axis=1, tiled=True)]
    convert_element_type x2 -> x0, other arithmetic: 6.69 us -> none  [the longest x1 5.28 us: per_device(): scaled = (scaled * step_size[..., None]).astype(jnp.bfloat16)]
    slice x2 -> x5, local copies, waits for them, and re-layouts: 0.55 us -> 3.11 us  [the longest x1 1.56 us: per_device(): b_new = sp[..., :state_dim]]
    all_to_all x1, blocking collectives: 33.5 us -> 31.1 us  [per_device(): back = lax.all_to_all(back, ('tz', 'txc', 'mlp'), 0, 0, tiled=True)]
    convert_element_type x2 -> x0, local copies, waits for them, and re-layouts: 2.24 us -> none  [per_device(): head_x.astype(jnp.float32).reshape(requests, new_len, heads_dev, head_dim)]
  transfers between devices with their start and end apart: 4 -> 2, of which waited for: 1 -> 1; matrix products, arithmetic and copies ran while one was open for 25% -> 14% of each run, Pallas kernels for 0% -> 0%
where the time goes in v4:
time: 182 us; the launch traced here: 181 us
  blocking collectives  94.9 us (52%)
  local copies, waits for them, and re-layouts  24.9 us (14%)
  matrix products  20.6 us (11%)
  other arithmetic  16.4 us (9%)
  between operations  13.8 us (8%)
  waiting for transfers between devices  10.7 us (6%)
    all_to_all x1, blocking collectives, per_device(): got = lax.all_to_all(packed, ('tz', 'txc', 'mlp'), 0, 0, tiled=True)  46.3 us
    all_to_all x1, blocking collectives, per_device(): back = lax.all_to_all(back, ('tz', 'txc', 'mlp'), 0, 0, tiled=True)  31.1 us
    all_to_all x1, blocking collectives, per_device(): lax.all_to_all(b_cache, 'tz', split_axis=1, concat_axis=1, tiled=True)  17.5 us
    dot_general x1, matrix products, per_device(): jnp.einsum('rns,rsc->rnc', probs_old, x_pair, preferred_element_type=jnp....  11.7 us
    all_gather x1, waiting for transfers between devices, per_device(): shared_b = lax.all_gather(part_b, 'txc', axis=2)  10.6 us
    another operation x6, other arithmetic  6.42 us
    dot_general x1, matrix products, per_device(): jnp.einsum('rhnj,rjhd->rnhd', probs_new, scaled, preferred_element_type=j...  5.63 us
    unnamed x25, local copies, waits for them, and re-layouts  4.73 us
  transfers between devices with their start and end apart: 2, of which 1 were waited for; matrix products, arithmetic and copies ran while one was open for 14% of the time, Pallas kernels for 0%

profile of v4, /device:TPU:1, one launch (start us, length us, event | category | flops | bytes accessed | tf_op | source)
XLA Modules:
  0.0 181.3 jit_solution(13305697408714112141)
XLA Ops:
  6.5 1.4 reshape.168
  8.0 0.4 copy.71
  8.4 1.2 reshape.169
  9.6 0.7 copy.72
  10.3 0.2 pad_maximum_fusion
  10.5 1.1 copy.73
  11.6 46.3 %all_to_all.15 = bf16[256,4,2,160]{3,2,1,0:T(2,128)(2,1)S(1)} all-to-all(bf16[256,4,2,160]{3,2,1,0:T(2,128)(2,1)S(1)} %copy.73), channel_id=1, replica_groups=mesh['tz'=8,'txc'=8,'mlp'=4] {'tz','txc','mlp'}, dimensions={0} | all-to-all | bytes 1310720 | tf_op jit(solution)/shard_map/all_to_all | solution.py:43
  58.0 0.5 copy.74
  58.5 1.0 copy-done
  59.5 0.2 slice.48
  59.7 1.0 copy.75
  60.8 17.5 %all_to_all.16 = bf16[4,8,48,128]{3,2,0,1:T(8,128)(2,1)} all-to-all(bf16[4,8,48,128]{3,2,0,1:T(8,128)(2,1)S(1)} %copy.77), channel_id=1, replica_groups=mesh['tz'=8,'txc'=8,'mlp'=4] {'tz'}, dimensions={1} | all-to-all | bytes 786432 | tf_op jit(solution)/shard_map/all_to_all | solution.py:51
  78.3 0.1 iota_compare_fusion
  78.4 0.1 broadcast_select_fusion
  78.5 0.1 reshape.173
  78.6 2.3 %reduce-window.14 = f32[4,2,24,128]{3,2,1,0:T(8,128)S(1)} reduce-window(f32[4,2,24,128]{3,2,1,0:T(8,128)S(1)} %reshape.173, f32[]{:T(128)} %constant.13.clone.1), window={size=1x1x1x128 pad=0_0x0_0x0_0x127_0}, to_apply=%region_0.0 | reduce-window | flops 3121152 | bytes 196612 | tf_op jit(solution)/shard_map/reduce-window
  80.9 0.2 slice_reduce_fusion
  81.1 0.8 reduce-window.15
  81.9 0.1 broadcast_add_fusion
  82.0 0.1 reduce_window_sum.39
  82.1 0.1 slice.52
  82.1 0.1 copy.91
  82.2 0.1 copy.81
  82.3 3.2 %copy.79 = bf16[4,3072,128]{1,2,0:T(8,128)(2,1)S(1)} copy(bf16[4,3072,128]{2,1,0:T(8,128)(2,1)} %param.19) | data formatting | bytes 6291456 | tf_op args[5]
  85.6 0.1 negate_bitcast_fusion
  85.7 2.4 %reduce-window.16 = f32[4,2,4,128]{3,2,1,0:T(4,128)S(1)} reduce-window(f32[4,2,4,128]{3,2,1,0:T(4,128)S(1)} %reshape.176, f32[]{:T(128)} %constant.13.clone.1), window={size=1x1x1x128 pad=0_0x0_0x0_0x127_0}, to_apply=%region_2.3 | reduce-window | flops 520192 | bytes 32772 | tf_op jit(solution)/shard_map/reduce-window.2
  88.1 0.2 slice_reduce_fusion.1
  88.3 0.7 reduce-window.19
  89.0 0.1 broadcast_add_fusion.1
  89.1 0.1 reshape.202
  89.2 1.4 gather_fusion.1
  90.6 0.1 exponential_bitcast_fusion
  90.7 4.0 %fusion.6 = (bf16[4,3072,128]{1,2,0:T(8,128)(2,1)}, bf16[4,3072,128]{1,2,0:T(8,128)(2,1)}) fusion(bf16[4,3072,128]{1,2,0:T(8,128)(2,1)S(1)} %copy.79, f32[4,3072,2]{1,2,0:T(2,128)S(1)} %exponential_bitcast_fusion), kind=kLoop, calls=%fused_computation.13 | loop fusion | flops 9437184 | bytes 9535488 | tf_op jit(solution)/shard_map/convert_element_type | solution.py:72
  94.7 0.1 broadcast_compare_fusion
  94.8 0.1 iota_subtract_fusion
  94.9 0.1 broadcast_compare_fusion.1
  95.0 0.1 iota_add_fusion
  95.1 1.8 compare_and_fusion
  96.9 0.2 slice.57
  97.1 0.1 copy_convert_fusion
  97.1 1.4 copy.83
  98.5 1.6 fusion.44
  100.1 0.4 copy.90
  100.5 2.6 %fusion.18 = f32[4,512,512]{2,1,0:T(8,128)} fusion(bf16[4,512,128]{2,1,0:T(8,128)(2,1)S(1)} %copy.90, bf16[4,512,128]{1,0,2:T(4,128)(2,1)S(1)} %get-tuple-element.12), kind=kOutput, calls=%fused_computation.34 | convolution fusion | flops 268435456 | bytes 5242880 | tf_op jit(solution)/shard_map/rnk,rjk->rnj/dot_general | solution.py:95
  103.1 10.6 %all-gather.7.cloned.1.call-done = bf16[4,8,384,128]{3,2,0,1:T(8,128)(2,1)} async-done(((bf16[4,8,48,128]{3,2,0,1:T(8,128)(2,1)}), bf16[4,8,384,128]{3,2,0,1:T(8,128)(2,1)}) %all-gather.7.cloned.1.call-update) | async-done | bytes 3145744 | tf_op jit(solution)/shard_map/all_gather | solution.py:52
  113.8 3.9 %copy.78 = bf16[4,8,384,128]{3,2,1,0:T(8,128)(2,1)} copy(bf16[4,8,384,128]{3,2,0,1:T(8,128)(2,1)} %all-gather.7.cloned.1.call-done) | data formatting | bytes 6291456 | tf_op jit(solution)/shard_map/all_gather | solution.py:52
  117.6 1.3 gather_fusion
  119.0 11.7 %fusion.1 = f32[4,512,256]{1,2,0:T(8,128)S(1)} fusion(s32[4]{0:T(128)S(1)} %copy-done.9, s32[4,512]{1,0:T(4,128)S(1)} %iota_add_fusion, pred[4,3072]{1,0:T(4,128)(4,1)S(1)} %iota_compare_fusion, bf16[4,3072,128]{1,2,0:T(8,128)(2,1)} %get-tuple-element.11, bf16[4,3072,128]{1,2,0:T(8,128)(2,1)} %get-tuple-element.10, bf16[4,512,128]{2,1,0:T(8,128)(2,1)S(1)} %copy.90, ...), kind=kOutput, calls=%fused_computation.5 | convolution fusion | flops 4875878400 | bytes 12079120 | tf_op jit(solution)/shard_map/rns,rsc->rnc/dot_general | solution.py:82
  130.7 0.2 slice_add_fusion
  130.9 5.6 %fusion.12 = f32[4,512,2,64]{1,3,2,0:T(8,128)S(1)} fusion(f32[4,2,512]{2,1,0:T(2,128)S(1)} %reduce_window_sum.41, f32[4,512,512]{2,1,0:T(8,128)} %fusion.18, pred[4,512,512]{2,1,0:T(8,128)(4,1)} %compare_and_fusion, f32[4,512,2,64]{1,3,2,0:T(8,128)S(1)} %bitcast.75, f32[4,512,2,64]{1,3,2,0:T(8,128)} %bitcast.76, f32[4,512,2]{1,2,0:T(2,128)S(1)} %copy-done.7, ...), kind=kOutput, calls=%fused_computation.20 | convolution fusion | flops 279969792 | bytes 8437760 | tf_op jit(solution)/shard_map/rhnj,rjhd->rnhd/dot_general | solution.py:102
  136.6 0.3 copy.85
  136.9 0.6 fusion.13
  137.5 0.4 copy.98
  137.9 31.1 %all_to_all.17 = bf16[256,4,2,128]{3,2,1,0:T(2,128)(2,1)S(1)} all-to-all(bf16[256,4,2,128]{3,2,1,0:T(2,128)(2,1)S(1)} %bitcast.70), channel_id=1, replica_groups=mesh['tz'=8,'txc'=8,'mlp'=4] {'tz','txc','mlp'}, dimensions={0} | all-to-all | bytes 1048576 | tf_op jit(solution)/shard_map/all_to_all | solution.py:108
  169.0 0.2 copy.87
  169.2 0.1 reshape.183
  169.3 1.5 fusion.42
  170.8 0.9 mul.89
  171.7 0.2 reduce_sum.9
  171.9 0.1 copy.88
  171.9 0.1 copy.89
  172.0 0.1 mul.90
  172.2 0.9 mul.91
  173.1 1.4 multiply_convert_fusion.6
  (34 shorter events, 0.3 us)
Async XLA Ops:
  6.5 92.0 %all-gather.5.cloned.1.call-start = ((), (), s32[]{:S(2)}) async-start(), calls=%async_computation.3 | async-start | bytes 1179648 | tf_op jit(solution)/shard_map/all_gather | solution.py:45
  10.5 50.2 %copy-start.3 = (bf16[4,8,48,128]{3,2,1,0:T(8,128)(2,1)S(1)}, bf16[4,8,48,128]{3,2,1,0:T(8,128)(2,1)}, u32[]{:S(2)}) copy-start(bf16[4,8,48,128]{3,2,1,0:T(8,128)(2,1)} %param.20) | copy-start | bytes 1179652
  11.6 66.7 %copy-start.8 = (s32[4]{0:T(128)S(1)}, s32[4]{0:T(128)}, u32[]{:S(2)}) copy-start(s32[4]{0:T(128)} %param.22) | copy-start | bytes 52
  11.6 66.8 %copy-start.4 = (f32[4,2,3072]{2,1,0:T(2,128)S(1)}, f32[4,2,3072]{2,1,0:T(2,128)}, u32[]{:S(2)}) copy-start(f32[4,2,3072]{2,1,0:T(2,128)} %param.21) | copy-start | bytes 294916
  58.5 1.0 copy-start
  60.7 53.1 %all-gather.7.cloned.1.call-start = ((), (), s32[]{:S(2)}) async-start(), calls=%async_computation.4 | async-start | bytes 3538944 | tf_op jit(solution)/shard_map/all_gather | solution.py:52
  60.8 24.7 %copy-start.10 = (f32[2]{0:T(128)S(1)}, f32[2]{0:T(128)}, u32[]{:S(2)}) copy-start(f32[2]{0:T(128)} %param.18) | copy-start | bytes 28
  60.8 24.8 %copy-start.7 = (f32[4,512,2]{1,2,0:T(2,128)S(1)}, f32[4,512,2]{1,2,0:T(2,128)}, u32[]{:S(2)}) copy-start(f32[4,512,2]{1,2,0:T(2,128)} %param.17) | copy-start | bytes 49156
  78.3 10.8 %copy-start.6 = (s32[4,4]{1,0:T(4,128)S(1)}, s32[4,4]{1,0:T(4,128)}, u32[]{:S(2)}) copy-start(s32[4,4]{1,0:T(4,128)} %param.23) | copy-start | bytes 196
  90.7 4.4 %copy-start.9 = (s32[4]{0:T(128)S(1)}, s32[4]{0:T(128)}, u32[]{:S(2)}) copy-start(s32[4]{0:T(128)} %param.24) | copy-start | bytes 52
  90.7 6.1 %copy-start.1 = (bf16[4,256,2,160]{3,0,2,1:T(4,128)(2,1)S(1)}, bf16[4,256,2,160]{3,0,2,1:T(4,128)(2,1)}, u32[]{:S(2)}) copy-start(bf16[4,256,2,160]{3,0,2,1:T(4,128)(2,1)} %copy-done) | copy-start | bytes 1966084
  136.6 32.7 %copy-start.2 = (bf16[16,2,8192]{2,1,0:T(2,128)(2,1)S(1)}, bf16[16,2,8192]{2,1,0:T(2,128)(2,1)}, u32[]{:S(2)}) copy-start(bf16[16,2,8192]{2,1,0:T(2,128)(2,1)} %param.15) | copy-start | bytes 1572868
  169.3 3.8 %copy-start.5 = (f32[8192]{0:T(1024)S(1)}, f32[8192]{0:T(1024)}, u32[]{:S(2)}) copy-start(f32[8192]{0:T(1024)} %param.25) | copy-start | bytes 98308
Sparse Core Ops, SparseCore 0:
  60.8 20.9 all-gather.4
  83.6 30.1 all-gather.6

commit v5 on v2

--- a/solution.py
+++ b/solution.py
@@ -76,6 +76,18 @@
     x_pair = jnp.concatenate([x_hi, x_lo], axis=-1)
 
     query_pos = lengths[:, None] + token_order[None, :]
+    score_new = jnp.einsum("rnk,rjk->rnj", c_now, b_new, preferred_element_type=jnp.float32)
+    new_gap = token_order[:, None] - token_order[None, :]
+    keep_new = (new_gap[None] >= 0) & (new_gap[None] < windows[:, None, None])
+    cum_t = cum_new.transpose(0, 2, 1)
+    decay_new = jnp.exp(jnp.minimum(cum_t[:, :, :, None] - cum_t[:, :, None, :], 0.0))
+    weight_new = jnp.where(keep_new[:, None], decay_new, 0.0)
+    probs_new = (score_new[:, None] * weight_new).astype(jnp.bfloat16)
+    new_out = jnp.einsum("rhnj,rjhd->rnhd", probs_new, scaled, preferred_element_type=jnp.float32)
+
+
+    new_out, x_pair, shared_b = lax.optimization_barrier((new_out, x_pair, shared_b))
+
     in_window = (query_pos[:, :, None] - positions[None, None, :] < windows[:, None, None]) & live[
         :, None, :
     ]
@@ -93,15 +105,6 @@
     score_sink = jnp.einsum("rnk,rjk->rnj", c_now, sink_b, preferred_element_type=jnp.float32)
     probs_sink = jnp.where(sink_only, score_sink, 0.0).astype(jnp.bfloat16)
     sink_out = jnp.einsum("rnj,rjc->rnc", probs_sink, sink_x, preferred_element_type=jnp.float32)
-
-    score_new = jnp.einsum("rnk,rjk->rnj", c_now, b_new, preferred_element_type=jnp.float32)
-    new_gap = token_order[:, None] - token_order[None, :]
-    keep_new = (new_gap[None] >= 0) & (new_gap[None] < windows[:, None, None])
-    cum_t = cum_new.transpose(0, 2, 1)
-    decay_new = jnp.exp(jnp.minimum(cum_t[:, :, :, None] - cum_t[:, :, None, :], 0.0))
-    weight_new = jnp.where(keep_new[:, None], decay_new, 0.0)
-    probs_new = (score_new[:, None] * weight_new).astype(jnp.bfloat16)
-    new_out = jnp.einsum("rhnj,rjhd->rnhd", probs_new, scaled, preferred_element_type=jnp.float32)
 
     mixer_out = (old_out + new_out).reshape(requests, new_len, chans) + sink_out
     mixer_out = mixer_out.astype(jnp.bfloat16)

time: 165 us -> 160 us (0.970)
  waiting for transfers between devices: 9.62 us -> 4.09 us
  other arithmetic: 24.8 us -> 27.5 us
  starting transfers between devices: 13.7 us -> 15.9 us
  matrix products: 20.9 us -> 18.8 us
  blocking collectives: 54.8 us -> 53 us
    all_to_all x1, waiting for transfers between devices: 9.09 us -> 1.94 us  [per_device(): lax.all_to_all(b_cache, 'tz', split_axis=1, concat_axis=1, tiled=True)]
    concatenate x0 -> x1, other arithmetic: none -> 3.09 us  [per_device(): x_pair = jnp.concatenate([x_hi, x_lo], axis=-1)]
    convert_element_type x1, other arithmetic: 3.88 us -> 1.17 us  [per_device(): x_hi = x_scaled.astype(jnp.bfloat16)]
    all_to_all x1, starting transfers between devices: 10 us -> 12.2 us  [per_device(): head_x = lax.all_to_all(x_part, ('tz', 'txc', 'mlp'), 0, 0, tiled=True)]
    dot_general x1, matrix products: 2.66 us -> 0.71 us  [per_device(): jnp.einsum('rnk,rjk->rnj', c_now, b_new, preferred_element_type=jnp.float32)]
    all_to_all x1, blocking collectives: 33.5 us -> 31.7 us  [per_device(): back = lax.all_to_all(back, ('tz', 'txc', 'mlp'), 0, 0, tiled=True)]
    unnamed x32 -> x24, local copies, waits for them, and re-layouts: 6.55 us -> 6.47 us
  transfers between devices with their start and end apart: 4 -> 4, of which waited for: 1 -> 2; matrix products, arithmetic and copies ran while one was open for 25% -> 28% of each run, Pallas kernels for 0% -> 0%
where the time goes in v5:
time: 160 us; the launch traced here: 159 us
  blocking collectives  53 us (33%)
  other arithmetic  27.5 us (17%)
  local copies, waits for them, and re-layouts  26.3 us (16%)
  matrix products  18.8 us (12%)
  starting transfers between devices  15.9 us (10%)
  between operations  13.8 us (9%)
  waiting for transfers between devices  4.09 us (3%)
    all_to_all x1, blocking collectives, per_device(): back = lax.all_to_all(back, ('tz', 'txc', 'mlp'), 0, 0, tiled=True)  31.7 us
    all_to_all x1, blocking collectives, per_device(): sp = lax.all_to_all(sp, ('tz', 'mlp'), 0, 0, tiled=True)  21.3 us
    dot_general x1, matrix products, per_device(): jnp.einsum('rns,rsc->rnc', probs_old, x_pair, preferred_element_type=jnp....  13.3 us
    all_to_all x1, starting transfers between devices, per_device(): head_x = lax.all_to_all(x_part, ('tz', 'txc', 'mlp'), 0, 0, tiled=True)  12.2 us
    unnamed x24, local copies, waits for them, and re-layouts  6.47 us
    another operation x6, other arithmetic  6.42 us
    convert_element_type x1, other arithmetic, per_device(): scaled = (scaled * step_size[..., None]).astype(jnp.bfloat16)  5.33 us
    dot_general x1, matrix products, per_device(): jnp.einsum('rhnj,rjhd->rnhd', probs_new, scaled, preferred_element_type=j...  4.22 us
  transfers between devices with their start and end apart: 4, of which 2 were waited for; matrix products, arithmetic and copies ran while one was open for 28% of the time, Pallas kernels for 0%

profile of v5, /device:TPU:1, one launch (start us, length us, event | category | flops | bytes accessed | tf_op | source)
XLA Modules:
  0.0 159.4 jit_solution(5985747772355849586)
XLA Ops:
  6.5 1.0 copy.71
  7.6 21.3 %all_to_all.20 = bf16[32,4,2,256]{3,2,1,0:T(2,128)(2,1)} all-to-all(bf16[32,4,2,256]{3,2,1,0:T(2,128)(2,1)S(1)} %bitcast.86), channel_id=1, replica_groups=mesh['tz'=8,'txc'=8,'mlp'=4] {'tz','mlp'}, dimensions={0} | all-to-all | bytes 262144 | tf_op jit(solution)/shard_map/all_to_all | solution.py:45
  28.9 1.8 %copy.79 = bf16[4,8,48,128]{3,2,0,1:T(8,128)(2,1)} copy(bf16[4,8,48,128]{3,2,1,0:T(8,128)(2,1)} %param.20) | data formatting | bytes 786432 | tf_op args[6]
  30.6 3.5 %all-to-all-start.2 = ((bf16[4,8,48,128]{3,2,0,1:T(8,128)(2,1)}), bf16[4,8,48,128]{3,2,0,1:T(8,128)(2,1)S(1)}, u32[]{:S(2)}, u32[]{:S(2)}) async-start(bf16[4,8,48,128]{3,2,0,1:T(8,128)(2,1)} %copy.79), calls=%async_computation.2 | async-start | bytes 786432 | tf_op jit(solution)/shard_map/all_to_all | solution.py:39
  34.1 0.7 exp.19
  34.8 0.8 negate_bitcast_fusion
  35.6 2.4 %reduce-window.14 = f32[4,2,4,128]{3,2,1,0:T(4,128)S(1)} reduce-window(f32[4,2,4,128]{3,2,1,0:T(4,128)S(1)} %reshape.174, f32[]{:T(128)} %constant.12.clone.1), window={size=1x1x1x128 pad=0_0x0_0x0_0x127_0}, to_apply=%region_0.0 | reduce-window | flops 520192 | bytes 32772 | tf_op jit(solution)/shard_map/reduce-window
  38.0 0.7 iota_compare_fusion
  38.8 0.2 slice_reduce_fusion.1
  38.9 0.7 reduce-window.15
  39.6 1.4 reshape.168
  41.1 0.4 copy.67
  41.5 1.3 copy.68
  42.8 1.6 %broadcast_select_fusion = f32[4,2,3072]{2,1,0:T(2,128)} fusion(f32[4,2,3072]{2,1,0:T(2,128)} %param.21, pred[4,3072]{1,0:T(4,128)(4,1)S(1)} %iota_compare_fusion), kind=kLoop, calls=%fused_computation.44 | loop fusion | flops 24576 | bytes 208896 | tf_op jit(solution)/shard_map/jit(_where)/select_n | solution.py:65
  44.4 1.9 %all-to-all-done.2 = bf16[4,8,48,128]{3,2,0,1:T(8,128)(2,1)S(1)} async-done(((bf16[4,8,48,128]{3,2,0,1:T(8,128)(2,1)}), bf16[4,8,48,128]{3,2,0,1:T(8,128)(2,1)S(1)}, u32[]{:S(2)}, u32[]{:S(2)}) %all-to-all-start.2) | async-done | bytes 393248 | tf_op jit(solution)/shard_map/all_to_all | solution.py:39
  46.4 12.2 %all-to-all-start = ((bf16[256,4,2,128]{3,2,1,0:T(2,128)(2,1)}), bf16[256,4,2,128]{3,2,1,0:T(2,128)(2,1)}, u32[]{:S(2)}, u32[]{:S(2)}) async-start(bf16[256,4,2,128]{3,2,1,0:T(2,128)(2,1)} %copy.68), calls=%async_computation | async-start | bytes 1048576 | tf_op jit(solution)/shard_map/all_to_all | solution.py:54
  58.6 0.2 all-gather.7.cloned.1.call-start
  58.8 0.5 all-gather.7.cloned.1.call-update
  59.4 0.1 broadcast_add_fusion.1
  59.4 1.4 copy.70
  60.8 3.2 %copy.76 = bf16[4,3072,128]{1,2,0:T(8,128)(2,1)S(1)} copy(bf16[4,3072,128]{2,1,0:T(8,128)(2,1)} %param.19) | data formatting | bytes 6291456 | tf_op args[5]
  64.0 0.1 reshape.176
  64.1 2.3 %reduce-window.16 = f32[4,2,24,128]{3,2,1,0:T(8,128)S(1)} reduce-window(f32[4,2,24,128]{3,2,1,0:T(8,128)S(1)} %reshape.176, f32[]{:T(128)} %constant.12.clone.1), window={size=1x1x1x128 pad=0_0x0_0x0_0x127_0}, to_apply=%region_2.3 | reduce-window | flops 3121152 | bytes 196612 | tf_op jit(solution)/shard_map/reduce-window.2
  66.4 0.2 slice_reduce_fusion
  66.6 0.8 reduce-window.19
  67.4 0.1 broadcast_add_fusion
  67.7 0.1 copy.90
  67.8 0.1 copy.78
  67.9 0.1 reshape.201
  67.9 1.4 gather_fusion.1
  69.4 0.1 exponential_bitcast_fusion
  69.5 1.2 fusion.5
  70.7 0.1 broadcast_compare_fusion
  70.8 0.1 iota_subtract_fusion
  71.1 1.7 %compare_and_fusion = pred[4,512,512]{2,1,0:T(8,128)(4,1)} fusion(s32[512,512]{1,0:T(8,128)S(1)} %iota_subtract_fusion, s32[4]{0:T(128)S(1)} %copy-done.9, pred[512,512]{1,0:T(8,128)(4,1)S(1)} %broadcast_compare_fusion), kind=kLoop, calls=%fused_computation.15 | loop fusion | flops 2097152 | bytes 2359312 | tf_op jit(solution)/shard_map/and | solution.py:81
  72.8 3.1 %pad_maximum_fusion = bf16[4,3072,256]{1,2,0:T(8,128)(2,1)} fusion(bf16[4,3072,128]{1,2,0:T(8,128)(2,1)S(1)} %get-tuple-element.15, bf16[4,3072,128]{1,2,0:T(8,128)(2,1)S(1)} %get-tuple-element.14), kind=kLoop, calls=%fused_computation.9 | loop fusion | flops 12582912 | bytes 12582912 | tf_op jit(solution)/shard_map/concatenate | solution.py:76
  75.9 1.6 %all-to-all-done = bf16[256,4,2,128]{3,2,1,0:T(2,128)(2,1)} async-done(((bf16[256,4,2,128]{3,2,1,0:T(2,128)(2,1)}), bf16[256,4,2,128]{3,2,1,0:T(2,128)(2,1)}, u32[]{:S(2)}, u32[]{:S(2)}) %all-to-all-start) | async-done | bytes 524320 | tf_op jit(solution)/shard_map/all_to_all | solution.py:54
  77.6 1.4 convert_bitcast_fusion
  79.0 0.4 copy.69
  79.3 1.9 %reshape.184 = f32[4,512,2,64]{3,2,1,0:T(2,128)S(1)} reshape(f32[4,256,2,128]{3,2,1,0:T(2,128)S(1)} %copy.69) | data formatting | bytes 2097152 | tf_op jit(solution)/shard_map/convert_element_type | solution.py:59
  81.2 5.3 %multiply_convert_fusion.2 = bf16[4,512,2,64]{3,2,1,0:T(2,128)(2,1)} fusion(f32[4,512,2,64]{3,2,1,0:T(2,128)S(1)} %reshape.184, f32[4,512,2]{2,1,0:T(8,128)} %copy.70), kind=kLoop, calls=%fused_computation.16 | loop fusion | flops 524288 | bytes 1589248 | tf_op jit(solution)/shard_map/convert_element_type | solution.py:60
  86.6 1.9 %copy.72 = bf16[8,4,8,4,2,256]{5,3,4,1,2,0:T(4,128)(2,1)S(1)} copy(bf16[8,4,8,4,2,256]{5,4,3,2,1,0:T(2,128)(2,1)} %bitcast.85) | data formatting | bytes 2097152 | tf_op jit(solution)/shard_map/reshape | solution.py:47
  88.5 0.4 fusion.47
  88.9 0.7 fusion.18
  89.6 4.2 %fusion.10 = f32[4,512,2,64]{1,3,2,0:T(8,128)} fusion(f32[4,2,512]{2,1,0:T(2,128)S(1)} %reduce_window_sum.39, f32[4,512,512]{2,1,0:T(8,128)S(1)} %fusion.18, pred[4,512,512]{2,1,0:T(8,128)(4,1)S(1)} %copy-done.1, bf16[4,512,2,64]{3,2,1,0:T(2,128)(2,1)S(1)} %copy-done.2), kind=kOutput, calls=%fused_computation.18 | convolution fusion | flops 278921216 | bytes 6832128 | tf_op jit(solution)/shard_map/rhnj,rjhd->rnhd/dot_general | solution.py:86
  93.8 3.9 %copy.80 = bf16[4,8,384,128]{3,2,1,0:T(8,128)(2,1)} copy(bf16[4,8,384,128]{3,2,0,1:T(8,128)(2,1)} %all-gather.7.cloned.1.call-done) | data formatting | bytes 6291456 | tf_op jit(solution)/shard_map/all_gather | solution.py:40
  97.7 1.3 gather_fusion
  99.0 13.3 %fusion.2 = f32[4,512,256]{1,2,0:T(8,128)S(1)} fusion(bf16[4,3072,256]{1,2,0:T(8,128)(2,1)} %pad_maximum_fusion, s32[4]{0:T(128)S(1)} %copy-done.9, s32[4,512]{1,0:T(4,128)S(1)} %iota_add_fusion, pred[4,3072]{1,0:T(4,128)(4,1)S(1)} %iota_compare_fusion, bf16[4,3072,128]{2,1,0:T(8,128)(2,1)} %bitcast.80, bf16[4,512,128]{2,0,1:T(4,128)(2,1)S(1)} %get-tuple-element.16), kind=kOutput, calls=%fused_computation.6 | convolution fusion | flops 4863295488 | bytes 12079120 | tf_op jit(solution)/shard_map/rns,rsc->rnc/dot_general | solution.py:96
  112.3 0.2 slice_add_fusion
  112.5 1.5 multiply_add_fusion
  114.1 0.3 copy.82
  114.4 0.6 fusion.11
  115.0 0.4 copy.104
  115.4 31.7 %all_to_all.21 = bf16[256,4,2,128]{3,2,1,0:T(2,128)(2,1)S(1)} all-to-all(bf16[256,4,2,128]{3,2,1,0:T(2,128)(2,1)S(1)} %bitcast.82), channel_id=1, replica_groups=mesh['tz'=8,'txc'=8,'mlp'=4] {'tz','txc','mlp'}, dimensions={0} | all-to-all | bytes 1048576 | tf_op jit(solution)/shard_map/all_to_all | solution.py:113
  147.1 0.2 copy.84
  147.3 0.1 reshape.183
  147.5 1.5 fusion.45
  148.9 0.9 mul.89
  149.8 0.2 reduce_sum.9
  150.0 0.1 copy.85
  150.1 0.1 copy.86
  150.2 0.1 mul.90
  150.3 0.9 mul.91
  151.2 1.4 multiply_convert_fusion.5
  (34 shorter events, 0.4 us)
Async XLA Ops:
  6.5 52.9 %copy-start.5 = (f32[4,512,2]{1,2,0:T(2,128)S(1)}, f32[4,512,2]{1,2,0:T(2,128)}, u32[]{:S(2)}) copy-start(f32[4,512,2]{1,2,0:T(2,128)} %param.17) | copy-start | bytes 49156
  6.5 80.0 %all-gather.5.cloned.1.call-start = ((), (), s32[]{:S(2)}) async-start(), calls=%async_computation.4 | async-start | bytes 1179648 | tf_op jit(solution)/shard_map/all_gather | solution.py:46
  30.6 15.7 %all-to-all-start.2 = ((bf16[4,8,48,128]{3,2,0,1:T(8,128)(2,1)}), bf16[4,8,48,128]{3,2,0,1:T(8,128)(2,1)S(1)}, u32[]{:S(2)}, u32[]{:S(2)}) async-start(bf16[4,8,48,128]{3,2,0,1:T(8,128)(2,1)} %copy.79), calls=%async_computation.2 | async-start | bytes 786432 | tf_op jit(solution)/shard_map/all_to_all | solution.py:39
  41.1 26.8 %copy-start.7 = (s32[4,4]{1,0:T(4,128)S(1)}, s32[4,4]{1,0:T(4,128)}, u32[]{:S(2)}) copy-start(s32[4,4]{1,0:T(4,128)} %param.23) | copy-start | bytes 196
  46.4 12.4 %copy-start = (bf16[4,8,48,128]{3,2,0,1:T(8,128)(2,1)}, bf16[4,8,48,128]{3,2,0,1:T(8,128)(2,1)S(1)}, u32[]{:S(2)}) copy-start(bf16[4,8,48,128]{3,2,0,1:T(8,128)(2,1)S(1)} %all-to-all-done.2) | copy-start | bytes 1179652
  46.4 31.2 %all-to-all-start = ((bf16[256,4,2,128]{3,2,1,0:T(2,128)(2,1)}), bf16[256,4,2,128]{3,2,1,0:T(2,128)(2,1)}, u32[]{:S(2)}, u32[]{:S(2)}) async-start(bf16[256,4,2,128]{3,2,1,0:T(2,128)(2,1)} %copy.68), calls=%async_computation | async-start | bytes 1048576 | tf_op jit(solution)/shard_map/all_to_all | solution.py:54
  58.6 35.2 %all-gather.7.cloned.1.call-start = ((), (), s32[]{:S(2)}) async-start(), calls=%async_computation.5 | async-start | bytes 3538944 | tf_op jit(solution)/shard_map/all_gather | solution.py:40
  59.3 4.7 %copy-start.4 = (f32[4,2,3072]{2,1,0:T(2,128)S(1)}, f32[4,2,3072]{2,1,0:T(2,128)}, u32[]{:S(2)}) copy-start(f32[4,2,3072]{2,1,0:T(2,128)} %broadcast_select_fusion) | copy-start | bytes 294916
  64.0 6.9 %copy-start.8 = (s32[4]{0:T(128)S(1)}, s32[4]{0:T(128)}, u32[]{:S(2)}) copy-start(s32[4]{0:T(128)} %param.22) | copy-start | bytes 52
  64.0 7.1 %copy-start.9 = (s32[4]{0:T(128)S(1)}, s32[4]{0:T(128)}, u32[]{:S(2)}) copy-start(s32[4]{0:T(128)} %param.24) | copy-start | bytes 52
  81.2 8.4 %copy-start.1 = (pred[4,512,512]{2,1,0:T(8,128)(4,1)S(1)}, pred[4,512,512]{2,1,0:T(8,128)(4,1)}, u32[]{:S(2)}) copy-start(pred[4,512,512]{2,1,0:T(8,128)(4,1)} %compare_and_fusion) | copy-start | bytes 3145732
  86.6 3.0 %copy-start.2 = (bf16[4,512,2,64]{3,2,1,0:T(2,128)(2,1)S(1)}, bf16[4,512,2,64]{3,2,1,0:T(2,128)(2,1)}, u32[]{:S(2)}) copy-start(bf16[4,512,2,64]{3,2,1,0:T(2,128)(2,1)} %multiply_convert_fusion.2) | copy-start | bytes 1572868
  112.5 34.9 %copy-start.3 = (bf16[16,2,8192]{2,1,0:T(2,128)(2,1)S(1)}, bf16[16,2,8192]{2,1,0:T(2,128)(2,1)}, u32[]{:S(2)}) copy-start(bf16[16,2,8192]{2,1,0:T(2,128)(2,1)} %param.15) | copy-start | bytes 1572868
  115.4 35.8 %copy-start.6 = (f32[8192]{0:T(1024)S(1)}, f32[8192]{0:T(1024)}, u32[]{:S(2)}) copy-start(f32[8192]{0:T(1024)} %param.25) | copy-start | bytes 98308
Sparse Core Ops, SparseCore 0:
  29.0 22.6 all-gather.4
  61.2 32.4 all-gather.6

commit v6 on v5

--- a/solution.py
+++ b/solution.py
@@ -71,9 +71,7 @@
     x_scaled = x_cache.astype(jnp.float32).reshape(requests, cache_len, heads_dev, head_dim)
     x_scaled = x_scaled * col_scale.transpose(0, 2, 1)[..., None]
     x_scaled = x_scaled.reshape(requests, cache_len, chans)
-    x_hi = x_scaled.astype(jnp.bfloat16)
-    x_lo = (x_scaled - x_hi.astype(jnp.float32)).astype(jnp.bfloat16)
-    x_pair = jnp.concatenate([x_hi, x_lo], axis=-1)
+    x_pair = x_scaled.astype(jnp.bfloat16)
 
     query_pos = lengths[:, None] + token_order[None, :]
     score_new = jnp.einsum("rnk,rjk->rnj", c_now, b_new, preferred_element_type=jnp.float32)
@@ -94,7 +92,7 @@
     score_old = jnp.einsum("rnk,rsk->rns", c_now, shared_b, preferred_element_type=jnp.float32)
     probs_old = jnp.where(in_window, score_old, 0.0).astype(jnp.bfloat16)
     acc = jnp.einsum("rns,rsc->rnc", probs_old, x_pair, preferred_element_type=jnp.float32)
-    old_out = (acc[..., :chans] + acc[..., chans:]).reshape(requests, new_len, heads_dev, head_dim)
+    old_out = acc.reshape(requests, new_len, heads_dev, head_dim)
     old_out = old_out * row_scale[..., None]
 
     sink_b = jnp.take_along_axis(shared_b, sink_pos[:, :, None], axis=1)

time: 160 us -> 157 us (0.981)
  waiting for transfers between devices: 4.09 us -> 6.45 us
  matrix products: 18.8 us -> 16.6 us
  starting transfers between devices: 15.9 us -> 13.8 us
  other arithmetic: 27.5 us -> 25.5 us
    concatenate x1 -> x0, other arithmetic: 3.09 us -> none  [per_device(): x_pair = jnp.concatenate([x_hi, x_lo], axis=-1)]
    all_to_all x1, waiting for transfers between devices: 1.94 us -> 4.21 us  [per_device(): lax.all_to_all(b_cache, 'tz', split_axis=1, concat_axis=1, tiled=True)]
    all_to_all x1, starting transfers between devices: 12.2 us -> 10 us  [per_device(): head_x = lax.all_to_all(x_part, ('tz', 'txc', 'mlp'), 0, 0, tiled=True)]
    unnamed x24 -> x28, local copies, waits for them, and re-layouts: 6.47 us -> 6.74 us
  transfers between devices with their start and end apart: 4 -> 4, of which waited for: 2 -> 3; matrix products, arithmetic and copies ran while one was open for 28% -> 27% of each run, Pallas kernels for 0% -> 0%
where the time goes in v6:
time: 157 us; the launch traced here: 156 us
  blocking collectives  53 us (34%)
  local copies, waits for them, and re-layouts  26.6 us (17%)
  other arithmetic  25.5 us (16%)
  matrix products  16.6 us (11%)
  starting transfers between devices  13.8 us (9%)
  between operations  13.8 us (9%)
  waiting for transfers between devices  6.45 us (4%)
    all_to_all x1, blocking collectives, per_device(): back = lax.all_to_all(back, ('tz', 'txc', 'mlp'), 0, 0, tiled=True)  31.7 us
    all_to_all x1, blocking collectives, per_device(): sp = lax.all_to_all(sp, ('tz', 'mlp'), 0, 0, tiled=True)  21.3 us
    dot_general x1, matrix products, per_device(): jnp.einsum('rns,rsc->rnc', probs_old, x_pair, preferred_element_type=jnp....  11.8 us
    all_to_all x1, starting transfers between devices, per_device(): head_x = lax.all_to_all(x_part, ('tz', 'txc', 'mlp'), 0, 0, tiled=True)  10 us
    unnamed x28, local copies, waits for them, and re-layouts  6.74 us
    another operation x6, other arithmetic  6.41 us
    convert_element_type x1, other arithmetic, per_device(): scaled = (scaled * step_size[..., None]).astype(jnp.bfloat16)  4.66 us
    all_to_all x1, waiting for transfers between devices, per_device(): lax.all_to_all(b_cache, 'tz', split_axis=1, concat_axis=1, tiled=True)  4.21 us
  transfers between devices with their start and end apart: 4, of which 3 were waited for; matrix products, arithmetic and copies ran while one was open for 27% of the time, Pallas kernels for 0%

profile of v6, /device:TPU:1, one launch (start us, length us, event | category | flops | bytes accessed | tf_op | source)
XLA Modules:
  0.0 155.7 jit_solution(14685760737478416126)
XLA Ops:
  6.5 1.0 copy.71
  7.6 21.3 %all_to_all.20 = bf16[32,4,2,256]{3,2,1,0:T(2,128)(2,1)} all-to-all(bf16[32,4,2,256]{3,2,1,0:T(2,128)(2,1)S(1)} %bitcast.82), channel_id=1, replica_groups=mesh['tz'=8,'txc'=8,'mlp'=4] {'tz','mlp'}, dimensions={0} | all-to-all | bytes 262144 | tf_op jit(solution)/shard_map/all_to_all | solution.py:45
  28.9 1.8 %copy.79 = bf16[4,8,48,128]{3,2,0,1:T(8,128)(2,1)} copy(bf16[4,8,48,128]{3,2,1,0:T(8,128)(2,1)} %param.20) | data formatting | bytes 786432 | tf_op args[6]
  30.7 3.6 %all-to-all-start.2 = ((bf16[4,8,48,128]{3,2,0,1:T(8,128)(2,1)}), bf16[4,8,48,128]{3,2,0,1:T(8,128)(2,1)S(1)}, u32[]{:S(2)}, u32[]{:S(2)}) async-start(bf16[4,8,48,128]{3,2,0,1:T(8,128)(2,1)} %copy.79), calls=%async_computation.2 | async-start | bytes 786432 | tf_op jit(solution)/shard_map/all_to_all | solution.py:39
  34.3 0.7 exp.19
  34.9 0.8 negate_bitcast_fusion
  35.8 2.4 %reduce-window.14 = f32[4,2,4,128]{3,2,1,0:T(4,128)S(1)} reduce-window(f32[4,2,4,128]{3,2,1,0:T(4,128)S(1)} %reshape.174, f32[]{:T(128)} %constant.12.clone.1), window={size=1x1x1x128 pad=0_0x0_0x0_0x127_0}, to_apply=%region_0.0 | reduce-window | flops 520192 | bytes 32772 | tf_op jit(solution)/shard_map/reduce-window
  38.2 0.2 slice_reduce_fusion.1
  38.4 0.7 reduce-window.15
  39.1 1.4 reshape.168
  40.5 0.4 copy.67
  40.9 1.3 copy.68
  42.3 0.1 iota_compare_fusion
  42.3 4.2 %all-to-all-done.2 = bf16[4,8,48,128]{3,2,0,1:T(8,128)(2,1)S(1)} async-done(((bf16[4,8,48,128]{3,2,0,1:T(8,128)(2,1)}), bf16[4,8,48,128]{3,2,0,1:T(8,128)(2,1)S(1)}, u32[]{:S(2)}, u32[]{:S(2)}) %all-to-all-start.2) | async-done | bytes 393248 | tf_op jit(solution)/shard_map/all_to_all | solution.py:39
  46.6 10.0 %all-to-all-start = ((bf16[256,4,2,128]{3,2,1,0:T(2,128)(2,1)}), bf16[256,4,2,128]{3,2,1,0:T(2,128)(2,1)}, u32[]{:S(2)}, u32[]{:S(2)}) async-start(bf16[256,4,2,128]{3,2,1,0:T(2,128)(2,1)} %copy.68), calls=%async_computation | async-start | bytes 1048576 | tf_op jit(solution)/shard_map/all_to_all | solution.py:54
  56.6 0.2 all-gather.7.cloned.1.call-start
  56.8 0.5 all-gather.7.cloned.1.call-update
  57.4 0.1 reshape.176
  57.5 2.3 %reduce-window.16 = f32[4,2,24,128]{3,2,1,0:T(8,128)S(1)} reduce-window(f32[4,2,24,128]{3,2,1,0:T(8,128)S(1)} %reshape.176, f32[]{:T(128)} %constant.12.clone.1), window={size=1x1x1x128 pad=0_0x0_0x0_0x127_0}, to_apply=%region_2.3 | reduce-window | flops 3121152 | bytes 196612 | tf_op jit(solution)/shard_map/reduce-window.2
  59.8 0.2 slice_reduce_fusion
  60.0 0.8 reduce-window.19
  60.8 0.1 broadcast_add_fusion
  61.0 0.1 copy.90
  61.1 0.1 copy.78
  61.2 1.1 iota_subtract_fusion
  62.4 0.5 and_bitcast_fusion
  63.0 0.1 exponential_bitcast_fusion
  63.1 0.1 broadcast_compare_fusion
  63.2 1.4 copy.70
  64.7 3.2 %copy.76 = bf16[4,3072,128]{1,2,0:T(8,128)(2,1)S(1)} copy(bf16[4,3072,128]{2,1,0:T(8,128)(2,1)} %param.19) | data formatting | bytes 6291456 | tf_op args[5]
  67.9 0.1 reshape.201
  68.0 1.4 gather_fusion.1
  69.4 2.4 %fusion.5 = bf16[4,3072,128]{1,2,0:T(8,128)(2,1)} fusion(bf16[4,3072,128]{1,2,0:T(8,128)(2,1)S(1)} %copy.76, f32[4,3072,2]{1,2,0:T(2,128)S(1)} %exponential_bitcast_fusion), kind=kLoop, calls=%fused_computation.10 | loop fusion | flops 4718592 | bytes 6389760 | tf_op jit(solution)/shard_map/convert_element_type | solution.py:74
  71.9 0.7 iota_add_fusion
  72.6 2.4 %compare_and_fusion = pred[4,512,512]{2,1,0:T(8,128)(4,1)} fusion(s32[512,512]{1,0:T(8,128)S(1)} %copy-done, s32[4]{0:T(128)} %param.24, pred[512,512]{1,0:T(8,128)(4,1)S(1)} %broadcast_compare_fusion), kind=kLoop, calls=%fused_computation.13 | loop fusion | flops 2097152 | bytes 2359312 | tf_op jit(solution)/shard_map/and | solution.py:79
  75.1 0.5 all-to-all-done
  75.6 1.4 convert_bitcast_fusion
  77.0 0.4 copy.69
  77.3 1.9 %reshape.184 = f32[4,512,2,64]{3,2,1,0:T(2,128)S(1)} reshape(f32[4,256,2,128]{3,2,1,0:T(2,128)S(1)} %copy.69) | data formatting | bytes 2097152 | tf_op jit(solution)/shard_map/convert_element_type | solution.py:59
  79.2 4.7 %multiply_convert_fusion.2 = bf16[4,512,2,64]{3,2,1,0:T(2,128)(2,1)S(1)} fusion(f32[4,512,2,64]{3,2,1,0:T(2,128)S(1)} %reshape.184, f32[4,512,2]{2,1,0:T(8,128)} %copy.70), kind=kLoop, calls=%fused_computation.15 | loop fusion | flops 524288 | bytes 1589248 | tf_op jit(solution)/shard_map/convert_element_type | solution.py:60
  83.9 1.8 %copy.72 = bf16[8,4,8,4,2,256]{5,3,4,1,2,0:T(4,128)(2,1)S(1)} copy(bf16[8,4,8,4,2,256]{5,4,3,2,1,0:T(2,128)(2,1)} %bitcast.81) | data formatting | bytes 2097152 | tf_op jit(solution)/shard_map/reshape | solution.py:47
  85.8 0.4 fusion.47
  86.1 0.7 fusion.18
  86.8 0.2 copy-done.2
  87.0 3.5 %fusion.10 = f32[4,512,2,64]{1,3,2,0:T(8,128)S(1)} fusion(f32[4,2,512]{2,1,0:T(2,128)S(1)} %reduce_window_sum.39, f32[4,512,512]{2,1,0:T(8,128)S(1)} %fusion.18, pred[4,512,512]{2,1,0:T(8,128)(4,1)S(1)} %copy-done.2, bf16[4,512,2,64]{3,2,1,0:T(2,128)(2,1)S(1)} %multiply_convert_fusion.2), kind=kOutput, calls=%fused_computation.16 | convolution fusion | flops 278921216 | bytes 6832128 | tf_op jit(solution)/shard_map/rhnj,rjhd->rnhd/dot_general | solution.py:84
  90.6 1.2 all-gather.7.cloned.1.call-done
  91.8 3.9 %copy.80 = bf16[4,8,384,128]{3,2,1,0:T(8,128)(2,1)} copy(bf16[4,8,384,128]{3,2,0,1:T(8,128)(2,1)} %all-gather.7.cloned.1.call-done) | data formatting | bytes 6291456 | tf_op jit(solution)/shard_map/all_gather | solution.py:40
  95.7 1.3 gather_fusion
  97.0 11.8 %fusion.2 = f32[4,512,128]{1,2,0:T(8,128)} fusion(bf16[4,3072,128]{1,2,0:T(8,128)(2,1)} %fusion.5, s32[4]{0:T(128)S(1)} %copy-done.11, s32[4,512]{1,0:T(4,128)S(1)} %iota_add_fusion, pred[4,3072]{1,0:T(4,128)(4,1)S(1)} %iota_compare_fusion, bf16[4,3072,128]{2,1,0:T(8,128)(2,1)} %bitcast.75, bf16[4,512,128]{2,0,1:T(4,128)(2,1)S(1)} %get-tuple-element.14), kind=kOutput, calls=%fused_computation.6 | convolution fusion | flops 3252682752 | bytes 7884816 | tf_op jit(solution)/shard_map/rns,rsc->rnc/dot_general | solution.py:94
  108.8 1.5 multiply_add_fusion
  110.3 0.3 copy.82
  110.6 0.6 fusion.11
  111.2 0.4 copy.104
  111.6 31.7 %all_to_all.21 = bf16[256,4,2,128]{3,2,1,0:T(2,128)(2,1)S(1)} all-to-all(bf16[256,4,2,128]{3,2,1,0:T(2,128)(2,1)S(1)} %bitcast.77), channel_id=1, replica_groups=mesh['tz'=8,'txc'=8,'mlp'=4] {'tz','txc','mlp'}, dimensions={0} | all-to-all | bytes 1048576 | tf_op jit(solution)/shard_map/all_to_all | solution.py:111
  143.3 0.2 copy.84
  143.5 0.1 reshape.183
  143.7 1.5 fusion.45
  145.2 0.9 mul.89
  146.1 0.2 reduce_sum.9
  146.2 0.1 copy.85
  146.3 0.1 copy.86
  146.4 0.1 mul.90
  146.6 0.9 mul.91
  147.5 1.4 multiply_convert_fusion.5
  (36 shorter events, 0.5 us)
Async XLA Ops:
  6.5 35.7 %copy-start.9 = (s32[4]{0:T(128)S(1)}, s32[4]{0:T(128)}, u32[]{:S(2)}) copy-start(s32[4]{0:T(128)} %param.22) | copy-start | bytes 52
  6.5 50.8 %copy-start.4 = (f32[4,2,3072]{2,1,0:T(2,128)S(1)}, f32[4,2,3072]{2,1,0:T(2,128)}, u32[]{:S(2)}) copy-start(f32[4,2,3072]{2,1,0:T(2,128)} %param.21) | copy-start | bytes 294916
  6.5 77.4 %all-gather.5.cloned.1.call-start = ((), (), s32[]{:S(2)}) async-start(), calls=%async_computation.4 | async-start | bytes 1179648 | tf_op jit(solution)/shard_map/all_gather | solution.py:46
  28.9 33.5 %copy-start.7 = (s32[4,4]{1,0:T(4,128)S(1)}, s32[4,4]{1,0:T(4,128)}, u32[]{:S(2)}) copy-start(s32[4,4]{1,0:T(4,128)} %param.23) | copy-start | bytes 196
  30.7 32.5 %copy-start.5 = (f32[4,512,2]{1,2,0:T(2,128)S(1)}, f32[4,512,2]{1,2,0:T(2,128)}, u32[]{:S(2)}) copy-start(f32[4,512,2]{1,2,0:T(2,128)} %param.17) | copy-start | bytes 49156
  30.7 15.9 %all-to-all-start.2 = ((bf16[4,8,48,128]{3,2,0,1:T(8,128)(2,1)}), bf16[4,8,48,128]{3,2,0,1:T(8,128)(2,1)S(1)}, u32[]{:S(2)}, u32[]{:S(2)}) async-start(bf16[4,8,48,128]{3,2,0,1:T(8,128)(2,1)} %copy.79), calls=%async_computation.2 | async-start | bytes 786432 | tf_op jit(solution)/shard_map/all_to_all | solution.py:39
  46.6 10.2 %copy-start.1 = (bf16[4,8,48,128]{3,2,0,1:T(8,128)(2,1)}, bf16[4,8,48,128]{3,2,0,1:T(8,128)(2,1)S(1)}, u32[]{:S(2)}) copy-start(bf16[4,8,48,128]{3,2,0,1:T(8,128)(2,1)S(1)} %all-to-all-done.2) | copy-start | bytes 1179652
  46.6 29.0 %all-to-all-start = ((bf16[256,4,2,128]{3,2,1,0:T(2,128)(2,1)}), bf16[256,4,2,128]{3,2,1,0:T(2,128)(2,1)}, u32[]{:S(2)}, u32[]{:S(2)}) async-start(bf16[256,4,2,128]{3,2,1,0:T(2,128)(2,1)} %copy.68), calls=%async_computation | async-start | bytes 1048576 | tf_op jit(solution)/shard_map/all_to_all | solution.py:54
  56.6 35.2 %all-gather.7.cloned.1.call-start = ((), (), s32[]{:S(2)}) async-start(), calls=%async_computation.5 | async-start | bytes 3538944 | tf_op jit(solution)/shard_map/all_gather | solution.py:40
  67.9 3.9 %copy-start.10 = (s32[4]{0:T(128)S(1)}, s32[4]{0:T(128)}, u32[]{:S(2)}) copy-start(s32[4]{0:T(128)} %param.22) | copy-start | bytes 52
  69.4 3.3 %copy-start = (s32[512,512]{1,0:T(8,128)S(1)}, s32[512,512]{1,0:T(8,128)}, u32[]{:S(2)}) copy-start(s32[512,512]{1,0:T(8,128)} %iota_subtract_fusion) | copy-start | bytes 3145732
  85.7 1.3 copy-start.2
  90.5 6.5 %copy-start.11 = (s32[4]{0:T(128)S(1)}, s32[4]{0:T(128)}, u32[]{:S(2)}) copy-start(s32[4]{0:T(128)} %param.24) | copy-start | bytes 52
  108.8 1.8 %copy-start.8 = (pred[4,4]{1,0:T(4,128)(4,1)S(1)}, pred[4,4]{1,0:T(4,128)(4,1)}, u32[]{:S(2)}) copy-start(pred[4,4]{1,0:T(4,128)(4,1)} %and_bitcast_fusion) | copy-start | bytes 52
  110.3 33.4 %copy-start.3 = (bf16[16,2,8192]{2,1,0:T(2,128)(2,1)S(1)}, bf16[16,2,8192]{2,1,0:T(2,128)(2,1)}, u32[]{:S(2)}) copy-start(bf16[16,2,8192]{2,1,0:T(2,128)(2,1)} %param.15) | copy-start | bytes 1572868
  143.7 3.8 %copy-start.6 = (f32[8192]{0:T(1024)S(1)}, f32[8192]{0:T(1024)}, u32[]{:S(2)}) copy-start(f32[8192]{0:T(1024)} %param.25) | copy-start | bytes 98308
Sparse Core Ops, SparseCore 0:
  29.0 22.5 all-gather.4
  59.2 32.5 all-gather.6

commit v7 on v6

--- a/solution.py
+++ b/solution.py
@@ -38,7 +38,7 @@
 
     part_b = lax.all_to_all(b_cache, "tz", split_axis=1, concat_axis=1, tiled=True)
     shared_b = lax.all_gather(part_b, "txc", axis=2)
-    shared_b = shared_b.reshape(requests, cache_len, state_dim)
+    shared_b = shared_b.reshape(requests, n_tz, cache_len // n_tz, state_dim)
 
     sp = state_proj.reshape(n_mlp, requests, tok_blk, groups, 2 * state_dim)
     sp = sp.transpose(3, 0, 1, 2, 4).reshape(groups * n_mlp, requests, tok_blk, -1)
@@ -89,13 +89,16 @@
     in_window = (query_pos[:, :, None] - positions[None, None, :] < windows[:, None, None]) & live[
         :, None, :
     ]
-    score_old = jnp.einsum("rnk,rsk->rns", c_now, shared_b, preferred_element_type=jnp.float32)
+    score_old = jnp.einsum("rnk,rtqk->rntq", c_now, shared_b, preferred_element_type=jnp.float32)
+    score_old = score_old.reshape(requests, new_len, cache_len)
     probs_old = jnp.where(in_window, score_old, 0.0).astype(jnp.bfloat16)
     acc = jnp.einsum("rns,rsc->rnc", probs_old, x_pair, preferred_element_type=jnp.float32)
     old_out = acc.reshape(requests, new_len, heads_dev, head_dim)
     old_out = old_out * row_scale[..., None]
 
-    sink_b = jnp.take_along_axis(shared_b, sink_pos[:, :, None], axis=1)
+    per_tz = cache_len // n_tz
+    request_ids = jnp.arange(requests, dtype=jnp.int32)[:, None]
+    sink_b = shared_b[request_ids, sink_pos // per_tz, sink_pos % per_tz]
     sink_x = jnp.take_along_axis(x_cache, sink_pos[:, :, None], axis=1)
     sink_live = sink_pos < lengths[:, None]
     sink_gap = query_pos[:, :, None] - sink_pos[:, None, :]

time: 157 us -> 181 us (1.15)
  local copies, waits for them, and re-layouts: 26.6 us -> 41.2 us
  matrix products: 16.6 us -> 24 us
    reshape x2 -> x3, local copies, waits for them, and re-layouts: 1.85 us -> 17.2 us  [the longest x1 16.7 us: per_device(): score_old = score_old.reshape(requests, new_len, cache_len)]
    dot_general x0 -> x1, matrix products: none -> 8.28 us  [per_device(): jnp.einsum('rnk,rtqk->rntq', c_now, shared_b, preferred_element_type=jnp....]
    all_gather x1 -> x0, local copies, waits for them, and re-layouts: 3.93 us -> none  [per_device(): shared_b = lax.all_gather(part_b, 'txc', axis=2)]
    all_to_all x1, waiting for transfers between devices: 4.21 us -> 7.68 us  [per_device(): lax.all_to_all(b_cache, 'tz', split_axis=1, concat_axis=1, tiled=True)]
    transpose x0 -> x1, local copies, waits for them, and re-layouts: none -> 2.32 us  [per_device(): sp.reshape(n_tz, n_mlp, n_txc, requests, tok_blk, -1)]
    dot_general x1, matrix products: 11.8 us -> 9.85 us  [per_device(): jnp.einsum('rns,rsc->rnc', probs_old, x_pair, preferred_element_type=jnp....]
    unnamed x28 -> x24, local copies, waits for them, and re-layouts: 6.74 us -> 6.46 us
  transfers between devices with their start and end apart: 4 -> 4, of which waited for: 3 -> 1; matrix products, arithmetic and copies ran while one was open for 27% -> 26% of each run, Pallas kernels for 0% -> 0%
where the time goes in v7:
time: 181 us; the launch traced here: 180 us
  blocking collectives  54.7 us (30%)
  local copies, waits for them, and re-layouts  41.2 us (23%)
  other arithmetic  25.2 us (14%)
  matrix products  24 us (13%)
  starting transfers between devices  13.7 us (8%)
  between operations  13.7 us (8%)
  waiting for transfers between devices  7.74 us (4%)
    all_to_all x1, blocking collectives, per_device(): back = lax.all_to_all(back, ('tz', 'txc', 'mlp'), 0, 0, tiled=True)  33.4 us
    all_to_all x1, blocking collectives, per_device(): sp = lax.all_to_all(sp, ('tz', 'mlp'), 0, 0, tiled=True)  21.3 us
    reshape x1, local copies, waits for them, and re-layouts, per_device(): score_old = score_old.reshape(requests, new_len, cache_len)  16.7 us
    all_to_all x1, starting transfers between devices, per_device(): head_x = lax.all_to_all(x_part, ('tz', 'txc', 'mlp'), 0, 0, tiled=True)  10 us
    dot_general x1, matrix products, per_device(): jnp.einsum('rns,rsc->rnc', probs_old, x_pair, preferred_element_type=jnp....  9.85 us
    dot_general x1, matrix products, per_device(): jnp.einsum('rnk,rtqk->rntq', c_now, shared_b, preferred_element_type=jnp....  8.28 us
    all_to_all x1, waiting for transfers between devices, per_device(): lax.all_to_all(b_cache, 'tz', split_axis=1, concat_axis=1, tiled=True)  7.68 us
    unnamed x24, local copies, waits for them, and re-layouts  6.46 us
  transfers between devices with their start and end apart: 4, of which 1 were waited for; matrix products, arithmetic and copies ran while one was open for 26% of the time, Pallas kernels for 0%

profile of v7, /device:TPU:1, one launch (start us, length us, event | category | flops | bytes accessed | tf_op | source)
XLA Modules:
  0.0 180.1 jit_solution(2034234501252324521)
XLA Ops:
  6.5 1.0 copy.69
  7.6 21.3 %all_to_all.20 = bf16[32,4,2,256]{3,2,1,0:T(2,128)(2,1)} all-to-all(bf16[32,4,2,256]{3,2,1,0:T(2,128)(2,1)S(1)} %bitcast.87), channel_id=1, replica_groups=mesh['tz'=8,'txc'=8,'mlp'=4] {'tz','mlp'}, dimensions={0} | all-to-all | bytes 262144 | tf_op jit(solution)/shard_map/all_to_all | solution.py:45
  28.9 1.8 copy.75
  30.7 3.5 %all-to-all-start.2 = ((bf16[4,8,48,128]{3,2,0,1:T(8,128)(2,1)}), bf16[4,8,48,128]{3,2,0,1:T(8,128)(2,1)S(1)}, u32[]{:S(2)}, u32[]{:S(2)}) async-start(bf16[4,8,48,128]{3,2,0,1:T(8,128)(2,1)} %copy.75), calls=%async_computation.2 | async-start | bytes 786432 | tf_op jit(solution)/shard_map/all_to_all | solution.py:39
  34.1 0.7 exp.19
  34.8 1.4 reshape.180
  36.2 0.4 copy.65
  36.7 1.3 copy.66
  38.0 0.7 iota_compare_fusion
  38.7 7.7 %all-to-all-done.2 = bf16[4,8,48,128]{3,2,0,1:T(8,128)(2,1)S(1)} async-done(((bf16[4,8,48,128]{3,2,0,1:T(8,128)(2,1)}), bf16[4,8,48,128]{3,2,0,1:T(8,128)(2,1)S(1)}, u32[]{:S(2)}, u32[]{:S(2)}) %all-to-all-start.2) | async-done | bytes 393248 | tf_op jit(solution)/shard_map/all_to_all | solution.py:39
  46.4 10.0 %all-to-all-start = ((bf16[256,4,2,128]{3,2,1,0:T(2,128)(2,1)}), bf16[256,4,2,128]{3,2,1,0:T(2,128)(2,1)}, u32[]{:S(2)}, u32[]{:S(2)}) async-start(bf16[256,4,2,128]{3,2,1,0:T(2,128)(2,1)} %copy.66), calls=%async_computation | async-start | bytes 1048576 | tf_op jit(solution)/shard_map/all_to_all | solution.py:54
  56.4 0.2 all-gather.7.cloned.1.call-start
  56.6 0.8 copy.76
  57.4 0.1 negate_bitcast_fusion
  57.5 2.4 %reduce-window.14 = f32[4,2,4,128]{3,2,1,0:T(4,128)S(1)} reduce-window(f32[4,2,4,128]{3,2,1,0:T(4,128)S(1)} %reshape.186, f32[]{:T(128)} %constant.35.clone.1), window={size=1x1x1x128 pad=0_0x0_0x0_0x127_0}, to_apply=%region_0.0 | reduce-window | flops 520192 | bytes 32772 | tf_op jit(solution)/shard_map/reduce-window
  60.0 0.2 slice_reduce_fusion.1
  60.1 0.7 reduce-window.15
  60.9 0.1 reshape.188
  61.0 2.3 %reduce-window.16 = f32[4,2,24,128]{3,2,1,0:T(8,128)S(1)} reduce-window(f32[4,2,24,128]{3,2,1,0:T(8,128)S(1)} %reshape.188, f32[]{:T(128)} %constant.35.clone.1), window={size=1x1x1x128 pad=0_0x0_0x0_0x127_0}, to_apply=%region_2.3 | reduce-window | flops 3121152 | bytes 196612 | tf_op jit(solution)/shard_map/reduce-window.2
  63.3 0.2 slice_reduce_fusion
  63.5 0.8 reduce-window.19
  64.3 0.1 broadcast_add_fusion
  64.6 0.1 copy.84
  64.7 0.1 copy.74
  64.8 1.2 iota_subtract_fusion
  65.9 0.1 broadcast_add_fusion.1
  66.0 0.1 exponential_bitcast_fusion
  66.1 0.1 broadcast_compare_fusion
  66.2 1.4 copy.68
  67.6 0.1 reshape.204
  67.7 0.1 reshape.198
  67.8 3.2 %copy.72 = bf16[4,3072,128]{1,2,0:T(8,128)(2,1)S(1)} copy(bf16[4,3072,128]{2,1,0:T(8,128)(2,1)} %param.17) | data formatting | bytes 6291456 | tf_op args[5]
  70.9 2.0 %gather_fusion.1 = bf16[16,128]{1,0:T(8,128)(2,1)} fusion(bf16[4,3072,128]{2,1,0:T(8,128)(2,1)} %param.17, s32[16]{0:T(128)S(1)} %reshape.204), kind=kCustom, calls=%fused_computation.1 | custom fusion | bytes 8320 | tf_op jit(solution)/shard_map/jit(take_along_axis)/gather | solution.py:102
  73.0 2.5 %fusion.3 = bf16[4,3072,128]{1,2,0:T(8,128)(2,1)} fusion(bf16[4,3072,128]{1,2,0:T(8,128)(2,1)S(1)} %copy.72, f32[4,3072,2]{1,2,0:T(2,128)S(1)} %exponential_bitcast_fusion), kind=kLoop, calls=%fused_computation.9 | loop fusion | flops 4718592 | bytes 6389760 | tf_op jit(solution)/shard_map/convert_element_type | solution.py:74
  75.5 0.8 compare_and_fusion.1
  76.3 0.7 iota_add_fusion
  77.0 2.5 %compare_and_fusion = pred[4,512,512]{2,1,0:T(8,128)(4,1)} fusion(s32[512,512]{1,0:T(8,128)S(1)} %copy-done, s32[4]{0:T(128)} %param.22, pred[512,512]{1,0:T(8,128)(4,1)S(1)} %broadcast_compare_fusion), kind=kLoop, calls=%fused_computation.12 | loop fusion | flops 2097152 | bytes 2359312 | tf_op jit(solution)/shard_map/and | solution.py:79
  79.5 1.4 convert_bitcast_fusion
  80.9 0.4 copy.67
  81.3 1.9 %reshape.197 = f32[4,512,2,64]{3,2,1,0:T(2,128)S(1)} reshape(f32[4,256,2,128]{3,2,1,0:T(2,128)S(1)} %copy.67) | data formatting | bytes 2097152 | tf_op jit(solution)/shard_map/convert_element_type | solution.py:59
  83.2 5.4 %multiply_convert_fusion.2 = bf16[4,512,2,64]{3,2,1,0:T(2,128)(2,1)} fusion(f32[4,512,2,64]{3,2,1,0:T(2,128)S(1)} %reshape.197, f32[4,512,2]{2,1,0:T(8,128)} %copy.68), kind=kLoop, calls=%fused_computation.13 | loop fusion | flops 524288 | bytes 1589248 | tf_op jit(solution)/shard_map/convert_element_type | solution.py:60
  88.5 2.3 %copy.70 = bf16[4,8,8,4,2,256]{5,4,3,2,1,0:T(2,128)(2,1)S(1)} copy(bf16[4,8,8,4,2,256]{5,4,0,2,3,1:T(2,128)(2,1)} %bitcast.86) | data formatting | bytes 2097152 | tf_op jit(solution)/shard_map/transpose | solution.py:47
  90.9 0.4 reshape.185
  91.3 0.7 fusion.14
  92.0 4.6 %fusion.6 = f32[4,512,2,64]{1,3,2,0:T(8,128)S(1)} fusion(f32[4,2,512]{2,1,0:T(2,128)S(1)} %reduce_window_sum.39, f32[4,512,512]{2,1,0:T(8,128)S(1)} %fusion.14, pred[4,512,512]{2,1,0:T(8,128)(4,1)S(1)} %copy-done.1, bf16[4,512,2,64]{3,2,1,0:T(2,128)(2,1)} %multiply_convert_fusion.2), kind=kOutput, calls=%fused_computation.14 | convolution fusion | flops 278921216 | bytes 6832128 | tf_op jit(solution)/shard_map/rhnj,rjhd->rnhd/dot_general | solution.py:84
  96.7 8.3 %fusion.16 = bf16[4,8,384,512]{3,2,1,0:T(8,128)(2,1)} fusion(bf16[4,8,384,128]{3,2,1,0:T(8,128)(2,1)} %all-gather.7.cloned.1.call-done, bf16[4,512,256]{2,1,0:T(8,128)(2,1)S(1)} %reshape.185), kind=kOutput, calls=%fused_computation.32 | convolution fusion | flops 1610612736 | bytes 16252928 | tf_op jit(solution)/shard_map/rnk,rtqk->rntq/dot_general | solution.py:92
  104.9 1.3 gather_fusion
  106.3 16.7 %copy.77 = bf16[4,512,3072]{2,1,0:T(8,128)(2,1)} copy(bf16[4,512,3072]{1,2,0:T(8,128)(2,1)} %bitcast.79) | data formatting | bytes 25165824 | tf_op jit(solution)/shard_map/reshape | solution.py:93
  123.0 9.8 %fusion.1 = f32[4,512,128]{1,2,0:T(8,128)S(1)} fusion(bf16[4,3072,128]{1,2,0:T(8,128)(2,1)} %fusion.3, bf16[4,512,3072]{2,1,0:T(8,128)(2,1)} %copy.77, s32[4]{0:T(128)S(1)} %copy-done.9, s32[4,512]{1,0:T(4,128)S(1)} %iota_add_fusion, pred[4,3072]{1,0:T(4,128)(4,1)S(1)} %iota_compare_fusion), kind=kOutput, calls=%fused_computation.5 | convolution fusion | flops 1635778560 | bytes 16797712 | tf_op jit(solution)/shard_map/rns,rsc->rnc/dot_general | solution.py:95
  132.8 0.2 multiply_add_fusion
  133.1 0.3 copy.78
  133.5 0.6 fusion.7
  134.0 0.4 copy.88
  134.4 33.4 %all_to_all.21 = bf16[256,4,2,128]{3,2,1,0:T(2,128)(2,1)S(1)} all-to-all(bf16[256,4,2,128]{3,2,1,0:T(2,128)(2,1)S(1)} %bitcast.83), channel_id=1, replica_groups=mesh['tz'=8,'txc'=8,'mlp'=4] {'tz','txc','mlp'}, dimensions={0} | all-to-all | bytes 1048576 | tf_op jit(solution)/shard_map/all_to_all | solution.py:114
  167.8 0.2 copy.80
  168.0 0.1 reshape.196
  168.1 1.5 fusion.46
  169.6 0.9 mul.89
  170.5 0.2 reduce_sum.9
  170.7 0.1 copy.81
  170.8 0.1 copy.82
  170.8 0.1 mul.90
  171.0 0.9 mul.91
  171.9 1.4 multiply_convert_fusion.5
  (34 shorter events, 0.4 us)
Async XLA Ops:
  6.5 50.9 %copy-start.4 = (f32[4,512,2]{1,2,0:T(2,128)S(1)}, f32[4,512,2]{1,2,0:T(2,128)}, u32[]{:S(2)}) copy-start(f32[4,512,2]{1,2,0:T(2,128)} %param.15) | copy-start | bytes 49156
  6.5 54.3 %copy-start.3 = (f32[4,2,3072]{2,1,0:T(2,128)S(1)}, f32[4,2,3072]{2,1,0:T(2,128)}, u32[]{:S(2)}) copy-start(f32[4,2,3072]{2,1,0:T(2,128)} %param.19) | copy-start | bytes 294916
  6.5 59.4 %copy-start.6 = (s32[4,4]{1,0:T(4,128)S(1)}, s32[4,4]{1,0:T(4,128)}, u32[]{:S(2)}) copy-start(s32[4,4]{1,0:T(4,128)} %param.21) | copy-start | bytes 196
  6.5 82.0 %all-gather.5.cloned.1.call-start = ((), (), s32[]{:S(2)}) async-start(), calls=%async_computation.4 | async-start | bytes 1179648 | tf_op jit(solution)/shard_map/all_gather | solution.py:46
  30.7 15.7 %all-to-all-start.2 = ((bf16[4,8,48,128]{3,2,0,1:T(8,128)(2,1)}), bf16[4,8,48,128]{3,2,0,1:T(8,128)(2,1)S(1)}, u32[]{:S(2)}, u32[]{:S(2)}) async-start(bf16[4,8,48,128]{3,2,0,1:T(8,128)(2,1)} %copy.75), calls=%async_computation.2 | async-start | bytes 786432 | tf_op jit(solution)/shard_map/all_to_all | solution.py:39
  46.4 33.1 %all-to-all-start = ((bf16[256,4,2,128]{3,2,1,0:T(2,128)(2,1)}), bf16[256,4,2,128]{3,2,1,0:T(2,128)(2,1)}, u32[]{:S(2)}, u32[]{:S(2)}) async-start(bf16[256,4,2,128]{3,2,1,0:T(2,128)(2,1)} %copy.66), calls=%async_computation | async-start | bytes 1048576 | tf_op jit(solution)/shard_map/all_to_all | solution.py:54
  56.4 40.2 %all-gather.7.cloned.1.call-start = ((), (), s32[]{:S(2)}) async-start(), calls=%async_computation.5 | async-start | bytes 3538944 | tf_op jit(solution)/shard_map/all_gather | solution.py:40
  73.0 4.0 %copy-start = (s32[512,512]{1,0:T(8,128)S(1)}, s32[512,512]{1,0:T(8,128)}, u32[]{:S(2)}) copy-start(s32[512,512]{1,0:T(8,128)} %iota_subtract_fusion) | copy-start | bytes 3145732
  83.1 8.9 %copy-start.1 = (pred[4,512,512]{2,1,0:T(8,128)(4,1)S(1)}, pred[4,512,512]{2,1,0:T(8,128)(4,1)}, u32[]{:S(2)}) copy-start(pred[4,512,512]{2,1,0:T(8,128)(4,1)} %compare_and_fusion) | copy-start | bytes 3145732
  106.3 16.7 %copy-start.9 = (s32[4]{0:T(128)S(1)}, s32[4]{0:T(128)}, u32[]{:S(2)}) copy-start(s32[4]{0:T(128)} %param.22) | copy-start | bytes 52
  123.0 10.5 %copy-start.7 = (s32[4,4]{1,0:T(4,128)S(1)}, s32[4,4]{1,0:T(4,128)}, u32[]{:S(2)}) copy-start(s32[4,4]{1,0:T(4,128)} %param.21) | copy-start | bytes 196
  123.0 10.5 %copy-start.8 = (bf16[16,128]{1,0:T(8,128)(2,1)S(1)}, bf16[16,128]{1,0:T(8,128)(2,1)}, u32[]{:S(2)}) copy-start(bf16[16,128]{1,0:T(8,128)(2,1)} %gather_fusion.1) | copy-start | bytes 12292
  133.4 34.7 %copy-start.2 = (bf16[16,2,8192]{2,1,0:T(2,128)(2,1)S(1)}, bf16[16,2,8192]{2,1,0:T(2,128)(2,1)}, u32[]{:S(2)}) copy-start(bf16[16,2,8192]{2,1,0:T(2,128)(2,1)} %param.13) | copy-start | bytes 1572868
  134.4 37.5 %copy-start.5 = (f32[8192]{0:T(1024)S(1)}, f32[8192]{0:T(1024)}, u32[]{:S(2)}) copy-start(f32[8192]{0:T(1024)} %param.23) | copy-start | bytes 98308
Sparse Core Ops, SparseCore 0:
  29.0 22.5 all-gather.4
  59.1 32.4 all-gather.6

commit v8 on v6

--- a/solution.py
+++ b/solution.py
@@ -5,6 +5,7 @@
 
 EPS = 1e-05
 GROUPS = 8
+WINDOW_LIMIT = 2048
 
 
 def per_device(
@@ -86,12 +87,18 @@
 
     new_out, x_pair, shared_b = lax.optimization_barrier((new_out, x_pair, shared_b))
 
-    in_window = (query_pos[:, :, None] - positions[None, None, :] < windows[:, None, None]) & live[
-        :, None, :
-    ]
-    score_old = jnp.einsum("rnk,rsk->rns", c_now, shared_b, preferred_element_type=jnp.float32)
+    win = min(WINDOW_LIMIT, cache_len)
+    start = jnp.clip(lengths - win, 0, cache_len - win)
+    take = jax.vmap(lambda a, at: lax.dynamic_slice_in_dim(a, at, win, 0))
+    b_win = take(shared_b, start)
+    x_win = take(x_pair, start)
+    pos_win = start[:, None] + jnp.arange(win, dtype=jnp.int32)[None, :]
+    in_window = (query_pos[:, :, None] - pos_win[:, None, :] < windows[:, None, None]) & (
+        pos_win < lengths[:, None]
+    )[:, None, :]
+    score_old = jnp.einsum("rnk,rsk->rns", c_now, b_win, preferred_element_type=jnp.float32)
     probs_old = jnp.where(in_window, score_old, 0.0).astype(jnp.bfloat16)
-    acc = jnp.einsum("rns,rsc->rnc", probs_old, x_pair, preferred_element_type=jnp.float32)
+    acc = jnp.einsum("rns,rsc->rnc", probs_old, x_win, preferred_element_type=jnp.float32)
     old_out = acc.reshape(requests, new_len, heads_dev, head_dim)
     old_out = old_out * row_scale[..., None]
 

time: 157 us -> 190 us (1.21)
  local copies, waits for them, and re-layouts: 26.6 us -> 57.3 us
  blocking collectives: 53 us -> 31.1 us
  starting transfers between devices: 13.8 us -> 30 us
  waiting for transfers between devices: 6.45 us -> 16.3 us
  matrix products: 16.6 us -> 14.1 us
    gather x0 -> x32, local copies, waits for them, and re-layouts: none -> 28.9 us
    all_to_all x1 -> x0, blocking collectives: 21.3 us -> none  [per_device(): sp = lax.all_to_all(sp, ('tz', 'mlp'), 0, 0, tiled=True)]
    all_to_all x0 -> x1, starting transfers between devices: none -> 12 us  [per_device(): sp = lax.all_to_all(sp, ('tz', 'mlp'), 0, 0, tiled=True)]
    all_to_all x0 -> x1, waiting for transfers between devices: none -> 7.55 us  [per_device(): sp = lax.all_to_all(sp, ('tz', 'mlp'), 0, 0, tiled=True)]
    all_to_all x1, waiting for transfers between devices: 0.48 us -> 6.63 us  [per_device(): head_x = lax.all_to_all(x_part, ('tz', 'txc', 'mlp'), 0, 0, tiled=True)]
    all_to_all x1, waiting for transfers between devices: 4.21 us -> 0.01 us  [per_device(): lax.all_to_all(b_cache, 'tz', split_axis=1, concat_axis=1, tiled=True)]
    all_to_all x1, starting transfers between devices: 10 us -> 14.1 us  [per_device(): head_x = lax.all_to_all(x_part, ('tz', 'txc', 'mlp'), 0, 0, tiled=True)]
    dot_general x1, matrix products: 11.8 us -> 8.54 us  [per_device(): jnp.einsum('rns,rsc->rnc', probs_old, x_win, preferred_element_type=jnp.f...]
  transfers between devices with their start and end apart: 4 -> 5, of which waited for: 3 -> 3; matrix products, arithmetic and copies ran while one was open for 27% -> 22% of each run, Pallas kernels for 0% -> 0%
where the time goes in v8:
time: 190 us; the launch traced here: 188 us
  local copies, waits for them, and re-layouts  57.3 us (30%)
  blocking collectives  31.1 us (16%)
  starting transfers between devices  30 us (16%)
  other arithmetic  25.3 us (13%)
  waiting for transfers between devices  16.3 us (9%)
  matrix products  14.1 us (7%)
  between operations  13.8 us (7%)
    all_to_all x1, blocking collectives, per_device(): back = lax.all_to_all(back, ('tz', 'txc', 'mlp'), 0, 0, tiled=True)  31.1 us
    gather x32, local copies, waits for them, and re-layouts  28.9 us
    all_to_all x1, starting transfers between devices, per_device(): head_x = lax.all_to_all(x_part, ('tz', 'txc', 'mlp'), 0, 0, tiled=True)  14.1 us
    all_to_all x1, starting transfers between devices, per_device(): sp = lax.all_to_all(sp, ('tz', 'mlp'), 0, 0, tiled=True)  12 us
    unnamed x30, local copies, waits for them, and re-layouts  9.05 us
    dot_general x1, matrix products, per_device(): jnp.einsum('rns,rsc->rnc', probs_old, x_win, preferred_element_type=jnp.f...  8.54 us
    all_to_all x1, waiting for transfers between devices, per_device(): sp = lax.all_to_all(sp, ('tz', 'mlp'), 0, 0, tiled=True)  7.55 us
    another operation x6, other arithmetic  7.01 us
  transfers between devices with their start and end apart: 5, of which 3 were waited for; matrix products, arithmetic and copies ran while one was open for 22% of the time, Pallas kernels for 0%

profile of v8, /device:TPU:1, one launch (start us, length us, event | category | flops | bytes accessed | tf_op | source)
XLA Modules:
  0.0 188.2 jit_solution(4647413509885531617)
XLA Ops:
  6.5 1.7 copy.85
  8.3 12.0 %all-to-all-start.1 = ((bf16[32,4,2,256]{3,2,1,0:T(2,128)(2,1)}), bf16[32,4,2,256]{3,2,1,0:T(2,128)(2,1)S(1)}, u32[]{:S(2)}, u32[]{:S(2)}) async-start(bf16[32,4,2,256]{3,2,1,0:T(2,128)(2,1)} %bitcast.5), calls=%async_computation.1 | async-start | bytes 262144 | tf_op jit(solution)/shard_map/all_to_all | solution.py:46
  20.3 1.8 copy.93
  22.1 7.6 %all-to-all-done.1 = bf16[32,4,2,256]{3,2,1,0:T(2,128)(2,1)S(1)} async-done(((bf16[32,4,2,256]{3,2,1,0:T(2,128)(2,1)}), bf16[32,4,2,256]{3,2,1,0:T(2,128)(2,1)S(1)}, u32[]{:S(2)}, u32[]{:S(2)}) %all-to-all-start.1) | async-done | bytes 131104 | tf_op jit(solution)/shard_map/all_to_all | solution.py:46
  29.6 3.6 %all-to-all-start.2 = ((bf16[4,8,48,128]{3,2,0,1:T(8,128)(2,1)}), bf16[4,8,48,128]{3,2,0,1:T(8,128)(2,1)S(1)}, u32[]{:S(2)}, u32[]{:S(2)}) async-start(bf16[4,8,48,128]{3,2,0,1:T(8,128)(2,1)} %copy.93), calls=%async_computation.2 | async-start | bytes 786432 | tf_op jit(solution)/shard_map/all_to_all | solution.py:40
  33.3 0.7 all-gather.5.cloned.1.call-update
  34.0 0.7 iota_compare_fusion
  34.7 0.7 exp.19
  35.4 0.8 negate_bitcast_fusion
  36.2 1.0 broadcast_select_fusion
  37.3 2.4 %reduce-window.14 = f32[4,2,4,128]{3,2,1,0:T(4,128)S(1)} reduce-window(f32[4,2,4,128]{3,2,1,0:T(4,128)S(1)} %reshape.214, f32[]{:T(128)} %constant.19.clone.1), window={size=1x1x1x128 pad=0_0x0_0x0_0x127_0}, to_apply=%region_0.0 | reduce-window | flops 520192 | bytes 32772 | tf_op jit(solution)/shard_map/reduce-window
  39.7 2.3 %reduce-window.16 = f32[4,2,24,128]{3,2,1,0:T(8,128)S(1)} reduce-window(f32[4,2,24,128]{3,2,1,0:T(8,128)S(1)} %reshape.216, f32[]{:T(128)} %constant.19.clone.1), window={size=1x1x1x128 pad=0_0x0_0x0_0x127_0}, to_apply=%region_2.3 | reduce-window | flops 3121152 | bytes 196612 | tf_op jit(solution)/shard_map/reduce-window.2
  42.3 0.7 reduce-window.15
  43.9 1.3 copy.82
  45.2 0.8 reduce-window.19
  46.0 0.7 broadcast_add_fusion
  46.8 14.1 %all-to-all-start = ((bf16[256,4,2,128]{3,2,1,0:T(2,128)(2,1)}), bf16[256,4,2,128]{3,2,1,0:T(2,128)(2,1)}, u32[]{:S(2)}, u32[]{:S(2)}) async-start(bf16[256,4,2,128]{3,2,1,0:T(2,128)(2,1)} %copy.82), calls=%async_computation | async-start | bytes 1048576 | tf_op jit(solution)/shard_map/all_to_all | solution.py:55
  61.2 0.5 all-gather.7.cloned.1.call-update
  61.7 1.4 copy.84
  63.2 3.2 %copy.90 = bf16[4,3072,128]{1,2,0:T(8,128)(2,1)S(1)} copy(bf16[4,3072,128]{2,1,0:T(8,128)(2,1)} %param.19) | data formatting | bytes 6291456 | tf_op args[5]
  66.9 1.4 gather_fusion.1
  68.5 2.5 %fusion.5 = bf16[4,3072,128]{1,2,0:T(8,128)(2,1)} fusion(bf16[4,3072,128]{1,2,0:T(8,128)(2,1)S(1)} %copy.90, f32[4,3072,2]{1,2,0:T(2,128)S(1)} %exponential_bitcast_fusion), kind=kLoop, calls=%fused_computation.15 | loop fusion | flops 4718592 | bytes 6389760 | tf_op jit(solution)/shard_map/convert_element_type | solution.py:75
  71.3 1.8 compare_and_fusion
  73.3 6.6 %all-to-all-done = bf16[256,4,2,128]{3,2,1,0:T(2,128)(2,1)} async-done(((bf16[256,4,2,128]{3,2,1,0:T(2,128)(2,1)}), bf16[256,4,2,128]{3,2,1,0:T(2,128)(2,1)}, u32[]{:S(2)}, u32[]{:S(2)}) %all-to-all-start) | async-done | bytes 524320 | tf_op jit(solution)/shard_map/all_to_all | solution.py:55
  79.9 1.4 convert_bitcast_fusion
  81.7 1.9 reshape.270
  83.5 4.7 %multiply_convert_fusion.2 = bf16[4,512,2,64]{3,2,1,0:T(2,128)(2,1)S(1)} fusion(f32[4,512,2,64]{3,2,1,0:T(2,128)S(1)} %reshape.270, f32[4,512,2]{2,1,0:T(8,128)} %copy.84), kind=kLoop, calls=%fused_computation.20 | loop fusion | flops 524288 | bytes 1589248 | tf_op jit(solution)/shard_map/convert_element_type | solution.py:61
  88.3 1.8 copy.86
  90.4 0.7 fusion.18
  91.7 4.2 %fusion.10 = f32[4,512,2,64]{1,3,2,0:T(8,128)} fusion(f32[4,2,512]{2,1,0:T(2,128)S(1)} %reduce_window_sum.39, f32[4,512,512]{2,1,0:T(8,128)S(1)} %fusion.18, pred[4,512,512]{2,1,0:T(8,128)(4,1)S(1)} %copy-done.1, bf16[4,512,2,64]{3,2,1,0:T(2,128)(2,1)S(1)} %multiply_convert_fusion.2), kind=kOutput, calls=%fused_computation.21 | convolution fusion | flops 278921216 | bytes 6832128 | tf_op jit(solution)/shard_map/rhnj,rjhd->rnhd/dot_general | solution.py:85
  95.9 0.9 all-gather.7.cloned.1.call-done
  96.7 3.9 %copy.94 = bf16[4,8,384,128]{3,2,1,0:T(8,128)(2,1)} copy(bf16[4,8,384,128]{3,2,0,1:T(8,128)(2,1)} %all-gather.7.cloned.1.call-done) | data formatting | bytes 6291456 | tf_op jit(solution)/shard_map/all_gather | solution.py:41
  100.6 1.6 broadcast.132.clone
  102.2 16.8 %while.3 = (s32[]{:T(128)}, bf16[4,3072,128]{1,2,0:T(8,128)(2,1)}, s32[4,3]{1,0:T(4,128)S(1)}, bf16[4,2048,128]{2,1,0:T(8,128)(2,1)}, s32[]{:T(128)}) while((s32[]{:T(128)}, bf16[4,3072,128]{1,2,0:T(8,128)(2,1)}, s32[4,3]{1,0:T(4,128)S(1)}, bf16[4,2048,128]{2,1,0:T(8,128)(2,1)}, s32[]{:T(128)}) %tuple.49), condition=%wide.while_cond.1, body=%wide.while_body.1.sunk | while | flops 2 | bytes 3145853 | solution.py:92
  102.2 0.6 fusion.56
  102.8 2.5 %constant_dynamic-slice_fusion.8 = bf16[1,2048,128]{1,2,0:T(8,128)(2,1)S(1)} fusion(bf16[4,3072,128]{1,2,0:T(8,128)(2,1)} %get-tuple-element.163, s32[]{:T(128)} %bitcast.84, s32[]{:T(128)} %bitcast.85), kind=kLoop, calls=%fused_computation.5.clone.1 | loop fusion | bytes 1048584 | tf_op jit(solution)/shard_map/vmap()/gather
  105.6 0.9 constant_dynamic-update-slice_fusion.2
  106.5 0.6 fusion.56
  107.0 2.5 %constant_dynamic-slice_fusion.8 = bf16[1,2048,128]{1,2,0:T(8,128)(2,1)S(1)} fusion(bf16[4,3072,128]{1,2,0:T(8,128)(2,1)} %get-tuple-element.163, s32[]{:T(128)} %bitcast.84, s32[]{:T(128)} %bitcast.85), kind=kLoop, calls=%fused_computation.5.clone.1 | loop fusion | bytes 1048584 | tf_op jit(solution)/shard_map/vmap()/gather
  109.8 0.8 constant_dynamic-update-slice_fusion.2
  110.7 0.6 fusion.56
  111.2 2.5 %constant_dynamic-slice_fusion.8 = bf16[1,2048,128]{1,2,0:T(8,128)(2,1)S(1)} fusion(bf16[4,3072,128]{1,2,0:T(8,128)(2,1)} %get-tuple-element.163, s32[]{:T(128)} %bitcast.84, s32[]{:T(128)} %bitcast.85), kind=kLoop, calls=%fused_computation.5.clone.1 | loop fusion | bytes 1048584 | tf_op jit(solution)/shard_map/vmap()/gather
  114.0 0.8 constant_dynamic-update-slice_fusion.2
  114.8 0.6 fusion.56
  115.4 2.5 %constant_dynamic-slice_fusion.8 = bf16[1,2048,128]{1,2,0:T(8,128)(2,1)S(1)} fusion(bf16[4,3072,128]{1,2,0:T(8,128)(2,1)} %get-tuple-element.163, s32[]{:T(128)} %bitcast.84, s32[]{:T(128)} %bitcast.85), kind=kLoop, calls=%fused_computation.5.clone.1 | loop fusion | bytes 1048584 | tf_op jit(solution)/shard_map/vmap()/gather
  118.2 0.9 constant_dynamic-update-slice_fusion.2
  119.1 1.3 gather_fusion
  120.7 12.4 %while.2 = (s32[]{:T(128)}, bf16[4,3072,128]{2,1,0:T(8,128)(2,1)}, s32[4,3]{1,0:T(4,128)S(1)}, bf16[4,2048,128]{2,1,0:T(8,128)(2,1)S(1)}, s32[]{:T(128)}) while((s32[]{:T(128)}, bf16[4,3072,128]{2,1,0:T(8,128)(2,1)}, s32[4,3]{1,0:T(4,128)S(1)}, bf16[4,2048,128]{2,1,0:T(8,128)(2,1)S(1)}, s32[]{:T(128)}) %tuple.60), condition=%wide.while_cond, body=%wide.while_body.sunk | while | flops 2 | bytes 1048701 | solution.py:92
  120.7 0.6 fusion.55
  121.3 2.4 %dynamic-slice_dynamic-update-slice_fusion.2 = bf16[4,2048,128]{2,1,0:T(8,128)(2,1)S(1)} fusion(bf16[4,2048,128]{2,1,0:T(8,128)(2,1)S(1)} %get-tuple-element.175, s32[]{:T(128)S(6)} %copy.137, bf16[4,3072,128]{2,1,0:T(8,128)(2,1)} %get-tuple-element.178, s32[]{:T(128)} %bitcast.82, s32[]{:T(128)} %bitcast.83), kind=kLoop, calls=%fused_computation.2.clone.1 | loop fusion | bytes 1048588 | tf_op jit(solution)/shard_map/vmap()/gather
  123.7 0.6 fusion.55
  124.3 2.4 %dynamic-slice_dynamic-update-slice_fusion.2 = bf16[4,2048,128]{2,1,0:T(8,128)(2,1)S(1)} fusion(bf16[4,2048,128]{2,1,0:T(8,128)(2,1)S(1)} %get-tuple-element.175, s32[]{:T(128)S(6)} %copy.137, bf16[4,3072,128]{2,1,0:T(8,128)(2,1)} %get-tuple-element.178, s32[]{:T(128)} %bitcast.82, s32[]{:T(128)} %bitcast.83), kind=kLoop, calls=%fused_computation.2.clone.1 | loop fusion | bytes 1048588 | tf_op jit(solution)/shard_map/vmap()/gather
  126.8 0.6 fusion.55
  127.4 2.4 %dynamic-slice_dynamic-update-slice_fusion.2 = bf16[4,2048,128]{2,1,0:T(8,128)(2,1)S(1)} fusion(bf16[4,2048,128]{2,1,0:T(8,128)(2,1)S(1)} %get-tuple-element.175, s32[]{:T(128)S(6)} %copy.137, bf16[4,3072,128]{2,1,0:T(8,128)(2,1)} %get-tuple-element.178, s32[]{:T(128)} %bitcast.82, s32[]{:T(128)} %bitcast.83), kind=kLoop, calls=%fused_computation.2.clone.1 | loop fusion | bytes 1048588 | tf_op jit(solution)/shard_map/vmap()/gather
  129.8 0.6 fusion.55
  130.4 2.4 %dynamic-slice_dynamic-update-slice_fusion.2 = bf16[4,2048,128]{2,1,0:T(8,128)(2,1)S(1)} fusion(bf16[4,2048,128]{2,1,0:T(8,128)(2,1)S(1)} %get-tuple-element.175, s32[]{:T(128)S(6)} %copy.137, bf16[4,3072,128]{2,1,0:T(8,128)(2,1)} %get-tuple-element.178, s32[]{:T(128)} %bitcast.82, s32[]{:T(128)} %bitcast.83), kind=kLoop, calls=%fused_computation.2.clone.1 | loop fusion | bytes 1048588 | tf_op jit(solution)/shard_map/vmap()/gather
  133.1 8.5 %fusion.2 = f32[4,512,128]{1,2,0:T(8,128)} fusion(bf16[4,2048,128]{2,1,0:T(8,128)(2,1)} %get-tuple-element.27, s32[4]{0:T(128)S(1)} %copy-done.10, s32[4,2048]{1,0:T(4,128)S(1)} %iota_add_fusion, s32[4,512]{1,0:T(4,128)S(1)} %iota_add_fusion.1, pred[4,2048]{1,0:T(4,128)(4,1)S(1)} %broadcast_compare_fusion.1, ...), kind=kOutput, calls=%fused_computation.12 | convolution fusion | flops 2168455168 | bytes 5816336 | tf_op jit(solution)/shard_map/rns,rsc->rnc/dot_general | solution.py:101
  141.6 1.8 multiply_add_fusion
  143.8 0.6 fusion.11
  144.8 31.1 %all_to_all.20 = bf16[256,4,2,128]{3,2,1,0:T(2,128)(2,1)S(1)} all-to-all(bf16[256,4,2,128]{3,2,1,0:T(2,128)(2,1)S(1)} %bitcast.91), channel_id=1, replica_groups=mesh['tz'=8,'txc'=8,'mlp'=4] {'tz','txc','mlp'}, dimensions={0} | all-to-all | bytes 1048576 | tf_op jit(solution)/shard_map/all_to_all | solution.py:118
  176.2 1.5 fusion.46
  177.7 0.9 mul.89
  179.1 0.9 mul.91
  180.0 1.4 multiply_convert_fusion.5
  (77 shorter events, 7.0 us)
Async XLA Ops:
  6.5 39.4 %copy-start.9 = (s32[4]{0:T(128)S(1)}, s32[4]{0:T(128)}, u32[]{:S(2)}) copy-start(s32[4]{0:T(128)} %param.22) | copy-start | bytes 52
  6.5 36.5 %copy-start.2 = (bf16[16,2,8192]{2,1,0:T(2,128)(2,1)S(1)}, bf16[16,2,8192]{2,1,0:T(2,128)(2,1)}, u32[]{:S(2)}) copy-start(bf16[16,2,8192]{2,1,0:T(2,128)(2,1)} %param.14) | copy-start | bytes 1572868
  8.3 21.4 %all-to-all-start.1 = ((bf16[32,4,2,256]{3,2,1,0:T(2,128)(2,1)}), bf16[32,4,2,256]{3,2,1,0:T(2,128)(2,1)S(1)}, u32[]{:S(2)}, u32[]{:S(2)}) async-start(bf16[32,4,2,256]{3,2,1,0:T(2,128)(2,1)} %bitcast.5), calls=%async_computation.1 | async-start | bytes 262144 | tf_op jit(solution)/shard_map/all_to_all | solution.py:46
  29.6 3.6 %copy-start.3 = (bf16[32,4,2,256]{3,2,1,0:T(2,128)(2,1)}, bf16[32,4,2,256]{3,2,1,0:T(2,128)(2,1)S(1)}, u32[]{:S(2)}) copy-start(bf16[32,4,2,256]{3,2,1,0:T(2,128)(2,1)S(1)} %all-to-all-done.1) | copy-start | bytes 393220
  29.6 32.1 %copy-start.6 = (f32[4,512,2]{1,2,0:T(2,128)S(1)}, f32[4,512,2]{1,2,0:T(2,128)}, u32[]{:S(2)}) copy-start(f32[4,512,2]{1,2,0:T(2,128)} %param.17) | copy-start | bytes 49156
  29.6 17.2 %all-to-all-start.2 = ((bf16[4,8,48,128]{3,2,0,1:T(8,128)(2,1)}), bf16[4,8,48,128]{3,2,0,1:T(8,128)(2,1)S(1)}, u32[]{:S(2)}, u32[]{:S(2)}) async-start(bf16[4,8,48,128]{3,2,0,1:T(8,128)(2,1)} %copy.93), calls=%async_computation.2 | async-start | bytes 786432 | tf_op jit(solution)/shard_map/all_to_all | solution.py:40
  33.2 55.0 %all-gather.5.cloned.1.call-start = ((), (), s32[]{:S(2)}) async-start(), calls=%async_computation.4 | async-start | bytes 1179648 | tf_op jit(solution)/shard_map/all_gather | solution.py:47
  46.8 14.4 %copy-start = (bf16[4,8,48,128]{3,2,0,1:T(8,128)(2,1)}, bf16[4,8,48,128]{3,2,0,1:T(8,128)(2,1)S(1)}, u32[]{:S(2)}) copy-start(bf16[4,8,48,128]{3,2,0,1:T(8,128)(2,1)S(1)} %all-to-all-done.2) | copy-start | bytes 1179652
  46.8 33.1 %all-to-all-start = ((bf16[256,4,2,128]{3,2,1,0:T(2,128)(2,1)}), bf16[256,4,2,128]{3,2,1,0:T(2,128)(2,1)}, u32[]{:S(2)}, u32[]{:S(2)}) async-start(bf16[256,4,2,128]{3,2,1,0:T(2,128)(2,1)} %copy.82), calls=%async_computation | async-start | bytes 1048576 | tf_op jit(solution)/shard_map/all_to_all | solution.py:55
  60.9 35.8 %all-gather.7.cloned.1.call-start = ((), (), s32[]{:S(2)}) async-start(), calls=%async_computation.5 | async-start | bytes 3538944 | tf_op jit(solution)/shard_map/all_gather | solution.py:41
  63.1 3.2 %copy-start.5 = (f32[4,2,24,128]{3,2,1,0:T(8,128)S(1)}, f32[4,2,24,128]{3,2,1,0:T(8,128)}, u32[]{:S(2)}) copy-start(f32[4,2,24,128]{3,2,1,0:T(8,128)} %broadcast_add_fusion) | copy-start | bytes 294916
  63.1 3.7 %copy-start.8 = (s32[4,4]{1,0:T(4,128)S(1)}, s32[4,4]{1,0:T(4,128)}, u32[]{:S(2)}) copy-start(s32[4,4]{1,0:T(4,128)} %param.23) | copy-start | bytes 196
  68.5 2.9 %copy-start.10 = (s32[4]{0:T(128)S(1)}, s32[4]{0:T(128)}, u32[]{:S(2)}) copy-start(s32[4]{0:T(128)} %param.24) | copy-start | bytes 52
  90.4 1.2 copy-start.1
  143.8 32.4 %copy-start.4 = (bf16[16,2,8192]{2,1,0:T(2,128)(2,1)S(1)}, bf16[16,2,8192]{2,1,0:T(2,128)(2,1)}, u32[]{:S(2)}) copy-start(bf16[16,2,8192]{2,1,0:T(2,128)(2,1)} %param.15) | copy-start | bytes 1572868
  177.7 2.3 %copy-start.7 = (f32[8192]{0:T(1024)S(1)}, f32[8192]{0:T(1024)}, u32[]{:S(2)}) copy-start(f32[8192]{0:T(1024)} %param.25) | copy-start | bytes 98308
Sparse Core Ops, SparseCore 0:
  35.9 27.5 all-gather.4
  65.3 31.3 all-gather.6

commit v9 on v8

--- a/solution.py
+++ b/solution.py
@@ -89,16 +89,18 @@
 
     win = min(WINDOW_LIMIT, cache_len)
     start = jnp.clip(lengths - win, 0, cache_len - win)
-    take = jax.vmap(lambda a, at: lax.dynamic_slice_in_dim(a, at, win, 0))
-    b_win = take(shared_b, start)
-    x_win = take(x_pair, start)
     pos_win = start[:, None] + jnp.arange(win, dtype=jnp.int32)[None, :]
     in_window = (query_pos[:, :, None] - pos_win[:, None, :] < windows[:, None, None]) & (
         pos_win < lengths[:, None]
     )[:, None, :]
-    score_old = jnp.einsum("rnk,rsk->rns", c_now, b_win, preferred_element_type=jnp.float32)
-    probs_old = jnp.where(in_window, score_old, 0.0).astype(jnp.bfloat16)
-    acc = jnp.einsum("rns,rsc->rnc", probs_old, x_win, preferred_element_type=jnp.float32)
+    accs = []
+    for r in range(requests):
+        b_win = lax.dynamic_slice_in_dim(shared_b[r], start[r], win, 0)
+        x_win = lax.dynamic_slice_in_dim(x_pair[r], start[r], win, 0)
+        score_old = jnp.dot(c_now[r], b_win.T, preferred_element_type=jnp.float32)
+        probs_old = jnp.where(in_window[r], score_old, 0.0).astype(jnp.bfloat16)
+        accs.append(jnp.dot(probs_old, x_win, preferred_element_type=jnp.float32))
+    acc = jnp.stack(accs)
     old_out = acc.reshape(requests, new_len, heads_dev, head_dim)
     old_out = old_out * row_scale[..., None]
 

time: 190 us -> 209 us (1.10)
  other arithmetic: 25.3 us -> 45.5 us
  local copies, waits for them, and re-layouts: 57.3 us -> 47.1 us
  between operations: 13.8 us -> 21.7 us
  waiting for transfers between devices: 16.3 us -> 10.3 us
  matrix products: 14.1 us -> 19 us
  starting transfers between devices: 30 us -> 32.9 us
    gather x32 -> x0, local copies, waits for them, and re-layouts: 28.9 us -> none
    another operation x6, other arithmetic: 7.01 us -> 16.8 us
    all_to_all x1, waiting for transfers between devices: 7.55 us -> 0.01 us  [per_device(): sp = lax.all_to_all(sp, ('tz', 'mlp'), 0, 0, tiled=True)]
    another operation x4, local copies, waits for them, and re-layouts: 0.34 us -> 6.21 us
    and x0 -> x1, other arithmetic: none -> 5.86 us  [per_device(): (query_pos[:, :, None] - pos_win[:, None, :] < windows[:, None, None]) &...]
    slice x1 -> x5, local copies, waits for them, and re-layouts: 0.16 us -> 5.89 us  [the longest x2 2.43 us: per_device(): b_win = lax.dynamic_slice_in_dim(shared_b[r], start[r], win, 0)]
    dot_general x1 -> x4, matrix products: 8.54 us -> 13.5 us  [per_device(): accs.append(jnp.dot(probs_old, x_win, preferred_element_type=jnp.float32))]
    reshape x2, local copies, waits for them, and re-layouts: 0.81 us -> 3.69 us  [per_device(): new_x.reshape(n_mlp, requests, tok_blk, n_tok, chans)]
  transfers between devices with their start and end apart: 5 -> 5, of which waited for: 3 -> 1; matrix products, arithmetic and copies ran while one was open for 22% -> 38% of each run, Pallas kernels for 0% -> 0%
where the time goes in v9:
time: 209 us; the launch traced here: 207 us
  local copies, waits for them, and re-layouts  47.1 us (23%)
  other arithmetic  45.5 us (22%)
  starting transfers between devices  32.9 us (16%)
  blocking collectives  30.2 us (14%)
  between operations  21.7 us (10%)
  matrix products  19 us (9%)
  waiting for transfers between devices  10.3 us (5%)
    all_to_all x1, blocking collectives, per_device(): back = lax.all_to_all(back, ('tz', 'txc', 'mlp'), 0, 0, tiled=True)  30.2 us
    another operation x6, other arithmetic  16.8 us
    all_to_all x1, starting transfers between devices, per_device(): head_x = lax.all_to_all(x_part, ('tz', 'txc', 'mlp'), 0, 0, tiled=True)  14.2 us
    dot_general x4, matrix products, per_device(): accs.append(jnp.dot(probs_old, x_win, preferred_element_type=jnp.float32))  13.5 us
    all_to_all x1, starting transfers between devices, per_device(): sp = lax.all_to_all(sp, ('tz', 'mlp'), 0, 0, tiled=True)  12 us
    unnamed x50, local copies, waits for them, and re-layouts  9.63 us
    all_to_all x1, waiting for transfers between devices, per_device(): head_x = lax.all_to_all(x_part, ('tz', 'txc', 'mlp'), 0, 0, tiled=True)  9.13 us
    all_to_all x1, starting transfers between devices, per_device(): lax.all_to_all(b_cache, 'tz', split_axis=1, concat_axis=1, tiled=True)  6.42 us
  transfers between devices with their start and end apart: 5, of which 1 were waited for; matrix products, arithmetic and copies ran while one was open for 38% of the time, Pallas kernels for 0%

profile of v9, /device:TPU:1, one launch (start us, length us, event | category | flops | bytes accessed | tf_op | source)
XLA Modules:
  0.0 206.7 jit_solution(9130618967376715989)
XLA Ops:
  6.5 1.7 copy.125
  8.2 12.0 %all-to-all-start.1 = ((bf16[32,4,2,256]{3,2,1,0:T(2,128)(2,1)}), bf16[32,4,2,256]{3,2,1,0:T(2,128)(2,1)S(1)}, u32[]{:S(2)}, u32[]{:S(2)}) async-start(bf16[32,4,2,256]{3,2,1,0:T(2,128)(2,1)} %bitcast.6), calls=%async_computation.1 | async-start | bytes 262144 | tf_op jit(solution)/shard_map/all_to_all | solution.py:46
  20.2 0.7 add_clamp_fusion
  20.9 0.7 iota_compare_fusion
  21.6 0.7 shift-left_or_fusion
  22.3 1.6 broadcast_select_fusion
  23.9 0.7 fusion.103
  29.8 0.7 exp.19
  30.6 3.2 %copy.130 = bf16[4,3072,128]{1,2,0:T(8,128)(2,1)S(1)} copy(bf16[4,3072,128]{2,1,0:T(8,128)(2,1)} %param.19) | data formatting | bytes 6291456 | tf_op args[5]
  33.8 1.4 gather_fusion.1
  35.2 1.4 copy.124
  36.6 1.8 copy.133
  38.4 3.8 %reduce-window.14 = f32[4,2,4,128]{3,2,1,0:T(4,128)} reduce-window(f32[4,2,4,128]{3,2,1,0:T(4,128)S(1)} %reshape.248, f32[]{:T(128)} %constant.39.clone.1), window={size=1x1x1x128 pad=0_0x0_0x0_0x127_0}, to_apply=%region_0.0 | reduce-window | flops 520192 | bytes 32772 | tf_op jit(solution)/shard_map/reduce-window
  42.2 0.6 copy-done.10
  42.9 6.4 %all-to-all-start.2 = ((bf16[4,8,48,128]{3,2,0,1:T(8,128)(2,1)}), bf16[4,8,48,128]{3,2,0,1:T(8,128)(2,1)S(1)}, u32[]{:S(2)}, u32[]{:S(2)}) async-start(bf16[4,8,48,128]{3,2,0,1:T(8,128)(2,1)} %copy.133), calls=%async_computation.2 | async-start | bytes 786432 | tf_op jit(solution)/shard_map/all_to_all | solution.py:40
  49.4 0.7 all-gather.5.cloned.1.call-update
  50.1 1.5 slice_reduce_fusion.1
  51.5 1.9 reduce-window.15
  53.4 1.6 reshape.250
  55.0 5.2 %reduce-window.16 = f32[4,2,24,128]{3,2,1,0:T(8,128)} reduce-window(f32[4,2,24,128]{3,2,1,0:T(8,128)} %reshape.250, f32[]{:T(128)} %constant.39.clone.1), window={size=1x1x1x128 pad=0_0x0_0x0_0x127_0}, to_apply=%region_2.3 | reduce-window | flops 3121152 | bytes 196612 | tf_op jit(solution)/shard_map/reduce-window.2
  60.2 1.7 slice_reduce_fusion
  61.8 2.9 %reduce-window.19 = f32[4,2,25]{2,1,0:T(2,128)} reduce-window(f32[4,2,24]{2,1,0:T(2,128)} %slice_reduce_fusion, f32[]{:T(128)} %constant.39.clone.1), window={size=1x1x24 pad=0_0x0_0x24_0}, to_apply=%region_3.4 | reduce-window | flops 4600 | bytes 1572 | tf_op jit(solution)/shard_map/reduce-window.3
  64.7 1.6 broadcast_add_fusion
  66.3 1.6 reduce_window_sum.41
  67.9 1.3 slice.127
  69.3 1.3 copy.170
  70.6 1.3 copy.132
  71.9 1.7 exponential_bitcast_fusion
  73.5 1.4 broadcast_add_fusion.1
  74.9 1.3 reduce_window_sum.39
  76.3 2.2 %reshape.242 = bf16[4,4,2,64,128]{4,3,2,1,0:T(8,128)(2,1)} reshape(bf16[16,2,8192]{2,1,0:T(2,128)(2,1)} %param.14) | data formatting | bytes 1048576 | tf_op jit(solution)/shard_map/reshape | solution.py:53
  78.5 1.5 copy.121
  80.0 1.3 copy.122
  83.9 3.3 %fusion.1 = bf16[4,3072,128]{1,2,0:T(8,128)(2,1)} fusion(bf16[4,3072,128]{1,2,0:T(8,128)(2,1)S(1)} %copy.130, f32[4,3072,2]{1,2,0:T(2,128)} %exponential_bitcast_fusion), kind=kLoop, calls=%fused_computation.6 | loop fusion | flops 4718592 | bytes 6389760 | tf_op jit(solution)/shard_map/convert_element_type | solution.py:75
  87.5 1.3 broadcast_compare_fusion.2
  88.8 14.2 %all-to-all-start = ((bf16[256,4,2,128]{3,2,1,0:T(2,128)(2,1)}), bf16[256,4,2,128]{3,2,1,0:T(2,128)(2,1)S(1)}, u32[]{:S(2)}, u32[]{:S(2)}) async-start(bf16[256,4,2,128]{3,2,1,0:T(2,128)(2,1)} %copy.122), calls=%async_computation | async-start | bytes 1048576 | tf_op jit(solution)/shard_map/all_to_all | solution.py:55
  103.8 0.7 iota_add_fusion.1
  104.5 0.7 exponential_bitcast_fusion.1
  105.2 2.5 %compare_and_fusion = pred[4,512,512]{2,1,0:T(8,128)(4,1)} fusion(s32[512,512]{1,0:T(8,128)S(1)} %iota_subtract_fusion, s32[4]{0:T(128)} %param.24, pred[512,512]{1,0:T(8,128)(4,1)S(1)} %broadcast_compare_fusion), kind=kLoop, calls=%fused_computation.21 | loop fusion | flops 2097152 | bytes 2359312 | tf_op jit(solution)/shard_map/and | solution.py:80
  107.9 5.9 %fusion = pred[4,512,2048]{1,2,0:T(32,128)(4,1)} fusion(s32[4]{0:T(128)S(1)} %copy-done.20, s32[4,2048]{1,0:T(4,128)S(1)} %iota_add_fusion, s32[4,512]{1,0:T(4,128)S(1)} %iota_add_fusion.1, pred[4,2048]{1,0:T(4,128)(4,1)S(1)} %broadcast_compare_fusion.1), kind=kLoop, calls=%fused_computation.3 | loop fusion | flops 12582912 | bytes 4243472 | tf_op jit(solution)/shard_map/and | solution.py:93
  113.7 9.1 %all-to-all-done = bf16[256,4,2,128]{3,2,1,0:T(2,128)(2,1)S(1)} async-done(((bf16[256,4,2,128]{3,2,1,0:T(2,128)(2,1)}), bf16[256,4,2,128]{3,2,1,0:T(2,128)(2,1)S(1)}, u32[]{:S(2)}, u32[]{:S(2)}) %all-to-all-start) | async-done | bytes 524320 | tf_op jit(solution)/shard_map/all_to_all | solution.py:55
  123.6 1.9 reshape.257
  125.5 4.7 %multiply_convert_fusion.2 = bf16[4,512,2,64]{3,2,1,0:T(2,128)(2,1)S(1)} fusion(f32[4,512,2,64]{3,2,1,0:T(2,128)S(1)} %reshape.257, f32[4,512,2]{2,1,0:T(8,128)} %copy.124), kind=kLoop, calls=%fused_computation.26 | loop fusion | flops 524288 | bytes 1589248 | tf_op jit(solution)/shard_map/convert_element_type | solution.py:61
  130.2 1.8 copy.126
  132.4 1.7 fusion.101
  134.1 0.7 fusion.29
  134.8 4.2 %fusion.12 = f32[4,512,2,64]{1,3,2,0:T(8,128)} fusion(f32[4,2,512]{2,1,0:T(2,128)S(1)} %copy-done.16, f32[4,512,512]{2,1,0:T(8,128)S(1)} %fusion.29, pred[4,512,512]{2,1,0:T(8,128)(4,1)S(1)} %copy-done.5, bf16[4,512,2,64]{3,2,1,0:T(2,128)(2,1)S(1)} %multiply_convert_fusion.2), kind=kOutput, calls=%fused_computation.27 | convolution fusion | flops 278921216 | bytes 6832128 | tf_op jit(solution)/shard_map/rhnj,rjhd->rnhd/dot_general | solution.py:85
  139.1 2.1 %copy.134 = bf16[4,8,384,128]{3,2,1,0:T(8,128)(2,1)S(1)} copy(bf16[4,8,384,128]{3,2,0,1:T(8,128)(2,1)} %all-gather.7.cloned.1.call-done) | data formatting | bytes 6291456 | tf_op jit(solution)/shard_map/all_gather | solution.py:41
  141.2 0.6 gather_fusion
  141.8 1.8 fusion.99
  143.6 1.3 copy-done
  145.1 1.4 constant_dynamic-slice_fusion
  146.6 2.8 %fusion.21 = f32[1,512,2,64]{1,3,2,0:T(8,128)S(1)} fusion(bf16[2,64,2048]{2,1,0:T(8,128)(2,1)} %bitcast.248, pred[4,512,2048]{1,2,0:T(32,128)(4,1)} %fusion, bf16[1,3072,128]{2,1,0:T(8,128)(2,1)S(1)} %copy-done.9, s32[]{:T(128)S(6)} %select_n.55, bf16[1,512,128]{2,0,1:T(2,128)(2,1)} %get-tuple-element.25), kind=kOutput, calls=%fused_computation.39 | convolution fusion | flops 538968064 | bytes 2621444 | tf_op jit(solution)/shard_map/dot_general | solution.py:102
  149.4 3.6 %fusion.20 = f32[1,512,2,64]{1,3,2,0:T(8,128)} fusion(bf16[2,64,2048]{2,1,0:T(8,128)(2,1)} %bitcast.247, pred[4,512,2048]{1,2,0:T(32,128)(4,1)} %fusion, bf16[1,3072,128]{2,1,0:T(8,128)(2,1)S(1)} %copy-done.8, s32[]{:T(128)S(6)} %select_n.53, bf16[1,512,128]{2,0,1:T(2,128)(2,1)} %get-tuple-element.23), kind=kOutput, calls=%fused_computation.38 | convolution fusion | flops 538968064 | bytes 2621444 | tf_op jit(solution)/shard_map/dot_general | solution.py:102
  153.0 1.4 constant_dynamic-slice_fusion.2
  154.4 3.6 %fusion.19 = f32[1,512,2,64]{1,3,2,0:T(8,128)} fusion(bf16[2,64,2048]{2,1,0:T(8,128)(2,1)} %bitcast.249, pred[4,512,2048]{1,2,0:T(32,128)(4,1)} %fusion, bf16[1,3072,128]{2,1,0:T(8,128)(2,1)S(1)} %copy-done.7, s32[]{:T(128)S(6)} %select_n.51, bf16[1,512,128]{2,0,1:T(2,128)(2,1)} %get-tuple-element.24), kind=kOutput, calls=%fused_computation.37 | convolution fusion | flops 538968064 | bytes 2621444 | tf_op jit(solution)/shard_map/dot_general | solution.py:102
  158.0 3.5 %fusion.18 = f32[1,512,2,64]{1,3,2,0:T(8,128)} fusion(bf16[2,64,2048]{2,1,0:T(8,128)(2,1)S(1)} %bitcast.246, pred[4,512,2048]{1,2,0:T(32,128)(4,1)} %fusion, bf16[1,3072,128]{2,1,0:T(8,128)(2,1)S(1)} %copy-done.6, s32[]{:T(128)S(6)} %select_n.49, bf16[1,512,128]{2,0,1:T(2,128)(2,1)} %get-tuple-element.22), kind=kOutput, calls=%fused_computation.36 | convolution fusion | flops 538968064 | bytes 2621444 | tf_op jit(solution)/shard_map/dot_general | solution.py:102
  161.6 1.2 fusion.27
  163.2 0.6 fusion.13
  164.2 30.2 %all_to_all.20 = bf16[256,4,2,128]{3,2,1,0:T(2,128)(2,1)S(1)} all-to-all(bf16[256,4,2,128]{3,2,1,0:T(2,128)(2,1)S(1)} %bitcast.242), channel_id=1, replica_groups=mesh['tz'=8,'txc'=8,'mlp'=4] {'tz','txc','mlp'}, dimensions={0} | all-to-all | bytes 1048576 | tf_op jit(solution)/shard_map/all_to_all | solution.py:120
  194.7 1.5 fusion.97
  196.2 0.9 mul.89
  197.6 0.9 mul.91
  198.5 1.4 multiply_convert_fusion.5
  (72 shorter events, 4.3 us)
Async XLA Ops:
  6.5 28.6 %copy-start.15 = (f32[4,512,2]{1,2,0:T(2,128)S(1)}, f32[4,512,2]{1,2,0:T(2,128)}, u32[]{:S(2)}) copy-start(f32[4,512,2]{1,2,0:T(2,128)} %param.17) | copy-start | bytes 49156
  8.2 34.0 %all-to-all-start.1 = ((bf16[32,4,2,256]{3,2,1,0:T(2,128)(2,1)}), bf16[32,4,2,256]{3,2,1,0:T(2,128)(2,1)S(1)}, u32[]{:S(2)}, u32[]{:S(2)}) async-start(bf16[32,4,2,256]{3,2,1,0:T(2,128)(2,1)} %bitcast.6), calls=%async_computation.1 | async-start | bytes 262144 | tf_op jit(solution)/shard_map/all_to_all | solution.py:46
  42.2 0.7 copy-start.10
  42.9 45.9 %all-to-all-start.2 = ((bf16[4,8,48,128]{3,2,0,1:T(8,128)(2,1)}), bf16[4,8,48,128]{3,2,0,1:T(8,128)(2,1)S(1)}, u32[]{:S(2)}, u32[]{:S(2)}) async-start(bf16[4,8,48,128]{3,2,0,1:T(8,128)(2,1)} %copy.133), calls=%async_computation.2 | async-start | bytes 786432 | tf_op jit(solution)/shard_map/all_to_all | solution.py:40
  49.3 80.8 %all-gather.5.cloned.1.call-start = ((), (), s32[]{:S(2)}) async-start(), calls=%async_computation.4 | async-start | bytes 1179648 | tf_op jit(solution)/shard_map/all_gather | solution.py:47
  80.0 7.5 %copy-start.18 = (s32[4,4]{1,0:T(4,128)S(1)}, s32[4,4]{1,0:T(4,128)}, u32[]{:S(2)}) copy-start(s32[4,4]{1,0:T(4,128)} %param.23) | copy-start | bytes 196
  87.3 20.4 %copy-start.19 = (s32[4]{0:T(128)S(1)}, s32[4]{0:T(128)}, u32[]{:S(2)}) copy-start(s32[4]{0:T(128)} %param.22) | copy-start | bytes 52
  87.3 20.6 %copy-start.20 = (s32[4]{0:T(128)S(1)}, s32[4]{0:T(128)}, u32[]{:S(2)}) copy-start(s32[4]{0:T(128)} %param.24) | copy-start | bytes 52
  88.8 14.4 %copy-start.3 = (bf16[4,8,48,128]{3,2,0,1:T(8,128)(2,1)}, bf16[4,8,48,128]{3,2,0,1:T(8,128)(2,1)S(1)}, u32[]{:S(2)}) copy-start(bf16[4,8,48,128]{3,2,0,1:T(8,128)(2,1)S(1)} %all-to-all-done.2) | copy-start | bytes 1179652
  88.8 34.0 %all-to-all-start = ((bf16[256,4,2,128]{3,2,1,0:T(2,128)(2,1)}), bf16[256,4,2,128]{3,2,1,0:T(2,128)(2,1)S(1)}, u32[]{:S(2)}, u32[]{:S(2)}) async-start(bf16[256,4,2,128]{3,2,1,0:T(2,128)(2,1)} %copy.122), calls=%async_computation | async-start | bytes 1048576 | tf_op jit(solution)/shard_map/all_to_all | solution.py:55
  103.0 36.1 %all-gather.7.cloned.1.call-start = ((), (), s32[]{:S(2)}) async-start(), calls=%async_computation.5 | async-start | bytes 3538944 | tf_op jit(solution)/shard_map/all_gather | solution.py:41
  132.4 1.7 copy-start.1
  132.4 2.4 %copy-start.5 = (pred[4,512,512]{2,1,0:T(8,128)(4,1)S(1)}, pred[4,512,512]{2,1,0:T(8,128)(4,1)}, u32[]{:S(2)}) copy-start(pred[4,512,512]{2,1,0:T(8,128)(4,1)} %compare_and_fusion) | copy-start | bytes 3145732
  132.4 2.4 %copy-start.16 = (f32[4,2,512]{2,1,0:T(2,128)S(1)}, f32[4,2,512]{2,1,0:T(2,128)}, u32[]{:S(2)}) copy-start(f32[4,2,512]{2,1,0:T(2,128)} %reduce_window_sum.39) | copy-start | bytes 49156
  141.8 3.0 %copy-start = (bf16[4,3072,128]{1,2,0:T(8,128)(2,1)S(1)}, bf16[4,3072,128]{1,2,0:T(8,128)(2,1)}, u32[]{:S(2)}) copy-start(bf16[4,3072,128]{1,2,0:T(8,128)(2,1)} %fusion.1) | copy-start | bytes 9437188
  144.8 1.7 copy-start.9
  145.1 4.3 %copy-start.8 = (bf16[1,3072,128]{2,1,0:T(8,128)(2,1)S(1)}, bf16[1,3072,128]{2,1,0:T(8,128)(2,1)}, u32[]{:S(2)}) copy-start(bf16[1,3072,128]{2,1,0:T(8,128)(2,1)} %get-tuple-element.16) | copy-start | bytes 2359300
  149.4 5.0 %copy-start.7 = (bf16[1,3072,128]{2,1,0:T(8,128)(2,1)S(1)}, bf16[1,3072,128]{2,1,0:T(8,128)(2,1)}, u32[]{:S(2)}) copy-start(bf16[1,3072,128]{2,1,0:T(8,128)(2,1)} %get-tuple-element.17) | copy-start | bytes 2359300
  153.0 5.0 %copy-start.6 = (bf16[1,3072,128]{2,1,0:T(8,128)(2,1)S(1)}, bf16[1,3072,128]{2,1,0:T(8,128)(2,1)}, u32[]{:S(2)}) copy-start(bf16[1,3072,128]{2,1,0:T(8,128)(2,1)} %get-tuple-element.14) | copy-start | bytes 2359300
  154.4 3.6 %copy-start.12 = (bf16[1,2048,128]{1,2,0:T(8,128)(2,1)S(1)}, bf16[1,2048,128]{1,2,0:T(8,128)(2,1)}, u32[]{:S(2)}) copy-start(bf16[1,2048,128]{1,2,0:T(8,128)(2,1)} %get-tuple-element.35) | copy-start | bytes 1572868
  158.0 3.5 %copy-start.4 = (f32[4,512,2,64]{1,3,2,0:T(8,128)S(1)}, f32[4,512,2,64]{1,3,2,0:T(8,128)}, u32[]{:S(2)}) copy-start(f32[4,512,2,64]{1,3,2,0:T(8,128)} %fusion.12) | copy-start | bytes 3145732
  158.0 3.5 %copy-start.13 = (f32[1,512,2,64]{1,3,2,0:T(8,128)S(1)}, f32[1,512,2,64]{1,3,2,0:T(8,128)}, u32[]{:S(2)}) copy-start(f32[1,512,2,64]{1,3,2,0:T(8,128)} %fusion.20) | copy-start | bytes 786436
  158.0 3.5 %copy-start.14 = (f32[1,512,2,64]{1,3,2,0:T(8,128)S(1)}, f32[1,512,2,64]{1,3,2,0:T(8,128)}, u32[]{:S(2)}) copy-start(f32[1,512,2,64]{1,3,2,0:T(8,128)} %fusion.19) | copy-start | bytes 786436
  161.5 1.6 copy-start.2
  161.5 1.6 copy-start.21
  161.6 1.6 copy-start.22
  162.8 31.9 %copy-start.11 = (bf16[16,2,8192]{2,1,0:T(2,128)(2,1)S(1)}, bf16[16,2,8192]{2,1,0:T(2,128)(2,1)}, u32[]{:S(2)}) copy-start(bf16[16,2,8192]{2,1,0:T(2,128)(2,1)} %param.15) | copy-start | bytes 1572868
  194.7 3.8 %copy-start.17 = (f32[8192]{0:T(1024)S(1)}, f32[8192]{0:T(1024)}, u32[]{:S(2)}) copy-start(f32[8192]{0:T(1024)} %param.25) | copy-start | bytes 98308
Sparse Core Ops, SparseCore 0:
  52.0 28.4 all-gather.4
  105.6 32.4 all-gather.6

commit v10 on v6

--- a/solution.py
+++ b/solution.py
@@ -109,14 +109,16 @@
 
     back = mixer_out.reshape(requests, n_dev, tok_blk, chans).transpose(1, 0, 2, 3)
     back = lax.all_to_all(back, ("tz", "txc", "mlp"), 0, 0, tiled=True)
-    back = back.reshape(n_tok, n_mlp, requests, tok_blk, chans).transpose(1, 2, 3, 0, 4)
-    mixer_tok = lax.optimization_barrier(back.reshape(n_mlp * requests, tok_blk, n_tok * chans))
+    back = back.reshape(n_tz, n_txc, n_mlp, requests, tok_blk, chans)
 
-    gated_out = mixer_tok.astype(jnp.float32) * jax.nn.silu(gate_input.astype(jnp.float32))
-    grouped = gated_out.reshape(gated_out.shape[0], gated_out.shape[1], groups, -1)
-    norm_scale = lax.rsqrt(jnp.mean(grouped * grouped, axis=-1, keepdims=True) + EPS)
-    normed = (grouped * norm_scale).reshape(gated_out.shape) * norm_gain
-    return normed.astype(jnp.bfloat16)
+    gate = gate_input.reshape(n_mlp, requests, tok_blk, n_tz, n_txc, chans)
+    gate = gate.transpose(3, 4, 0, 1, 2, 5).astype(jnp.float32)
+    gated_out = back.astype(jnp.float32) * jax.nn.silu(gate)
+    norm_scale = lax.rsqrt(jnp.mean(gated_out * gated_out, axis=(1, 5), keepdims=True) + EPS)
+    gain = norm_gain.reshape(n_tz, n_txc, 1, 1, 1, chans)
+    normed = (gated_out * norm_scale * gain).astype(jnp.bfloat16)
+    normed = normed.transpose(2, 3, 4, 0, 1, 5)
+    return normed.reshape(n_mlp * requests, tok_blk, n_tok * chans)
 
 
 def solution(mesh):

time: 157 us -> 161 us (1.025)
  blocking collectives: 53 us -> 21.3 us
  waiting for transfers between devices: 6.45 us -> 29.1 us
  starting transfers between devices: 13.8 us -> 27.5 us
    all_to_all x1 -> x0, blocking collectives: 31.7 us -> none  [per_device(): back = lax.all_to_all(back, ('tz', 'txc', 'mlp'), 0, 0, tiled=True)]
    all_to_all x0 -> x1, waiting for transfers between devices: none -> 19.5 us  [per_device(): back = lax.all_to_all(back, ('tz', 'txc', 'mlp'), 0, 0, tiled=True)]
    all_to_all x0 -> x1, starting transfers between devices: none -> 13.8 us  [per_device(): back = lax.all_to_all(back, ('tz', 'txc', 'mlp'), 0, 0, tiled=True)]
    all_to_all x1, waiting for transfers between devices: 4.21 us -> 9 us  [per_device(): lax.all_to_all(b_cache, 'tz', split_axis=1, concat_axis=1, tiled=True)]
    mul x3 -> x0, local copies, waits for them, and re-layouts: 1.93 us -> none  [the longest x2 1.03 us: per_device(): normed = (grouped * norm_scale).reshape(gated_out.shape) * norm_gain]
    reduce_sum x1, other arithmetic: 0.15 us -> 1.99 us  [per_device(): jnp.mean(gated_out * gated_out, axis=(1, 5), keepdims=True) + EPS]
    unnamed x28 -> x32, local copies, waits for them, and re-layouts: 6.74 us -> 6.7 us
  transfers between devices with their start and end apart: 4 -> 5, of which waited for: 3 -> 2; matrix products, arithmetic and copies ran while one was open for 27% -> 27% of each run, Pallas kernels for 0% -> 0%
where the time goes in v10:
time: 161 us; the launch traced here: 160 us
  waiting for transfers between devices  29.1 us (18%)
  starting transfers between devices  27.5 us (17%)
  local copies, waits for them, and re-layouts  26.4 us (16%)
  other arithmetic  25.1 us (16%)
  blocking collectives  21.3 us (13%)
  matrix products  16.6 us (10%)
  between operations  13.8 us (9%)
    all_to_all x1, blocking collectives, per_device(): sp = lax.all_to_all(sp, ('tz', 'mlp'), 0, 0, tiled=True)  21.3 us
    all_to_all x1, waiting for transfers between devices, per_device(): back = lax.all_to_all(back, ('tz', 'txc', 'mlp'), 0, 0, tiled=True)  19.5 us
    all_to_all x1, starting transfers between devices, per_device(): back = lax.all_to_all(back, ('tz', 'txc', 'mlp'), 0, 0, tiled=True)  13.8 us
    dot_general x1, matrix products, per_device(): jnp.einsum('rns,rsc->rnc', probs_old, x_pair, preferred_element_type=jnp....  11.8 us
    all_to_all x1, starting transfers between devices, per_device(): head_x = lax.all_to_all(x_part, ('tz', 'txc', 'mlp'), 0, 0, tiled=True)  10 us
    all_to_all x1, waiting for transfers between devices, per_device(): lax.all_to_all(b_cache, 'tz', split_axis=1, concat_axis=1, tiled=True)  9 us
    unnamed x32, local copies, waits for them, and re-layouts  6.7 us
    another operation x6, other arithmetic  6.41 us
  transfers between devices with their start and end apart: 5, of which 2 were waited for; matrix products, arithmetic and copies ran while one was open for 27% of the time, Pallas kernels for 0%

profile of v10, /device:TPU:1, one launch (start us, length us, event | category | flops | bytes accessed | tf_op | source)
XLA Modules:
  0.0 159.7 jit_solution(11497144001817974383)
XLA Ops:
  6.5 0.0 all-gather.5.cloned.1.call-start
  6.6 1.1 copy.34
  7.6 21.3 %all_to_all.20 = bf16[32,4,2,256]{3,2,1,0:T(2,128)(2,1)} all-to-all(bf16[32,4,2,256]{3,2,1,0:T(2,128)(2,1)S(1)} %bitcast.91), channel_id=1, replica_groups=mesh['tz'=8,'txc'=8,'mlp'=4] {'tz','mlp'}, dimensions={0} | all-to-all | bytes 262144 | tf_op jit(solution)/shard_map/all_to_all | solution.py:45
  28.9 1.8 %copy.42 = bf16[4,8,48,128]{3,2,0,1:T(8,128)(2,1)} copy(bf16[4,8,48,128]{3,2,1,0:T(8,128)(2,1)} %param.20) | data formatting | bytes 786432 | tf_op args[6]
  30.7 3.5 %all-to-all-start.2 = ((bf16[4,8,48,128]{3,2,0,1:T(8,128)(2,1)}), bf16[4,8,48,128]{3,2,0,1:T(8,128)(2,1)S(1)}, u32[]{:S(2)}, u32[]{:S(2)}) async-start(bf16[4,8,48,128]{3,2,0,1:T(8,128)(2,1)} %copy.42), calls=%async_computation.2 | async-start | bytes 786432 | tf_op jit(solution)/shard_map/all_to_all | solution.py:39
  34.2 1.4 reshape.168
  35.6 0.4 copy.30
  36.0 1.3 copy.31
  37.4 0.1 iota_compare_fusion
  37.5 9.0 %all-to-all-done.2 = bf16[4,8,48,128]{3,2,0,1:T(8,128)(2,1)S(1)} async-done(((bf16[4,8,48,128]{3,2,0,1:T(8,128)(2,1)}), bf16[4,8,48,128]{3,2,0,1:T(8,128)(2,1)S(1)}, u32[]{:S(2)}, u32[]{:S(2)}) %all-to-all-start.2) | async-done | bytes 393248 | tf_op jit(solution)/shard_map/all_to_all | solution.py:39
  46.5 10.0 %all-to-all-start = ((bf16[256,4,2,128]{3,2,1,0:T(2,128)(2,1)}), bf16[256,4,2,128]{3,2,1,0:T(2,128)(2,1)}, u32[]{:S(2)}, u32[]{:S(2)}) async-start(bf16[256,4,2,128]{3,2,1,0:T(2,128)(2,1)} %copy.31), calls=%async_computation | async-start | bytes 1048576 | tf_op jit(solution)/shard_map/all_to_all | solution.py:54
  56.5 0.2 all-gather.7.cloned.1.call-start
  56.7 0.5 all-gather.7.cloned.1.call-update
  57.2 0.1 broadcast_select_fusion
  57.3 0.1 reshape.176
  57.4 2.3 %reduce-window.16 = f32[4,2,24,128]{3,2,1,0:T(8,128)S(1)} reduce-window(f32[4,2,24,128]{3,2,1,0:T(8,128)S(1)} %reshape.176, f32[]{:T(128)} %constant.12.clone.1), window={size=1x1x1x128 pad=0_0x0_0x0_0x127_0}, to_apply=%region_2.3 | reduce-window | flops 3121152 | bytes 196612 | tf_op jit(solution)/shard_map/reduce-window.2
  59.7 0.2 slice_reduce_fusion
  59.9 0.8 reduce-window.19
  60.7 0.1 broadcast_add_fusion
  60.8 0.1 reduce_window_sum.41
  60.9 0.1 slice.38
  60.9 0.1 copy.52
  61.0 0.1 copy.41
  61.1 0.1 negate_bitcast_fusion
  61.3 2.4 %reduce-window.14 = f32[4,2,4,128]{3,2,1,0:T(4,128)S(1)} reduce-window(f32[4,2,4,128]{3,2,1,0:T(4,128)S(1)} %reshape.174, f32[]{:T(128)} %constant.12.clone.1), window={size=1x1x1x128 pad=0_0x0_0x0_0x127_0}, to_apply=%region_0.0 | reduce-window | flops 520192 | bytes 32772 | tf_op jit(solution)/shard_map/reduce-window
  63.7 0.2 slice_reduce_fusion.1
  63.9 0.7 reduce-window.15
  64.6 1.1 iota_subtract_fusion
  65.7 0.6 and_bitcast_fusion
  66.3 0.5 shift-left_or_fusion
  66.8 0.1 broadcast_add_fusion.1
  66.9 0.1 exponential_bitcast_fusion
  67.1 0.1 broadcast_compare_fusion
  67.2 1.4 copy.33
  68.6 3.2 %copy.39 = bf16[4,3072,128]{1,2,0:T(8,128)(2,1)S(1)} copy(bf16[4,3072,128]{2,1,0:T(8,128)(2,1)} %param.19) | data formatting | bytes 6291456 | tf_op args[5]
  71.8 0.7 reshape.202
  72.5 1.4 gather_fusion.1
  74.0 2.5 %fusion.5 = bf16[4,3072,128]{1,2,0:T(8,128)(2,1)} fusion(bf16[4,3072,128]{1,2,0:T(8,128)(2,1)S(1)} %copy.39, f32[4,3072,2]{1,2,0:T(2,128)S(1)} %exponential_bitcast_fusion), kind=kLoop, calls=%fused_computation.10 | loop fusion | flops 4718592 | bytes 6389760 | tf_op jit(solution)/shard_map/convert_element_type | solution.py:74
  76.4 0.1 broadcast_compare_fusion.1
  76.5 0.7 iota_add_fusion
  77.3 2.4 %compare_and_fusion = pred[4,512,512]{2,1,0:T(8,128)(4,1)} fusion(s32[512,512]{1,0:T(8,128)S(1)} %copy-done, s32[4]{0:T(128)} %param.24, pred[512,512]{1,0:T(8,128)(4,1)S(1)} %broadcast_compare_fusion), kind=kLoop, calls=%fused_computation.13 | loop fusion | flops 2097152 | bytes 2359312 | tf_op jit(solution)/shard_map/and | solution.py:79
  79.7 1.4 convert_bitcast_fusion
  81.1 0.4 copy.32
  81.5 1.9 %reshape.183 = f32[4,512,2,64]{3,2,1,0:T(2,128)S(1)} reshape(f32[4,256,2,128]{3,2,1,0:T(2,128)S(1)} %copy.32) | data formatting | bytes 2097152 | tf_op jit(solution)/shard_map/convert_element_type | solution.py:59
  83.4 4.7 %multiply_convert_fusion.2 = bf16[4,512,2,64]{3,2,1,0:T(2,128)(2,1)S(1)} fusion(f32[4,512,2,64]{3,2,1,0:T(2,128)S(1)} %reshape.183, f32[4,512,2]{2,1,0:T(8,128)} %copy.33), kind=kLoop, calls=%fused_computation.15 | loop fusion | flops 524288 | bytes 1589248 | tf_op jit(solution)/shard_map/convert_element_type | solution.py:60
  88.1 1.8 %copy.35 = bf16[8,4,8,4,2,256]{5,3,4,1,2,0:T(4,128)(2,1)S(1)} copy(bf16[8,4,8,4,2,256]{5,4,3,2,1,0:T(2,128)(2,1)} %bitcast.90) | data formatting | bytes 2097152 | tf_op jit(solution)/shard_map/reshape | solution.py:47
  89.9 0.4 fusion.47
  90.3 0.7 fusion.19
  91.0 0.2 copy-done.2
  91.1 3.5 %fusion.10 = f32[4,512,2,64]{1,3,2,0:T(8,128)S(1)} fusion(f32[4,2,512]{2,1,0:T(2,128)S(1)} %reduce_window_sum.39, f32[4,512,512]{2,1,0:T(8,128)S(1)} %fusion.19, pred[4,512,512]{2,1,0:T(8,128)(4,1)S(1)} %copy-done.2, bf16[4,512,2,64]{3,2,1,0:T(2,128)(2,1)S(1)} %multiply_convert_fusion.2), kind=kOutput, calls=%fused_computation.16 | convolution fusion | flops 278921216 | bytes 6832128 | tf_op jit(solution)/shard_map/rhnj,rjhd->rnhd/dot_general | solution.py:84
  94.7 3.9 %copy.43 = bf16[4,8,384,128]{3,2,1,0:T(8,128)(2,1)} copy(bf16[4,8,384,128]{3,2,0,1:T(8,128)(2,1)} %all-gather.7.cloned.1.call-done) | data formatting | bytes 6291456 | tf_op jit(solution)/shard_map/all_gather | solution.py:40
  98.6 1.3 gather_fusion
  99.9 11.8 %fusion.2 = f32[4,512,128]{1,2,0:T(8,128)} fusion(bf16[4,3072,128]{1,2,0:T(8,128)(2,1)} %fusion.5, s32[4]{0:T(128)S(1)} %copy-done.12, s32[4,512]{1,0:T(4,128)S(1)} %iota_add_fusion, pred[4,3072]{1,0:T(4,128)(4,1)S(1)} %iota_compare_fusion, bf16[4,3072,128]{2,1,0:T(8,128)(2,1)} %bitcast.85, bf16[4,512,128]{2,0,1:T(4,128)(2,1)S(1)} %get-tuple-element.14), kind=kOutput, calls=%fused_computation.6 | convolution fusion | flops 3252682752 | bytes 7884816 | tf_op jit(solution)/shard_map/rns,rsc->rnc/dot_general | solution.py:94
  111.7 1.5 multiply_add_fusion
  113.3 0.3 copy.45
  113.6 0.6 fusion.11
  114.2 1.2 copy.68
  115.4 13.8 %all-to-all-start.3 = ((bf16[256,4,2,128]{3,2,1,0:T(2,128)(2,1)}), bf16[256,4,2,128]{3,2,1,0:T(2,128)(2,1)S(1)}, u32[]{:S(2)}, u32[]{:S(2)}) async-start(bf16[256,4,2,128]{3,2,1,0:T(2,128)(2,1)} %bitcast.79), calls=%async_computation.3 | async-start | bytes 1048576 | tf_op jit(solution)/shard_map/all_to_all | solution.py:111
  129.2 0.3 reshape.185
  129.6 19.5 %all-to-all-done.3 = bf16[256,4,2,128]{3,2,1,0:T(2,128)(2,1)S(1)} async-done(((bf16[256,4,2,128]{3,2,1,0:T(2,128)(2,1)}), bf16[256,4,2,128]{3,2,1,0:T(2,128)(2,1)S(1)}, u32[]{:S(2)}, u32[]{:S(2)}) %all-to-all-start.3) | async-done | bytes 524320 | tf_op jit(solution)/shard_map/all_to_all | solution.py:111
  149.1 2.0 %multiply_reduce_fusion = (f32[8,4,4,2]{3,2,1,0:T(4,128)S(1)}, f32[8,8,4,4,2,128]{5,4,3,2,1,0:T(2,128)S(1)}) fusion(f32[4,4,2,8,8,128]{5,4,3,2,1,0:T(8,128)S(1)} %reshape.185, bf16[8,8,4,4,2,128]{5,4,3,2,1,0:T(2,128)(2,1)S(1)} %bitcast.87), kind=kLoop, calls=%fused_computation.30 | loop fusion | flops 2096896 | bytes 2622464 | tf_op jit(solution)/shard_map/reduce_sum | solution.py:117
  151.1 0.7 fusion.18
  151.8 0.2 copy.48
  152.0 0.9 reshape.182
  (36 shorter events, 0.2 us)
Async XLA Ops:
  6.5 30.8 %copy-start.10 = (s32[4]{0:T(128)S(1)}, s32[4]{0:T(128)}, u32[]{:S(2)}) copy-start(s32[4]{0:T(128)} %param.22) | copy-start | bytes 52
  6.5 50.7 %copy-start.4 = (f32[4,2,3072]{2,1,0:T(2,128)S(1)}, f32[4,2,3072]{2,1,0:T(2,128)}, u32[]{:S(2)}) copy-start(f32[4,2,3072]{2,1,0:T(2,128)} %param.21) | copy-start | bytes 294916
  6.5 54.6 %copy-start.13 = (f32[2]{0:T(128)S(1)}, f32[2]{0:T(128)}, u32[]{:S(2)}) copy-start(f32[2]{0:T(128)} %param.18) | copy-start | bytes 28
  6.5 54.6 %copy-start.5 = (f32[4,512,2]{1,2,0:T(2,128)S(1)}, f32[4,512,2]{1,2,0:T(2,128)}, u32[]{:S(2)}) copy-start(f32[4,512,2]{1,2,0:T(2,128)} %param.17) | copy-start | bytes 49156
  6.5 81.5 %all-gather.5.cloned.1.call-start = ((), (), s32[]{:S(2)}) async-start(), calls=%async_computation.4 | async-start | bytes 1179648 | tf_op jit(solution)/shard_map/all_gather | solution.py:46
  28.9 36.8 %copy-start.7 = (s32[4,4]{1,0:T(4,128)S(1)}, s32[4,4]{1,0:T(4,128)}, u32[]{:S(2)}) copy-start(s32[4,4]{1,0:T(4,128)} %param.23) | copy-start | bytes 196
  30.7 15.7 %all-to-all-start.2 = ((bf16[4,8,48,128]{3,2,0,1:T(8,128)(2,1)}), bf16[4,8,48,128]{3,2,0,1:T(8,128)(2,1)S(1)}, u32[]{:S(2)}, u32[]{:S(2)}) async-start(bf16[4,8,48,128]{3,2,0,1:T(8,128)(2,1)} %copy.42), calls=%async_computation.2 | async-start | bytes 786432 | tf_op jit(solution)/shard_map/all_to_all | solution.py:39
  46.5 10.2 %copy-start.1 = (bf16[4,8,48,128]{3,2,0,1:T(8,128)(2,1)}, bf16[4,8,48,128]{3,2,0,1:T(8,128)(2,1)S(1)}, u32[]{:S(2)}) copy-start(bf16[4,8,48,128]{3,2,0,1:T(8,128)(2,1)S(1)} %all-to-all-done.2) | copy-start | bytes 1179652
  46.5 33.2 %all-to-all-start = ((bf16[256,4,2,128]{3,2,1,0:T(2,128)(2,1)}), bf16[256,4,2,128]{3,2,1,0:T(2,128)(2,1)}, u32[]{:S(2)}, u32[]{:S(2)}) async-start(bf16[256,4,2,128]{3,2,1,0:T(2,128)(2,1)} %copy.31), calls=%async_computation | async-start | bytes 1048576 | tf_op jit(solution)/shard_map/all_to_all | solution.py:54
  56.5 38.2 %all-gather.7.cloned.1.call-start = ((), (), s32[]{:S(2)}) async-start(), calls=%async_computation.5 | async-start | bytes 3538944 | tf_op jit(solution)/shard_map/all_gather | solution.py:40
  71.8 4.7 %copy-start.8 = (s32[4,4]{1,0:T(4,128)S(1)}, s32[4,4]{1,0:T(4,128)}, u32[]{:S(2)}) copy-start(s32[4,4]{1,0:T(4,128)} %param.23) | copy-start | bytes 196
  71.8 4.6 %copy-start.11 = (s32[4]{0:T(128)S(1)}, s32[4]{0:T(128)}, u32[]{:S(2)}) copy-start(s32[4]{0:T(128)} %param.22) | copy-start | bytes 52
  74.0 3.3 %copy-start = (s32[512,512]{1,0:T(8,128)S(1)}, s32[512,512]{1,0:T(8,128)}, u32[]{:S(2)}) copy-start(s32[512,512]{1,0:T(8,128)} %iota_subtract_fusion) | copy-start | bytes 3145732
  89.9 1.3 copy-start.2
  94.6 5.3 %copy-start.12 = (s32[4]{0:T(128)S(1)}, s32[4]{0:T(128)}, u32[]{:S(2)}) copy-start(s32[4]{0:T(128)} %param.24) | copy-start | bytes 52
  111.7 1.9 %copy-start.9 = (pred[4,4]{1,0:T(4,128)(4,1)S(1)}, pred[4,4]{1,0:T(4,128)(4,1)}, u32[]{:S(2)}) copy-start(pred[4,4]{1,0:T(4,128)(4,1)} %and_bitcast_fusion) | copy-start | bytes 52
  111.7 17.5 %copy-start.3 = (bf16[16,2,8192]{2,1,0:T(2,128)(2,1)S(1)}, bf16[16,2,8192]{2,1,0:T(2,128)(2,1)}, u32[]{:S(2)}) copy-start(bf16[16,2,8192]{2,1,0:T(2,128)(2,1)} %param.15) | copy-start | bytes 1572868
  113.6 37.5 %copy-start.6 = (f32[8192]{0:T(1024)S(1)}, f32[8192]{0:T(1024)}, u32[]{:S(2)}) copy-start(f32[8192]{0:T(1024)} %param.25) | copy-start | bytes 98308
  115.4 33.7 %all-to-all-start.3 = ((bf16[256,4,2,128]{3,2,1,0:T(2,128)(2,1)}), bf16[256,4,2,128]{3,2,1,0:T(2,128)(2,1)S(1)}, u32[]{:S(2)}, u32[]{:S(2)}) async-start(bf16[256,4,2,128]{3,2,1,0:T(2,128)(2,1)} %bitcast.79), calls=%async_computation.3 | async-start | bytes 1048576 | tf_op jit(solution)/shard_map/all_to_all | solution.py:111
Sparse Core Ops, SparseCore 0:
  29.1 22.5 all-gather.4
  59.1 32.5 all-gather.6

commit v11 on v6

--- a/solution.py
+++ b/solution.py
@@ -110,7 +110,7 @@
     back = mixer_out.reshape(requests, n_dev, tok_blk, chans).transpose(1, 0, 2, 3)
     back = lax.all_to_all(back, ("tz", "txc", "mlp"), 0, 0, tiled=True)
     back = back.reshape(n_tok, n_mlp, requests, tok_blk, chans).transpose(1, 2, 3, 0, 4)
-    mixer_tok = lax.optimization_barrier(back.reshape(n_mlp * requests, tok_blk, n_tok * chans))
+    mixer_tok = back.reshape(n_mlp * requests, tok_blk, n_tok * chans)
 
     gated_out = mixer_tok.astype(jnp.float32) * jax.nn.silu(gate_input.astype(jnp.float32))
     grouped = gated_out.reshape(gated_out.shape[0], gated_out.shape[1], groups, -1)

time: 157 us -> 159 us (1.013)
  other arithmetic: 25.5 us -> 27.1 us
    unnamed x28 -> x26, local copies, waits for them, and re-layouts: 6.74 us -> 6.74 us
where the time goes in v11:
time: 159 us; the launch traced here: 158 us
  blocking collectives  53 us (33%)
  local copies, waits for them, and re-layouts  27.5 us (17%)
  other arithmetic  27.1 us (17%)
  matrix products  16.6 us (10%)
  starting transfers between devices  13.8 us (9%)
  between operations  13.8 us (9%)
  waiting for transfers between devices  6.43 us (4%)
    all_to_all x1, blocking collectives, per_device(): back = lax.all_to_all(back, ('tz', 'txc', 'mlp'), 0, 0, tiled=True)  31.7 us
    all_to_all x1, blocking collectives, per_device(): sp = lax.all_to_all(sp, ('tz', 'mlp'), 0, 0, tiled=True)  21.3 us
    dot_general x1, matrix products, per_device(): jnp.einsum('rns,rsc->rnc', probs_old, x_pair, preferred_element_type=jnp....  11.8 us
    all_to_all x1, starting transfers between devices, per_device(): head_x = lax.all_to_all(x_part, ('tz', 'txc', 'mlp'), 0, 0, tiled=True)  10 us
    unnamed x26, local copies, waits for them, and re-layouts  6.74 us
    another operation x6, other arithmetic  6.41 us
    convert_element_type x1, other arithmetic, per_device(): scaled = (scaled * step_size[..., None]).astype(jnp.bfloat16)  4.66 us
    all_to_all x1, waiting for transfers between devices, per_device(): lax.all_to_all(b_cache, 'tz', split_axis=1, concat_axis=1, tiled=True)  4.21 us
  transfers between devices with their start and end apart: 4, of which 3 were waited for; matrix products, arithmetic and copies ran while one was open for 27% of the time, Pallas kernels for 0%

profile of v11, /device:TPU:1, one launch (start us, length us, event | category | flops | bytes accessed | tf_op | source)
XLA Modules:
  0.0 158.1 jit_solution(7766129945176589313)
XLA Ops:
  6.5 1.0 copy.71
  7.6 21.3 %all_to_all.20 = bf16[32,4,2,256]{3,2,1,0:T(2,128)(2,1)} all-to-all(bf16[32,4,2,256]{3,2,1,0:T(2,128)(2,1)S(1)} %bitcast.83), channel_id=1, replica_groups=mesh['tz'=8,'txc'=8,'mlp'=4] {'tz','mlp'}, dimensions={0} | all-to-all | bytes 262144 | tf_op jit(solution)/shard_map/all_to_all | solution.py:45
  28.9 1.8 %copy.79 = bf16[4,8,48,128]{3,2,0,1:T(8,128)(2,1)} copy(bf16[4,8,48,128]{3,2,1,0:T(8,128)(2,1)} %param.20) | data formatting | bytes 786432 | tf_op args[6]
  30.7 3.6 %all-to-all-start.2 = ((bf16[4,8,48,128]{3,2,0,1:T(8,128)(2,1)}), bf16[4,8,48,128]{3,2,0,1:T(8,128)(2,1)S(1)}, u32[]{:S(2)}, u32[]{:S(2)}) async-start(bf16[4,8,48,128]{3,2,0,1:T(8,128)(2,1)} %copy.79), calls=%async_computation.2 | async-start | bytes 786432 | tf_op jit(solution)/shard_map/all_to_all | solution.py:39
  34.3 0.7 exp.19
  34.9 0.8 negate_bitcast_fusion
  35.8 2.4 %reduce-window.14 = f32[4,2,4,128]{3,2,1,0:T(4,128)S(1)} reduce-window(f32[4,2,4,128]{3,2,1,0:T(4,128)S(1)} %reshape.174, f32[]{:T(128)} %constant.12.clone.1), window={size=1x1x1x128 pad=0_0x0_0x0_0x127_0}, to_apply=%region_0.0 | reduce-window | flops 520192 | bytes 32772 | tf_op jit(solution)/shard_map/reduce-window
  38.2 0.2 slice_reduce_fusion.1
  38.4 0.7 reduce-window.15
  39.1 1.4 reshape.168
  40.5 0.4 copy.67
  40.9 1.3 copy.68
  42.3 0.1 iota_compare_fusion
  42.3 4.2 %all-to-all-done.2 = bf16[4,8,48,128]{3,2,0,1:T(8,128)(2,1)S(1)} async-done(((bf16[4,8,48,128]{3,2,0,1:T(8,128)(2,1)}), bf16[4,8,48,128]{3,2,0,1:T(8,128)(2,1)S(1)}, u32[]{:S(2)}, u32[]{:S(2)}) %all-to-all-start.2) | async-done | bytes 393248 | tf_op jit(solution)/shard_map/all_to_all | solution.py:39
  46.6 10.0 %all-to-all-start = ((bf16[256,4,2,128]{3,2,1,0:T(2,128)(2,1)}), bf16[256,4,2,128]{3,2,1,0:T(2,128)(2,1)}, u32[]{:S(2)}, u32[]{:S(2)}) async-start(bf16[256,4,2,128]{3,2,1,0:T(2,128)(2,1)} %copy.68), calls=%async_computation | async-start | bytes 1048576 | tf_op jit(solution)/shard_map/all_to_all | solution.py:54
  56.6 0.2 all-gather.7.cloned.1.call-start
  56.8 0.5 all-gather.7.cloned.1.call-update
  57.4 0.1 reshape.176
  57.5 2.3 %reduce-window.16 = f32[4,2,24,128]{3,2,1,0:T(8,128)S(1)} reduce-window(f32[4,2,24,128]{3,2,1,0:T(8,128)S(1)} %reshape.176, f32[]{:T(128)} %constant.12.clone.1), window={size=1x1x1x128 pad=0_0x0_0x0_0x127_0}, to_apply=%region_2.3 | reduce-window | flops 3121152 | bytes 196612 | tf_op jit(solution)/shard_map/reduce-window.2
  59.8 0.2 slice_reduce_fusion
  60.0 0.8 reduce-window.19
  60.8 0.1 broadcast_add_fusion
  61.0 0.1 copy.90
  61.1 0.1 copy.78
  61.2 1.1 iota_subtract_fusion
  62.4 0.6 and_bitcast_fusion
  63.0 0.1 exponential_bitcast_fusion
  63.1 0.1 broadcast_compare_fusion
  63.2 1.4 copy.70
  64.7 3.2 %copy.76 = bf16[4,3072,128]{1,2,0:T(8,128)(2,1)S(1)} copy(bf16[4,3072,128]{2,1,0:T(8,128)(2,1)} %param.19) | data formatting | bytes 6291456 | tf_op args[5]
  67.9 0.1 reshape.201
  68.0 1.4 gather_fusion.1
  69.4 2.5 %fusion.5 = bf16[4,3072,128]{1,2,0:T(8,128)(2,1)} fusion(bf16[4,3072,128]{1,2,0:T(8,128)(2,1)S(1)} %copy.76, f32[4,3072,2]{1,2,0:T(2,128)S(1)} %exponential_bitcast_fusion), kind=kLoop, calls=%fused_computation.10 | loop fusion | flops 4718592 | bytes 6389760 | tf_op jit(solution)/shard_map/convert_element_type | solution.py:74
  71.9 0.7 iota_add_fusion
  72.7 2.4 %compare_and_fusion = pred[4,512,512]{2,1,0:T(8,128)(4,1)} fusion(s32[512,512]{1,0:T(8,128)S(1)} %copy-done, s32[4]{0:T(128)} %param.24, pred[512,512]{1,0:T(8,128)(4,1)S(1)} %broadcast_compare_fusion), kind=kLoop, calls=%fused_computation.13 | loop fusion | flops 2097152 | bytes 2359312 | tf_op jit(solution)/shard_map/and | solution.py:79
  75.1 0.5 all-to-all-done
  75.6 1.4 convert_bitcast_fusion.1
  77.0 0.4 copy.69
  77.3 1.9 %reshape.182 = f32[4,512,2,64]{3,2,1,0:T(2,128)S(1)} reshape(f32[4,256,2,128]{3,2,1,0:T(2,128)S(1)} %copy.69) | data formatting | bytes 2097152 | tf_op jit(solution)/shard_map/convert_element_type | solution.py:59
  79.2 4.7 %multiply_convert_fusion.2 = bf16[4,512,2,64]{3,2,1,0:T(2,128)(2,1)S(1)} fusion(f32[4,512,2,64]{3,2,1,0:T(2,128)S(1)} %reshape.182, f32[4,512,2]{2,1,0:T(8,128)} %copy.70), kind=kLoop, calls=%fused_computation.15 | loop fusion | flops 524288 | bytes 1589248 | tf_op jit(solution)/shard_map/convert_element_type | solution.py:60
  83.9 1.8 %copy.72 = bf16[8,4,8,4,2,256]{5,3,4,1,2,0:T(4,128)(2,1)S(1)} copy(bf16[8,4,8,4,2,256]{5,4,3,2,1,0:T(2,128)(2,1)} %bitcast.82) | data formatting | bytes 2097152 | tf_op jit(solution)/shard_map/reshape | solution.py:47
  85.7 0.4 fusion.47
  86.1 0.7 fusion.18
  86.8 0.2 copy-done.2
  87.0 3.5 %fusion.10 = f32[4,512,2,64]{1,3,2,0:T(8,128)S(1)} fusion(f32[4,2,512]{2,1,0:T(2,128)S(1)} %reduce_window_sum.39, f32[4,512,512]{2,1,0:T(8,128)S(1)} %fusion.18, pred[4,512,512]{2,1,0:T(8,128)(4,1)S(1)} %copy-done.2, bf16[4,512,2,64]{3,2,1,0:T(2,128)(2,1)S(1)} %multiply_convert_fusion.2), kind=kOutput, calls=%fused_computation.16 | convolution fusion | flops 278921216 | bytes 6832128 | tf_op jit(solution)/shard_map/rhnj,rjhd->rnhd/dot_general | solution.py:84
  90.5 1.2 all-gather.7.cloned.1.call-done
  91.8 3.9 %copy.80 = bf16[4,8,384,128]{3,2,1,0:T(8,128)(2,1)} copy(bf16[4,8,384,128]{3,2,0,1:T(8,128)(2,1)} %all-gather.7.cloned.1.call-done) | data formatting | bytes 6291456 | tf_op jit(solution)/shard_map/all_gather | solution.py:40
  95.7 1.3 gather_fusion
  97.0 11.8 %fusion.2 = f32[4,512,128]{1,2,0:T(8,128)} fusion(bf16[4,3072,128]{1,2,0:T(8,128)(2,1)} %fusion.5, s32[4]{0:T(128)S(1)} %copy-done.10, s32[4,512]{1,0:T(4,128)S(1)} %iota_add_fusion, pred[4,3072]{1,0:T(4,128)(4,1)S(1)} %iota_compare_fusion, bf16[4,3072,128]{2,1,0:T(8,128)(2,1)} %bitcast.76, bf16[4,512,128]{2,0,1:T(4,128)(2,1)S(1)} %get-tuple-element.14), kind=kOutput, calls=%fused_computation.6 | convolution fusion | flops 3252682752 | bytes 7884816 | tf_op jit(solution)/shard_map/rns,rsc->rnc/dot_general | solution.py:94
  108.8 1.5 multiply_add_fusion
  110.3 0.3 copy.82
  110.6 0.6 fusion.11
  111.2 0.4 copy.104
  111.6 31.7 %all_to_all.21 = bf16[256,4,2,128]{3,2,1,0:T(2,128)(2,1)S(1)} all-to-all(bf16[256,4,2,128]{3,2,1,0:T(2,128)(2,1)S(1)} %bitcast.79), channel_id=1, replica_groups=mesh['tz'=8,'txc'=8,'mlp'=4] {'tz','txc','mlp'}, dimensions={0} | all-to-all | bytes 1048576 | tf_op jit(solution)/shard_map/all_to_all | solution.py:111
  143.3 0.6 convert_bitcast_fusion
  143.9 0.6 copy.84
  144.5 0.6 reshape.183
  145.1 2.5 %fusion.45 = (f32[16,2,8192]{2,1,0:T(2,128)S(1)}, f32[16,2,8192]{2,1,0:T(2,128)S(1)}) fusion(f32[16,2,8192]{2,1,0:T(2,128)S(1)} %reshape.183, bf16[16,2,8192]{2,1,0:T(2,128)(2,1)} %param.15), kind=kLoop, calls=%fused_computation.71 | loop fusion | flops 1835008 | bytes 3670016 | tf_op jit(solution)/shard_map/mul | solution.py:117
  147.6 0.9 mul.89
  148.5 0.2 reduce_sum.9
  148.8 0.1 copy.86
  148.9 0.1 mul.90
  149.0 0.9 mul.91
  149.9 1.4 multiply_convert_fusion.5
  (35 shorter events, 0.6 us)
Async XLA Ops:
  6.5 35.7 %copy-start.8 = (s32[4]{0:T(128)S(1)}, s32[4]{0:T(128)}, u32[]{:S(2)}) copy-start(s32[4]{0:T(128)} %param.22) | copy-start | bytes 52
  6.5 50.8 %copy-start.3 = (f32[4,2,3072]{2,1,0:T(2,128)S(1)}, f32[4,2,3072]{2,1,0:T(2,128)}, u32[]{:S(2)}) copy-start(f32[4,2,3072]{2,1,0:T(2,128)} %param.21) | copy-start | bytes 294916
  6.5 77.4 %all-gather.5.cloned.1.call-start = ((), (), s32[]{:S(2)}) async-start(), calls=%async_computation.4 | async-start | bytes 1179648 | tf_op jit(solution)/shard_map/all_gather | solution.py:46
  28.9 33.5 %copy-start.6 = (s32[4,4]{1,0:T(4,128)S(1)}, s32[4,4]{1,0:T(4,128)}, u32[]{:S(2)}) copy-start(s32[4,4]{1,0:T(4,128)} %param.23) | copy-start | bytes 196
  30.7 32.5 %copy-start.4 = (f32[4,512,2]{1,2,0:T(2,128)S(1)}, f32[4,512,2]{1,2,0:T(2,128)}, u32[]{:S(2)}) copy-start(f32[4,512,2]{1,2,0:T(2,128)} %param.17) | copy-start | bytes 49156
  30.7 15.9 %all-to-all-start.2 = ((bf16[4,8,48,128]{3,2,0,1:T(8,128)(2,1)}), bf16[4,8,48,128]{3,2,0,1:T(8,128)(2,1)S(1)}, u32[]{:S(2)}, u32[]{:S(2)}) async-start(bf16[4,8,48,128]{3,2,0,1:T(8,128)(2,1)} %copy.79), calls=%async_computation.2 | async-start | bytes 786432 | tf_op jit(solution)/shard_map/all_to_all | solution.py:39
  46.6 10.2 %copy-start.1 = (bf16[4,8,48,128]{3,2,0,1:T(8,128)(2,1)}, bf16[4,8,48,128]{3,2,0,1:T(8,128)(2,1)S(1)}, u32[]{:S(2)}) copy-start(bf16[4,8,48,128]{3,2,0,1:T(8,128)(2,1)S(1)} %all-to-all-done.2) | copy-start | bytes 1179652
  46.6 29.0 %all-to-all-start = ((bf16[256,4,2,128]{3,2,1,0:T(2,128)(2,1)}), bf16[256,4,2,128]{3,2,1,0:T(2,128)(2,1)}, u32[]{:S(2)}, u32[]{:S(2)}) async-start(bf16[256,4,2,128]{3,2,1,0:T(2,128)(2,1)} %copy.68), calls=%async_computation | async-start | bytes 1048576 | tf_op jit(solution)/shard_map/all_to_all | solution.py:54
  56.6 35.2 %all-gather.7.cloned.1.call-start = ((), (), s32[]{:S(2)}) async-start(), calls=%async_computation.5 | async-start | bytes 3538944 | tf_op jit(solution)/shard_map/all_gather | solution.py:40
  67.9 4.0 %copy-start.9 = (s32[4]{0:T(128)S(1)}, s32[4]{0:T(128)}, u32[]{:S(2)}) copy-start(s32[4]{0:T(128)} %param.22) | copy-start | bytes 52
  69.4 3.3 %copy-start = (s32[512,512]{1,0:T(8,128)S(1)}, s32[512,512]{1,0:T(8,128)}, u32[]{:S(2)}) copy-start(s32[512,512]{1,0:T(8,128)} %iota_subtract_fusion) | copy-start | bytes 3145732
  85.7 1.3 copy-start.2
  90.5 6.5 %copy-start.10 = (s32[4]{0:T(128)S(1)}, s32[4]{0:T(128)}, u32[]{:S(2)}) copy-start(s32[4]{0:T(128)} %param.24) | copy-start | bytes 52
  108.8 1.8 %copy-start.7 = (pred[4,4]{1,0:T(4,128)(4,1)S(1)}, pred[4,4]{1,0:T(4,128)(4,1)}, u32[]{:S(2)}) copy-start(pred[4,4]{1,0:T(4,128)(4,1)} %and_bitcast_fusion) | copy-start | bytes 52
  145.1 4.8 %copy-start.5 = (f32[8192]{0:T(1024)S(1)}, f32[8192]{0:T(1024)}, u32[]{:S(2)}) copy-start(f32[8192]{0:T(1024)} %param.25) | copy-start | bytes 98308
Sparse Core Ops, SparseCore 0:
  29.0 22.5 all-gather.4
  59.2 32.4 all-gather.6

commit v12 on v6

--- a/solution.py
+++ b/solution.py
@@ -51,6 +51,7 @@
 
     x_part = new_x.reshape(n_mlp, requests, tok_blk, n_tok, chans).transpose(3, 0, 1, 2, 4)
     x_part = x_part.reshape(n_dev, requests, tok_blk, chans)
+    x_part, sp = lax.optimization_barrier((x_part, sp))
     head_x = lax.all_to_all(x_part, ("tz", "txc", "mlp"), 0, 0, tiled=True)
     head_x = head_x.transpose(1, 0, 2, 3).reshape(requests, new_len, chans)
 

time: 157 us -> 167 us (1.064)
  waiting for transfers between devices: 6.45 us -> 17.6 us
  blocking collectives: 53 us -> 47.4 us
  local copies, waits for them, and re-layouts: 26.6 us -> 31.8 us
  other arithmetic: 25.5 us -> 22.4 us
  matrix products: 16.6 us -> 19.4 us
    all_to_all x1, waiting for transfers between devices: 0.48 us -> 15 us  [per_device(): head_x = lax.all_to_all(x_part, ('tz', 'txc', 'mlp'), 0, 0, tiled=True)]
    all_to_all x1, blocking collectives: 31.7 us -> 26.1 us  [per_device(): back = lax.all_to_all(back, ('tz', 'txc', 'mlp'), 0, 0, tiled=True)]
    optimization_barrier x0 -> x1, local copies, waits for them, and re-layouts: none -> 2.4 us  [per_device(): x_part, sp = lax.optimization_barrier((x_part, sp))]
    convert_element_type x2, local copies, waits for them, and re-layouts: 2.24 us -> 4.44 us  [per_device(): head_x.astype(jnp.float32).reshape(requests, new_len, heads_dev, head_dim)]
    dot_general x1, matrix products: 0.71 us -> 2.65 us  [per_device(): jnp.einsum('rnk,rjk->rnj', c_now, b_new, preferred_element_type=jnp.float32)]
    all_to_all x1, waiting for transfers between devices: 4.21 us -> 2.53 us  [per_device(): lax.all_to_all(b_cache, 'tz', split_axis=1, concat_axis=1, tiled=True)]
    unnamed x28 -> x26, local copies, waits for them, and re-layouts: 6.74 us -> 7.92 us
  transfers between devices with their start and end apart: 4 -> 4, of which waited for: 3 -> 2; matrix products, arithmetic and copies ran while one was open for 27% -> 28% of each run, Pallas kernels for 0% -> 0%
where the time goes in v12:
time: 167 us; the launch traced here: 166 us
  blocking collectives  47.4 us (28%)
  local copies, waits for them, and re-layouts  31.8 us (19%)
  other arithmetic  22.4 us (13%)
  matrix products  19.4 us (12%)
  waiting for transfers between devices  17.6 us (11%)
  starting transfers between devices  14.1 us (8%)
  between operations  13.8 us (8%)
    all_to_all x1, blocking collectives, per_device(): back = lax.all_to_all(back, ('tz', 'txc', 'mlp'), 0, 0, tiled=True)  26.1 us
    all_to_all x1, blocking collectives, per_device(): sp = lax.all_to_all(sp, ('tz', 'mlp'), 0, 0, tiled=True)  21.3 us
    all_to_all x1, waiting for transfers between devices, per_device(): head_x = lax.all_to_all(x_part, ('tz', 'txc', 'mlp'), 0, 0, tiled=True)  15 us
    dot_general x1, matrix products, per_device(): jnp.einsum('rns,rsc->rnc', probs_old, x_pair, preferred_element_type=jnp....  11.6 us
    all_to_all x1, starting transfers between devices, per_device(): head_x = lax.all_to_all(x_part, ('tz', 'txc', 'mlp'), 0, 0, tiled=True)  10.6 us
    unnamed x26, local copies, waits for them, and re-layouts  7.92 us
    another operation x6, other arithmetic  6.42 us
    convert_element_type x1, other arithmetic, per_device(): scaled = (scaled * step_size[..., None]).astype(jnp.bfloat16)  4.81 us
  transfers between devices with their start and end apart: 4, of which 2 were waited for; matrix products, arithmetic and copies ran while one was open for 28% of the time, Pallas kernels for 0%

profile of v12, /device:TPU:1, one launch (start us, length us, event | category | flops | bytes accessed | tf_op | source)
XLA Modules:
  0.0 166.5 jit_solution(520905029935314556)
XLA Ops:
  6.5 1.0 copy.68
  7.6 21.3 %all_to_all.20 = bf16[32,4,2,256]{3,2,1,0:T(2,128)(2,1)} all-to-all(bf16[32,4,2,256]{3,2,1,0:T(2,128)(2,1)S(1)} %bitcast.82), channel_id=1, replica_groups=mesh['tz'=8,'txc'=8,'mlp'=4] {'tz','mlp'}, dimensions={0} | all-to-all | bytes 262144 | tf_op jit(solution)/shard_map/all_to_all | solution.py:45
  28.9 1.8 %copy.79 = bf16[4,8,48,128]{3,2,0,1:T(8,128)(2,1)} copy(bf16[4,8,48,128]{3,2,1,0:T(8,128)(2,1)} %param.20) | data formatting | bytes 786432 | tf_op args[6]
  30.7 3.5 %all-to-all-start.2 = ((bf16[4,8,48,128]{3,2,0,1:T(8,128)(2,1)}), bf16[4,8,48,128]{3,2,0,1:T(8,128)(2,1)S(1)}, u32[]{:S(2)}, u32[]{:S(2)}) async-start(bf16[4,8,48,128]{3,2,0,1:T(8,128)(2,1)} %copy.79), calls=%async_computation.2 | async-start | bytes 786432 | tf_op jit(solution)/shard_map/all_to_all | solution.py:39
  34.2 0.7 exp.19
  34.8 0.8 negate_bitcast_fusion
  35.7 2.4 %reduce-window.14 = f32[4,2,4,128]{3,2,1,0:T(4,128)S(1)} reduce-window(f32[4,2,4,128]{3,2,1,0:T(4,128)S(1)} %reshape.174, f32[]{:T(128)} %constant.12.clone.1), window={size=1x1x1x128 pad=0_0x0_0x0_0x127_0}, to_apply=%region_0.0 | reduce-window | flops 520192 | bytes 32772 | tf_op jit(solution)/shard_map/reduce-window
  38.1 0.2 slice_reduce_fusion.1
  38.3 0.7 reduce-window.15
  39.0 0.1 broadcast_add_fusion.1
  39.1 2.1 %copy.72 = f32[4,512,2]{2,1,0:T(8,128)} copy(f32[4,512,2]{1,2,0:T(2,128)} %param.17) | data formatting | bytes 32768 | tf_op args[3]
  41.1 1.4 reshape.168
  42.6 1.2 copy.67
  43.8 0.1 iota_compare_fusion
  43.9 2.5 %all-to-all-done.2 = bf16[4,8,48,128]{3,2,0,1:T(8,128)(2,1)S(1)} async-done(((bf16[4,8,48,128]{3,2,0,1:T(8,128)(2,1)}), bf16[4,8,48,128]{3,2,0,1:T(8,128)(2,1)S(1)}, u32[]{:S(2)}, u32[]{:S(2)}) %all-to-all-start.2) | async-done | bytes 393248 | tf_op jit(solution)/shard_map/all_to_all | solution.py:39
  46.4 0.7 copy-done.1
  47.3 0.1 reshape.176
  47.4 2.3 %reduce-window.16 = f32[4,2,24,128]{3,2,1,0:T(8,128)S(1)} reduce-window(f32[4,2,24,128]{3,2,1,0:T(8,128)S(1)} %reshape.176, f32[]{:T(128)} %constant.12.clone.1), window={size=1x1x1x128 pad=0_0x0_0x0_0x127_0}, to_apply=%region_2.3 | reduce-window | flops 3121152 | bytes 196612 | tf_op jit(solution)/shard_map/reduce-window.2
  49.7 0.2 slice_reduce_fusion
  49.9 0.8 reduce-window.19
  50.7 0.1 broadcast_add_fusion
  50.8 0.1 slice.38
  50.9 0.1 copy.90
  51.0 0.1 copy.78
  51.1 3.2 %copy.76 = bf16[4,3072,128]{1,2,0:T(8,128)(2,1)S(1)} copy(bf16[4,3072,128]{2,1,0:T(8,128)(2,1)} %param.19) | data formatting | bytes 6291456 | tf_op args[5]
  54.3 0.7 shift-left_or_fusion
  55.1 0.1 reshape.201
  55.1 1.4 gather_fusion.1
  56.5 0.1 exponential_bitcast_fusion
  56.7 2.4 %fusion.5 = bf16[4,3072,128]{1,2,0:T(8,128)(2,1)} fusion(bf16[4,3072,128]{1,2,0:T(8,128)(2,1)S(1)} %copy.76, f32[4,3072,2]{1,2,0:T(2,128)S(1)} %exponential_bitcast_fusion), kind=kLoop, calls=%fused_computation.10 | loop fusion | flops 4718592 | bytes 6389760 | tf_op jit(solution)/shard_map/convert_element_type | solution.py:75
  59.1 0.1 iota_subtract_fusion
  59.3 0.1 broadcast_compare_fusion.1
  59.4 0.1 iota_add_fusion
  59.5 1.8 %copy.69 = bf16[8,4,8,4,2,256]{5,3,4,1,2,0:T(4,128)(2,1)S(1)} copy(bf16[8,4,8,4,2,256]{5,4,3,2,1,0:T(2,128)(2,1)} %bitcast.81) | data formatting | bytes 2097152 | tf_op jit(solution)/shard_map/reshape | solution.py:47
  61.3 2.4 %copy.70 = bf16[256,4,2,128]{3,2,1,0:T(2,128)(2,1)} copy(bf16[256,4,2,128]{3,0,2,1:T(8,128)(2,1)} %bitcast.76) | data formatting | bytes 1048576 | tf_op jit(solution)/shard_map/optimization_barrier | solution.py:54
  63.7 10.6 %all-to-all-start.1 = ((bf16[256,4,2,128]{3,2,1,0:T(2,128)(2,1)}), bf16[256,4,2,128]{3,2,1,0:T(2,128)(2,1)S(1)}, u32[]{:S(2)}, u32[]{:S(2)}) async-start(bf16[256,4,2,128]{3,2,1,0:T(2,128)(2,1)} %copy.70), calls=%async_computation.1 | async-start | bytes 1048576 | tf_op jit(solution)/shard_map/all_to_all | solution.py:55
  74.3 0.1 broadcast_compare_fusion
  74.4 1.7 %compare_and_fusion = pred[4,512,512]{2,1,0:T(8,128)(4,1)} fusion(s32[512,512]{1,0:T(8,128)S(1)} %iota_subtract_fusion, s32[4]{0:T(128)S(1)} %copy-done.10, pred[512,512]{1,0:T(8,128)(4,1)S(1)} %broadcast_compare_fusion), kind=kLoop, calls=%fused_computation.13 | loop fusion | flops 2097152 | bytes 2359312 | tf_op jit(solution)/shard_map/and | solution.py:80
  76.1 0.4 fusion.47
  76.5 2.7 %fusion.18 = f32[4,512,512]{2,1,0:T(8,128)} fusion(bf16[4,512,128]{2,0,1:T(4,128)(2,1)S(1)} %get-tuple-element.17, bf16[4,512,128]{2,0,1:T(4,128)(2,1)S(1)} %get-tuple-element.16), kind=kOutput, calls=%fused_computation.32 | convolution fusion | flops 268435456 | bytes 5242880 | tf_op jit(solution)/shard_map/rnk,rjk->rnj/dot_general | solution.py:78
  79.2 15.0 %all-to-all-done.1 = bf16[256,4,2,128]{3,2,1,0:T(2,128)(2,1)S(1)} async-done(((bf16[256,4,2,128]{3,2,1,0:T(2,128)(2,1)}), bf16[256,4,2,128]{3,2,1,0:T(2,128)(2,1)S(1)}, u32[]{:S(2)}, u32[]{:S(2)}) %all-to-all-start.1) | async-done | bytes 524320 | tf_op jit(solution)/shard_map/all_to_all | solution.py:55
  94.1 0.4 convert_bitcast_fusion
  94.5 1.4 copy.71
  95.9 3.0 %reshape.184 = f32[4,512,2,64]{3,2,1,0:T(2,128)S(1)} reshape(f32[4,256,2,128]{3,2,1,0:T(2,128)} %copy.71) | data formatting | bytes 2097152 | tf_op jit(solution)/shard_map/convert_element_type | solution.py:60
  99.0 4.8 %multiply_convert_fusion.2 = bf16[4,512,2,64]{3,2,1,0:T(2,128)(2,1)S(1)} fusion(f32[4,512,2,64]{3,2,1,0:T(2,128)S(1)} %reshape.184, f32[4,512,2]{2,1,0:T(8,128)} %copy.72), kind=kLoop, calls=%fused_computation.15 | loop fusion | flops 524288 | bytes 1589248 | tf_op jit(solution)/shard_map/convert_element_type | solution.py:61
  103.8 4.6 %fusion.10 = f32[4,512,2,64]{1,3,2,0:T(8,128)S(1)} fusion(f32[4,2,512]{2,1,0:T(2,128)S(1)} %reduce_window_sum.39, f32[4,512,512]{2,1,0:T(8,128)S(1)} %copy-done, pred[4,512,512]{2,1,0:T(8,128)(4,1)} %compare_and_fusion, bf16[4,512,2,64]{3,2,1,0:T(2,128)(2,1)S(1)} %multiply_convert_fusion.2), kind=kOutput, calls=%fused_computation.16 | convolution fusion | flops 278921216 | bytes 6832128 | tf_op jit(solution)/shard_map/rhnj,rjhd->rnhd/dot_general | solution.py:85
  108.4 3.9 %copy.80 = bf16[4,8,384,128]{3,2,1,0:T(8,128)(2,1)} copy(bf16[4,8,384,128]{3,2,0,1:T(8,128)(2,1)} %all-gather.7.cloned.1.call-done) | data formatting | bytes 6291456 | tf_op jit(solution)/shard_map/all_gather | solution.py:40
  112.3 1.3 gather_fusion
  113.6 11.6 %fusion.2 = f32[4,512,128]{1,2,0:T(8,128)} fusion(bf16[4,3072,128]{1,2,0:T(8,128)(2,1)} %fusion.5, s32[4]{0:T(128)S(1)} %copy-done.10, s32[4,512]{1,0:T(4,128)S(1)} %iota_add_fusion, pred[4,3072]{1,0:T(4,128)(4,1)S(1)} %copy-done.5, bf16[4,3072,128]{2,1,0:T(8,128)(2,1)} %bitcast.75, bf16[4,512,128]{2,0,1:T(4,128)(2,1)S(1)} %get-tuple-element.16), kind=kOutput, calls=%fused_computation.6 | convolution fusion | flops 3252682752 | bytes 7884816 | tf_op jit(solution)/shard_map/rns,rsc->rnc/dot_general | solution.py:95
  125.2 1.5 multiply_add_fusion
  126.7 0.3 copy.82
  127.0 0.6 fusion.11
  127.6 0.4 copy.104
  128.0 26.1 %all_to_all.21 = bf16[256,4,2,128]{3,2,1,0:T(2,128)(2,1)S(1)} all-to-all(bf16[256,4,2,128]{3,2,1,0:T(2,128)(2,1)S(1)} %bitcast.77), channel_id=1, replica_groups=mesh['tz'=8,'txc'=8,'mlp'=4] {'tz','txc','mlp'}, dimensions={0} | all-to-all | bytes 1048576 | tf_op jit(solution)/shard_map/all_to_all | solution.py:112
  154.1 0.2 copy.84
  154.3 0.1 reshape.183
  154.5 1.5 fusion.45
  156.0 0.9 mul.89
  156.9 0.2 reduce_sum.9
  157.0 0.1 copy.85
  157.1 0.1 copy.86
  157.2 0.1 mul.90
  157.3 0.9 mul.91
  158.2 1.4 multiply_convert_fusion.5
  (34 shorter events, 0.4 us)
Async XLA Ops:
  6.5 37.2 %copy-start.8 = (s32[4]{0:T(128)S(1)}, s32[4]{0:T(128)}, u32[]{:S(2)}) copy-start(s32[4]{0:T(128)} %param.22) | copy-start | bytes 52
  6.5 40.7 %copy-start.3 = (f32[4,2,3072]{2,1,0:T(2,128)S(1)}, f32[4,2,3072]{2,1,0:T(2,128)}, u32[]{:S(2)}) copy-start(f32[4,2,3072]{2,1,0:T(2,128)} %param.21) | copy-start | bytes 294916
  6.5 52.9 %all-gather.5.cloned.1.call-start = ((), (), s32[]{:S(2)}) async-start(), calls=%async_computation.4 | async-start | bytes 1179648 | tf_op jit(solution)/shard_map/all_gather | solution.py:46
  30.7 15.7 %all-to-all-start.2 = ((bf16[4,8,48,128]{3,2,0,1:T(8,128)(2,1)}), bf16[4,8,48,128]{3,2,0,1:T(8,128)(2,1)S(1)}, u32[]{:S(2)}, u32[]{:S(2)}) async-start(bf16[4,8,48,128]{3,2,0,1:T(8,128)(2,1)} %copy.79), calls=%async_computation.2 | async-start | bytes 786432 | tf_op jit(solution)/shard_map/all_to_all | solution.py:39
  34.1 74.3 %all-gather.7.cloned.1.call-start = ((), (), s32[]{:S(2)}) async-start(), calls=%async_computation.5 | async-start | bytes 3538944 | tf_op jit(solution)/shard_map/all_gather | solution.py:40
  43.9 3.3 %copy-start.4 = (pred[4,3072]{1,0:T(4,128)(4,1)}, pred[4,3072]{1,0:T(4,128)(4,1)S(1)}, u32[]{:S(2)}) copy-start(pred[4,3072]{1,0:T(4,128)(4,1)S(1)} %iota_compare_fusion) | copy-start | bytes 36868
  46.4 0.7 copy-start.1
  54.3 5.0 %copy-start.7 = (s32[4,4]{1,0:T(4,128)S(1)}, s32[4,4]{1,0:T(4,128)}, u32[]{:S(2)}) copy-start(s32[4,4]{1,0:T(4,128)} %param.23) | copy-start | bytes 196
  54.3 5.0 %copy-start.9 = (s32[4]{0:T(128)S(1)}, s32[4]{0:T(128)}, u32[]{:S(2)}) copy-start(s32[4]{0:T(128)} %param.22) | copy-start | bytes 52
  59.1 15.3 %copy-start.10 = (s32[4]{0:T(128)S(1)}, s32[4]{0:T(128)}, u32[]{:S(2)}) copy-start(s32[4]{0:T(128)} %param.24) | copy-start | bytes 52
  63.7 30.4 %all-to-all-start.1 = ((bf16[256,4,2,128]{3,2,1,0:T(2,128)(2,1)}), bf16[256,4,2,128]{3,2,1,0:T(2,128)(2,1)S(1)}, u32[]{:S(2)}, u32[]{:S(2)}) async-start(bf16[256,4,2,128]{3,2,1,0:T(2,128)(2,1)} %copy.70), calls=%async_computation.1 | async-start | bytes 1048576 | tf_op jit(solution)/shard_map/all_to_all | solution.py:55
  98.9 4.8 %copy-start = (f32[4,512,512]{2,1,0:T(8,128)S(1)}, f32[4,512,512]{2,1,0:T(8,128)}, u32[]{:S(2)}) copy-start(f32[4,512,512]{2,1,0:T(8,128)} %fusion.18) | copy-start | bytes 12582916
  108.4 5.2 %copy-start.5 = (pred[4,3072]{1,0:T(4,128)(4,1)S(1)}, pred[4,3072]{1,0:T(4,128)(4,1)}, u32[]{:S(2)}) copy-start(pred[4,3072]{1,0:T(4,128)(4,1)} %copy-done.4) | copy-start | bytes 36868
  126.6 27.8 %copy-start.2 = (bf16[16,2,8192]{2,1,0:T(2,128)(2,1)S(1)}, bf16[16,2,8192]{2,1,0:T(2,128)(2,1)}, u32[]{:S(2)}) copy-start(bf16[16,2,8192]{2,1,0:T(2,128)(2,1)} %param.15) | copy-start | bytes 1572868
  154.5 3.8 %copy-start.6 = (f32[8192]{0:T(1024)S(1)}, f32[8192]{0:T(1024)}, u32[]{:S(2)}) copy-start(f32[8192]{0:T(1024)} %param.25) | copy-start | bytes 98308
Sparse Core Ops, SparseCore 0:
  29.0 22.6 all-gather.4
  53.5 35.2 all-gather.6
